TPU v7x, 1024 devices: a whole 8x8x8 slice. The times are simulated.
1024 devices in a mesh: section: 2 (over core), ctx: 64 (over x, y), head: 8 (over z).
Axes of the slice: x: 8, y: 8, z: 8, core: 2. Of those that a mesh axis runs over, the one named last changes fastest.
Arguments:
- layer_in: bfloat16 [2, 8192, 8192], P('section', 'ctx', 'head'), may hold values from -200 to 200
- kv_in: bfloat16 [2, 8192, 2048], P('section', 'ctx', 'head'), may hold values from -12 to 12
- out_grad: bfloat16 [8192, 8192], P('ctx', 'head'), may hold values from -6 to 6
- sentences: int32 [8192], P('ctx'), may hold values from 0 to 255, never falling along the last dimension, each value on 1 to 96 neighbouring positions
- anchor_blocks: int32 [4], replicated, may hold values from 0 to 63, as said below
- anchor_pick: int32 [64, 2], P('ctx'), may hold values from 0 to 3, all different within a row
Outputs:
- input_grad: bfloat16 [2, 8192, 8192], P('section', 'ctx', 'head')
- kv_grad: bfloat16 [2, 8192, 2048], P('section', 'ctx', 'head')
Inputs may be any that keep to these rules, and one draw needn't show every extreme that they name: `anchor_blocks`: the anchor blocks are distinct; anchor a lies among the tokens of a ctx index in the a-th of 4 equal ranges of ctx indices, so no two lie among the 128 tokens of one index of ctx.
All inputs are finite; a program needn't handle non-finite values.
Results may differ from a plain program's by a relative error of at most 0.0061.
Values may be sent and summed in bfloat16 or wider, within the bound.
No kernel may reach another device: no remote copies, remote signals or barrier semaphores. Data moves between devices by JAX's collectives and lax.ppermute only.
A program may use at most 32 MiB of HBM per device.

v0:
```python
import jax
import jax.numpy as jnp
from jax import lax
from jax.sharding import PartitionSpec as P

HEAD_SIZE = 128
BLK = 128


def from_behind(x, axis, by):
    peers = lax.axis_size(axis)
    pairs = [(i, i + by) for i in range(peers) if 0 <= i + by < peers]
    return lax.ppermute(x, axis, pairs)


def attend(query_rows, keyvals, anchor_kv, cot, sentences, picks, anchor_blocks, blocks):
    rows, width = query_rows.shape
    feat = keyvals.shape[1]
    kvh = feat // (2 * HEAD_SIZE)
    group_size = width // (kvh * HEAD_SIZE)
    per_dev = rows // BLK
    npick = picks.shape[1]
    nanch = anchor_kv.shape[0]
    scale = HEAD_SIZE ** (-0.5)
    q_blocks = query_rows.reshape(per_dev, BLK, kvh, group_size, HEAD_SIZE)
    own = keyvals.reshape(per_dev, BLK, kvh, 2, HEAD_SIZE)
    far = anchor_kv.reshape(nanch, BLK, kvh, 2, HEAD_SIZE)[picks].reshape(
        per_dev, npick * BLK, kvh, 2, HEAD_SIZE
    )
    keys = jnp.concatenate([own, far], axis=1)
    kk = keys[:, :, :, 0]
    vv = keys[:, :, :, 1]
    score = (
        jnp.einsum("bqkgd,blkd->bkgql", q_blocks, kk, preferred_element_type=jnp.float32) * scale
    )
    sent = sentences.reshape(per_dev, BLK)
    idx = jnp.arange(BLK, dtype=jnp.int32)
    band = (idx[None, :, None] >= idx[None, None, :]) & (sent[:, :, None] == sent[:, None, :])
    valid = jnp.repeat(anchor_blocks[picks] < blocks[:, None], BLK, axis=1)
    far_mask = jnp.broadcast_to(valid[:, None, :], (per_dev, BLK, npick * BLK))
    mask = jnp.concatenate([band, far_mask], axis=2)[:, None, None]
    score = jnp.where(mask, score, jnp.float32(-1e30))
    top = jnp.max(score, axis=-1, keepdims=True)
    expo = jnp.exp(score - top)
    probs = expo / jnp.sum(expo, axis=-1, keepdims=True)
    pb = probs.astype(jnp.bfloat16)
    outp = jnp.einsum("bkgql,blkd->bqkgd", pb, vv, preferred_element_type=jnp.float32)
    c_blocks = cot.reshape(per_dev, BLK, kvh, group_size, HEAD_SIZE)
    delta = jnp.sum(c_blocks.astype(jnp.float32) * outp, axis=-1).transpose(0, 2, 3, 1)[..., None]
    dprob = jnp.einsum("bqkgd,blkd->bkgql", c_blocks, vv, preferred_element_type=jnp.float32)
    dscore = (probs * (dprob - delta)).astype(jnp.bfloat16)
    dq = jnp.einsum("bkgql,blkd->bqkgd", dscore, kk, preferred_element_type=jnp.float32) * scale
    dk = (
        jnp.einsum("bkgql,bqkgd->blkd", dscore, q_blocks, preferred_element_type=jnp.float32)
        * scale
    )
    dv = jnp.einsum("bkgql,bqkgd->blkd", pb, c_blocks, preferred_element_type=jnp.float32)
    dkv = jnp.stack([dk, dv], axis=3)
    band_grad = dkv[:, :BLK].reshape(rows, feat)
    far_grad = dkv[:, BLK:].reshape(per_dev, npick, BLK * feat)
    onehot = (picks[:, :, None] == jnp.arange(nanch, dtype=jnp.int32)[None, None, :]).astype(
        jnp.float32
    )
    anchor_term = jnp.einsum("ban,bam->nm", onehot, far_grad, precision=lax.Precision.HIGHEST)
    return (dq.reshape(rows, width), band_grad, anchor_term.reshape(nanch, BLK, feat))


def body(layer_in, kv_in, out_grad, sentences, anchor_blocks, anchor_pick):
    query_rows = layer_in[0]
    keyvals = kv_in[0]
    rows, width = query_rows.shape
    feat = keyvals.shape[1]
    per_dev = rows // BLK
    section_one = lax.axis_index("section") == 1
    blocks = lax.axis_index("ctx") * per_dev + jnp.arange(per_dev, dtype=jnp.int32)
    kv_blocks = keyvals.reshape(per_dev, BLK, feat)
    hit = anchor_blocks[None, :] == blocks[:, None]
    hit_float = hit.astype(jnp.float32)
    holder = jnp.sum(hit_float, axis=1).astype(jnp.bfloat16)
    mine = jnp.einsum("b,bmf->mf", holder, kv_blocks, preferred_element_type=jnp.float32).astype(
        jnp.bfloat16
    )
    gathered = lax.all_gather(mine[None], "ctx", axis=0, tiled=True)
    anchor_kv = gathered[anchor_blocks // per_dev]
    dq_first, band_first, term_first = attend(
        query_rows, keyvals, anchor_kv, out_grad, sentences, anchor_pick, anchor_blocks, blocks
    )
    sent_back = dq_first.astype(jnp.bfloat16)
    arrived = from_behind(sent_back, "section", -1)
    dq_second, band_second, term_second = attend(
        query_rows, keyvals, anchor_kv, arrived, sentences, anchor_pick, anchor_blocks, blocks
    )
    band_grad = jnp.where(section_one, band_first, band_second)
    anchor_term = jnp.where(section_one, term_first, term_second)
    summed = lax.psum(anchor_term, "ctx")
    owned = jnp.einsum("bn,nmf->bmf", hit_float, summed, precision=lax.Precision.HIGHEST)
    kv_grad = (band_grad + owned.reshape(band_grad.shape)).astype(jnp.bfloat16)
    input_grad = jnp.where(section_one, sent_back, dq_second.astype(jnp.bfloat16))
    return (input_grad[None], kv_grad[None])


def solution(mesh):
    placed = (
        P("section", "ctx", "head"),
        P("section", "ctx", "head"),
        P("ctx", "head"),
        P("ctx"),
        P(),
        P("ctx", None),
    )
    return jax.shard_map(
        body,
        mesh=mesh,
        in_specs=placed,
        out_specs=(P("section", "ctx", "head"), P("section", "ctx", "head")),
        check_vma=False,
    )
```

profile of v0, /device:TPU:2, one launch (start us, length us, event | category | flops | bytes accessed | tf_op | source)
XLA Modules:
  0.0 309.3 jit_solution(4947984256231851221)
XLA Ops:
  7.3 1.3 fusion.31
  9.2 1.5 multiply_convert_fusion
  10.8 1.0 copy.102
  11.7 1.1 copy.144
  12.9 1.1 copy.109
  14.0 0.6 gather_fusion.2
  15.3 99.9 %all-gather.2.cloned.1.call-done = bf16[64,128,256]{2,1,0:T(8,128)(2,1)} async-done(((bf16[1,128,256]{2,1,0:T(8,128)(2,1)}), bf16[64,128,256]{2,1,0:T(8,128)(2,1)}) %all-gather.2.cloned.1.call-update) | async-done | bytes 4194320 | tf_op jit(solution)/shard_map/all_gather | solution.py:83
  115.2 2.7 gather_fusion
  118.3 0.6 gather_fusion.1
  119.5 1.2 multiply_reduce_fusion
  120.7 0.4 convolution_bitcast_fusion.3
  121.2 0.5 fusion.6
  122.4 1.3 collective-permute-start
  124.2 0.8 fusion.26
  124.9 1.0 collective-permute-done
  125.9 1.4 convolution_bitcast_fusion.1
  127.4 1.1 fusion.18
  128.5 1.4 fusion.7
  129.9 0.4 fusion.14
  130.8 1.6 convolution_select_fusion
  133.0 0.9 copy.127
  133.8 166.3 %all-reduce.2.cloned.1.call-done = f32[4,128,256]{2,0,1:T(4,128)} async-done(((f32[4,128,256]{2,0,1:T(4,128)}), f32[4,128,256]{2,0,1:T(4,128)}) %all-reduce.2.cloned.1.call-update) | async-done | bytes 524304 | tf_op jit(solution)/shard_map/psum | solution.py:95
  300.2 1.6 fusion.28
  301.8 0.6 fusion.23
  (53 shorter events, 3.8 us)
Async XLA Ops:
  7.2 6.8 %copy-start = (s32[4]{0:T(128)S(1)}, s32[4]{0:T(128)}, u32[]{:S(2)}) copy-start(s32[4]{0:T(128)} %param.10) | copy-start | bytes 52
  7.2 6.8 %copy-start.10 = (s32[1,2]{1,0:T(1,128)S(1)}, s32[1,2]{1,0:T(1,128)}, u32[]{:S(2)}) copy-start(s32[1,2]{1,0:T(1,128)} %param.11) | copy-start | bytes 28
  7.2 7.6 %copy-start.8 = (bf16[1,128,1024]{2,1,0:T(8,128)(2,1)S(1)}, bf16[1,128,1024]{2,1,0:T(8,128)(2,1)}, u32[]{:S(2)}) copy-start(bf16[1,128,1024]{2,1,0:T(8,128)(2,1)} %param.6) | copy-start | bytes 786436
  7.2 7.9 %copy-start.9 = (s32[128]{0:T(128)S(1)}, s32[128]{0:T(128)}, u32[]{:S(2)}) copy-start(s32[128]{0:T(128)} %param.9) | copy-start | bytes 1540
  7.2 108.0 %all-gather.2.cloned.1.call-start = ((), (), s32[]{:S(2)}) async-start(), calls=%async_computation | async-start | bytes 4259840 | tf_op jit(solution)/shard_map/all_gather | solution.py:83
  10.7 289.4 %all-reduce.2.cloned.1.call-start = ((), (), s32[]{:S(2)}) async-start(), calls=%async_computation.1 | async-start | bytes 1048576 | tf_op jit(solution)/shard_map/psum | solution.py:95
  121.2 2.5 copy-start.3
  122.4 5.0 %copy-start.1 = (bf16[128,8,128]{2,0,1:T(8,128)(2,1)}, bf16[128,8,128]{2,0,1:T(8,128)(2,1)S(1)}, u32[]{:S(2)}) copy-start(bf16[128,8,128]{2,0,1:T(8,128)(2,1)S(1)} %fusion.8) | copy-start | bytes 786436
  122.4 3.6 %collective-permute-start = (bf16[128,1024]{0,1:T(8,128)(2,1)S(1)}, bf16[128,1024]{0,1:T(8,128)(2,1)}, u32[]{:S(2)}, u32[]{:S(2)}) collective-permute-start(bf16[128,1024]{0,1:T(8,128)(2,1)S(1)} %bitcast.197), channel_id=1, source_target_pairs={{512,0},{513,1},{514,2},{515,3},{516,4},{517,5},{518,6},{519,7},{5... | collective-permute-start | bytes 786440 | tf_op jit(solution)/shard_map/ppermute | solution.py:13
  125.9 1.5 copy-start.7
  127.4 2.9 copy-start.5
  130.3 2.1 copy-start.4
  130.3 2.1 copy-start.6
  130.8 1.8 copy-start.2
Sparse Core Ops, SparseCore 0:
  12.8 102.3 all-gather.1
  132.6 167.5 all-reduce.1
where the time goes:
time: 310 us; the launch traced here: 309 us
  waiting for transfers between devices  267 us (86%)
  between operations  15.1 us (5%)
  matrix products  10.7 us (3%)
  local copies, waits for them, and re-layouts  9.76 us (3%)
  other arithmetic  5.03 us (2%)
    psum x1, waiting for transfers between devices, body(): summed = lax.psum(anchor_term, 'ctx')  166 us
    all_gather x1, waiting for transfers between devices, body(): gathered = lax.all_gather(mine[None], 'ctx', axis=0, tiled=True)  99.9 us
  transfers between devices with their start and end apart: 3, of which 3 were waited for; matrix products, arithmetic and copies ran while one was open for 2% of the time, Pallas kernels for 0%

commit v1 on v0

--- a/solution.py
+++ b/solution.py
@@ -11,6 +11,11 @@
     peers = lax.axis_size(axis)
     pairs = [(i, i + by) for i in range(peers) if 0 <= i + by < peers]
     return lax.ppermute(x, axis, pairs)
+
+
+def swap(x, axis, bit):
+    peers = lax.axis_size(axis)
+    return lax.ppermute(x, axis, [(i, i ^ bit) for i in range(peers)])
 
 
 def attend(query_rows, keyvals, anchor_kv, cot, sentences, picks, anchor_blocks, blocks):
@@ -65,23 +70,61 @@
     return (dq.reshape(rows, width), band_grad, anchor_term.reshape(nanch, BLK, feat))
 
 
+def spread_anchors(mine, span, nanch, rank):
+    bit = 1
+    while bit < span:
+        mine = mine + swap(mine, "ctx", bit)
+        bit *= 2
+    got = mine[None]
+    bit = 1
+    while bit < nanch:
+        other = swap(got, "ctx", bit * span)
+        lower = (rank & bit) == 0
+        got = jnp.where(
+            lower, jnp.concatenate([got, other], axis=0), jnp.concatenate([other, got], axis=0)
+        )
+        bit *= 2
+    return got
+
+
+def gather_grads(acc, span, nanch, rank):
+    size = nanch
+    bit = nanch // 2
+    while bit >= 1:
+        half = size // 2
+        upper = (rank & bit) != 0
+        lo, hi = acc[:half], acc[half:]
+        keep = jnp.where(upper, hi, lo)
+        send = jnp.where(upper, lo, hi)
+        acc = keep + swap(send, "ctx", bit * span)
+        size = half
+        bit //= 2
+    bit = 1
+    while bit < span:
+        acc = acc + swap(acc, "ctx", bit)
+        bit *= 2
+    return acc[0]
+
+
 def body(layer_in, kv_in, out_grad, sentences, anchor_blocks, anchor_pick):
     query_rows = layer_in[0]
     keyvals = kv_in[0]
     rows, width = query_rows.shape
     feat = keyvals.shape[1]
     per_dev = rows // BLK
+    nanch = anchor_blocks.shape[0]
+    span = lax.axis_size("ctx") // nanch
+    ctx = lax.axis_index("ctx")
+    rank = ctx // span
     section_one = lax.axis_index("section") == 1
-    blocks = lax.axis_index("ctx") * per_dev + jnp.arange(per_dev, dtype=jnp.int32)
+    blocks = ctx * per_dev + jnp.arange(per_dev, dtype=jnp.int32)
     kv_blocks = keyvals.reshape(per_dev, BLK, feat)
     hit = anchor_blocks[None, :] == blocks[:, None]
-    hit_float = hit.astype(jnp.float32)
-    holder = jnp.sum(hit_float, axis=1).astype(jnp.bfloat16)
+    holder = jnp.sum(hit.astype(jnp.float32), axis=1).astype(jnp.bfloat16)
     mine = jnp.einsum("b,bmf->mf", holder, kv_blocks, preferred_element_type=jnp.float32).astype(
         jnp.bfloat16
     )
-    gathered = lax.all_gather(mine[None], "ctx", axis=0, tiled=True)
-    anchor_kv = gathered[anchor_blocks // per_dev]
+    anchor_kv = spread_anchors(mine, span, nanch, rank)
     dq_first, band_first, term_first = attend(
         query_rows, keyvals, anchor_kv, out_grad, sentences, anchor_pick, anchor_blocks, blocks
     )
@@ -92,8 +135,9 @@
     )
     band_grad = jnp.where(section_one, band_first, band_second)
     anchor_term = jnp.where(section_one, term_first, term_second)
-    summed = lax.psum(anchor_term, "ctx")
-    owned = jnp.einsum("bn,nmf->bmf", hit_float, summed, precision=lax.Precision.HIGHEST)
+    total = gather_grads(anchor_term, span, nanch, rank)
+    owner = (anchor_blocks[rank] == blocks).astype(jnp.float32)
+    owned = owner[:, None, None] * total[None]
     kv_grad = (band_grad + owned.reshape(band_grad.shape)).astype(jnp.bfloat16)
     input_grad = jnp.where(section_one, sent_back, dq_second.astype(jnp.bfloat16))
     return (input_grad[None], kv_grad[None])

time: 310 us -> 145 us (0.47)
  the two profiles are of different devices: /device:TPU:2 before, /device:TPU:6 now
where the time goes in v1:
time: 145 us; the launch traced here: 144 us
  waiting for transfers between devices  71 us (49%)
  starting transfers between devices  49.4 us (34%)
  matrix products  8.22 us (6%)
  local copies, waits for them, and re-layouts  7.13 us (5%)
  other arithmetic  5.7 us (4%)
  between operations  2.52 us (2%)
    ppermute x12, waiting for transfers between devices, swap(): return lax.ppermute(x, axis, [(i, i ^ bit) for i in range(peers)])  70.1 us
    ppermute x12, starting transfers between devices, swap(): return lax.ppermute(x, axis, [(i, i ^ bit) for i in range(peers)])  48.1 us
  transfers between devices with their start and end apart: 13, of which 13 were waited for; matrix products, arithmetic and copies ran while one was open for 5% of the time, Pallas kernels for 0%

profile of v1, /device:TPU:6, one launch (start us, length us, event | category | flops | bytes accessed | tf_op | source)
XLA Modules:
  0.0 144.0 jit_solution(3968254549684121958)
XLA Ops:
  3.6 3.7 %collective-permute-start = (bf16[128,256]{0,1:T(8,128)(2,1)S(1)}, bf16[128,256]{0,1:T(8,128)(2,1)S(1)}, u32[]{:S(2)}, u32[]{:S(2)}) collective-permute-start(bf16[128,256]{0,1:T(8,128)(2,1)S(1)} %fusion.25), channel_id=1, source_target_pairs={{0,8},{8,0},{16,24},{24,16},{32,40},{40,32},{48,56},{56,48},{64,72... | collective-permute-start | bytes 196616 | tf_op jit(solution)/shard_map/ppermute | solution.py:18
  8.2 1.7 %collective-permute-done = bf16[128,256]{0,1:T(8,128)(2,1)S(1)} collective-permute-done((bf16[128,256]{0,1:T(8,128)(2,1)S(1)}, bf16[128,256]{0,1:T(8,128)(2,1)S(1)}, u32[]{:S(2)}, u32[]{:S(2)}) %collective-permute-start) | collective-permute-done | bytes 65568 | tf_op jit(solution)/shard_map/ppermute | solution.py:18
  9.9 4.7 %collective-permute-start.1 = (bf16[128,256]{0,1:T(8,128)(2,1)S(1)}, bf16[128,256]{0,1:T(8,128)(2,1)S(1)}, u32[]{:S(2)}, u32[]{:S(2)}) collective-permute-start(bf16[128,256]{0,1:T(8,128)(2,1)S(1)} %fusion.60), channel_id=1, source_target_pairs={{0,16},{8,24},{16,0},{24,8},{32,48},{40,56},{48,32},{56,40},{64,80... | collective-permute-start | bytes 196616 | tf_op jit(solution)/shard_map/ppermute | solution.py:18
  15.3 1.7 %collective-permute-done.1 = bf16[128,256]{0,1:T(8,128)(2,1)S(1)} collective-permute-done((bf16[128,256]{0,1:T(8,128)(2,1)S(1)}, bf16[128,256]{0,1:T(8,128)(2,1)S(1)}, u32[]{:S(2)}, u32[]{:S(2)}) %collective-permute-start.1) | collective-permute-done | bytes 65568 | tf_op jit(solution)/shard_map/ppermute | solution.py:18
  17.0 8.9 %collective-permute-start.2 = (bf16[128,256]{0,1:T(8,128)(2,1)S(1)}, bf16[128,256]{0,1:T(8,128)(2,1)S(1)}, u32[]{:S(2)}, u32[]{:S(2)}) collective-permute-start(bf16[128,256]{0,1:T(8,128)(2,1)S(1)} %add.48), channel_id=1, source_target_pairs={{0,32},{8,40},{16,48},{24,56},{32,0},{40,8},{48,16},{56,24},{64,96... | collective-permute-start | bytes 196616 | tf_op jit(solution)/shard_map/ppermute | solution.py:18
  27.2 1.5 %collective-permute-done.2 = bf16[128,256]{0,1:T(8,128)(2,1)S(1)} collective-permute-done((bf16[128,256]{0,1:T(8,128)(2,1)S(1)}, bf16[128,256]{0,1:T(8,128)(2,1)S(1)}, u32[]{:S(2)}, u32[]{:S(2)}) %collective-permute-start.2) | collective-permute-done | bytes 65568 | tf_op jit(solution)/shard_map/ppermute | solution.py:18
  28.8 2.4 %collective-permute-start.3 = (bf16[128,256]{0,1:T(8,128)(2,1)S(1)}, bf16[128,256]{0,1:T(8,128)(2,1)S(1)}, u32[]{:S(2)}, u32[]{:S(2)}) collective-permute-start(bf16[128,256]{0,1:T(8,128)(2,1)S(1)} %add.49), channel_id=1, source_target_pairs={{0,64},{8,72},{16,80},{24,88},{32,96},{40,104},{48,112},{56,120},{... | collective-permute-start | bytes 196616 | tf_op jit(solution)/shard_map/ppermute | solution.py:18
  31.2 3.7 %collective-permute-done.3 = bf16[128,256]{0,1:T(8,128)(2,1)S(1)} collective-permute-done((bf16[128,256]{0,1:T(8,128)(2,1)S(1)}, bf16[128,256]{0,1:T(8,128)(2,1)S(1)}, u32[]{:S(2)}, u32[]{:S(2)}) %collective-permute-start.3) | collective-permute-done | bytes 65568 | tf_op jit(solution)/shard_map/ppermute | solution.py:18
  35.0 12.9 %collective-permute-start.4 = (bf16[1,128,256]{1,2,0:T(8,128)(2,1)S(1)}, bf16[1,128,256]{1,2,0:T(8,128)(2,1)S(1)}, u32[]{:S(2)}, u32[]{:S(2)}) collective-permute-start(bf16[1,128,256]{1,2,0:T(8,128)(2,1)S(1)} %bitcast.203), channel_id=1, source_target_pairs={{0,128},{8,136},{16,144},{24,152},{32,160},{40,168},{48,176},{56,1... | collective-permute-start | bytes 196616 | tf_op jit(solution)/shard_map/ppermute | solution.py:18
  48.0 2.1 %collective-permute-done.4 = bf16[1,128,256]{1,2,0:T(8,128)(2,1)S(1)} collective-permute-done((bf16[1,128,256]{1,2,0:T(8,128)(2,1)S(1)}, bf16[1,128,256]{1,2,0:T(8,128)(2,1)S(1)}, u32[]{:S(2)}, u32[]{:S(2)}) %collective-permute-start.4) | collective-permute-done | bytes 65568 | tf_op jit(solution)/shard_map/ppermute | solution.py:18
  50.1 1.9 %collective-permute-start.5 = (bf16[2,128,256]{1,2,0:T(8,128)(2,1)S(1)}, bf16[2,128,256]{1,2,0:T(8,128)(2,1)S(1)}, u32[]{:S(2)}, u32[]{:S(2)}) collective-permute-start(bf16[2,128,256]{1,2,0:T(8,128)(2,1)S(1)} %maximum_select_fusion.3), channel_id=1, source_target_pairs={{0,256},{8,264},{16,272},{24,280},{32,288},{40,296},{48,304},{56,3... | collective-permute-start | bytes 393224 | tf_op jit(solution)/shard_map/ppermute | solution.py:18
  53.1 9.2 %collective-permute-done.5 = bf16[2,128,256]{1,2,0:T(8,128)(2,1)S(1)} collective-permute-done((bf16[2,128,256]{1,2,0:T(8,128)(2,1)S(1)}, bf16[2,128,256]{1,2,0:T(8,128)(2,1)S(1)}, u32[]{:S(2)}, u32[]{:S(2)}) %collective-permute-start.5) | collective-permute-done | bytes 131104 | tf_op jit(solution)/shard_map/ppermute | solution.py:18
  75.9 1.9 %collective-permute-start.7 = (f32[2,128,256]{2,0,1:T(2,128)S(1)}, f32[2,128,256]{2,0,1:T(2,128)S(1)}, u32[]{:S(2)}, u32[]{:S(2)}) collective-permute-start(f32[2,128,256]{2,0,1:T(2,128)S(1)} %broadcast_select_fusion), channel_id=1, source_target_pairs={{0,256},{8,264},{16,272},{24,280},{32,288},{40,296},{48,304},{56,3... | collective-permute-start | bytes 786440 | tf_op jit(solution)/shard_map/ppermute | solution.py:18
  77.9 18.4 %collective-permute-done.7 = f32[2,128,256]{2,0,1:T(2,128)S(1)} collective-permute-done((f32[2,128,256]{2,0,1:T(2,128)S(1)}, f32[2,128,256]{2,0,1:T(2,128)S(1)}, u32[]{:S(2)}, u32[]{:S(2)}) %collective-permute-start.7) | collective-permute-done | bytes 262176 | tf_op jit(solution)/shard_map/ppermute | solution.py:18
  96.7 3.7 %collective-permute-start.8 = (f32[1,128,256]{2,0,1:T(1,128)S(1)}, f32[1,128,256]{2,0,1:T(1,128)S(1)}, u32[]{:S(2)}, u32[]{:S(2)}) collective-permute-start(f32[1,128,256]{2,0,1:T(1,128)S(1)} %broadcast_select_fusion.1), channel_id=1, source_target_pairs={{0,128},{8,136},{16,144},{24,152},{32,160},{40,168},{48,176},{56,1... | collective-permute-start | bytes 393224 | tf_op jit(solution)/shard_map/ppermute | solution.py:18
  100.4 7.3 %collective-permute-done.8 = f32[1,128,256]{2,0,1:T(1,128)S(1)} collective-permute-done((f32[1,128,256]{2,0,1:T(1,128)S(1)}, f32[1,128,256]{2,0,1:T(1,128)S(1)}, u32[]{:S(2)}, u32[]{:S(2)}) %collective-permute-start.8) | collective-permute-done | bytes 131104 | tf_op jit(solution)/shard_map/ppermute | solution.py:18
  107.9 2.1 %collective-permute-start.9 = (f32[1,128,256]{2,0,1:T(1,128)S(1)}, f32[1,128,256]{2,0,1:T(1,128)S(1)}, u32[]{:S(2)}, u32[]{:S(2)}) collective-permute-start(f32[1,128,256]{2,0,1:T(1,128)S(1)} %fusion.20), channel_id=1, source_target_pairs={{0,8},{8,0},{16,24},{24,16},{32,40},{40,32},{48,56},{56,48},{64,72... | collective-permute-start | bytes 393224 | tf_op jit(solution)/shard_map/ppermute | solution.py:18
  109.9 5.1 %collective-permute-done.9 = f32[1,128,256]{2,0,1:T(1,128)S(1)} collective-permute-done((f32[1,128,256]{2,0,1:T(1,128)S(1)}, f32[1,128,256]{2,0,1:T(1,128)S(1)}, u32[]{:S(2)}, u32[]{:S(2)}) %collective-permute-start.9) | collective-permute-done | bytes 131104 | tf_op jit(solution)/shard_map/ppermute | solution.py:18
  115.2 1.9 %collective-permute-start.10 = (f32[1,128,256]{2,0,1:T(1,128)S(1)}, f32[1,128,256]{2,0,1:T(1,128)S(1)}, u32[]{:S(2)}, u32[]{:S(2)}) collective-permute-start(f32[1,128,256]{2,0,1:T(1,128)S(1)} %add.56), channel_id=1, source_target_pairs={{0,16},{8,24},{16,0},{24,8},{32,48},{40,56},{48,32},{56,40},{64,80... | collective-permute-start | bytes 393224 | tf_op jit(solution)/shard_map/ppermute | solution.py:18
  117.1 8.0 %collective-permute-done.10 = f32[1,128,256]{2,0,1:T(1,128)S(1)} collective-permute-done((f32[1,128,256]{2,0,1:T(1,128)S(1)}, f32[1,128,256]{2,0,1:T(1,128)S(1)}, u32[]{:S(2)}, u32[]{:S(2)}) %collective-permute-start.10) | collective-permute-done | bytes 131104 | tf_op jit(solution)/shard_map/ppermute | solution.py:18
  125.3 1.9 %collective-permute-start.11 = (f32[1,128,256]{2,0,1:T(1,128)S(1)}, f32[1,128,256]{2,0,1:T(1,128)S(1)}, u32[]{:S(2)}, u32[]{:S(2)}) collective-permute-start(f32[1,128,256]{2,0,1:T(1,128)S(1)} %add.57), channel_id=1, source_target_pairs={{0,32},{8,40},{16,48},{24,56},{32,0},{40,8},{48,16},{56,24},{64,96... | collective-permute-start | bytes 393224 | tf_op jit(solution)/shard_map/ppermute | solution.py:18
  128.5 7.6 %collective-permute-done.11 = f32[1,128,256]{2,0,1:T(1,128)S(1)} collective-permute-done((f32[1,128,256]{2,0,1:T(1,128)S(1)}, f32[1,128,256]{2,0,1:T(1,128)S(1)}, u32[]{:S(2)}, u32[]{:S(2)}) %collective-permute-start.11) | collective-permute-done | bytes 131104 | tf_op jit(solution)/shard_map/ppermute | solution.py:18
  136.3 1.9 %collective-permute-start.12 = (f32[1,128,256]{2,0,1:T(1,128)S(1)}, f32[1,128,256]{2,0,1:T(1,128)S(1)}, u32[]{:S(2)}, u32[]{:S(2)}) collective-permute-start(f32[1,128,256]{2,0,1:T(1,128)S(1)} %add.58), channel_id=1, source_target_pairs={{0,64},{8,72},{16,80},{24,88},{32,96},{40,104},{48,112},{56,120},{... | collective-permute-start | bytes 393224 | tf_op jit(solution)/shard_map/ppermute | solution.py:18
  139.6 3.6 %collective-permute-done.12 = f32[1,128,256]{2,0,1:T(1,128)S(1)} collective-permute-done((f32[1,128,256]{2,0,1:T(1,128)S(1)}, f32[1,128,256]{2,0,1:T(1,128)S(1)}, u32[]{:S(2)}, u32[]{:S(2)}) %collective-permute-start.12) | collective-permute-done | bytes 131104 | tf_op jit(solution)/shard_map/ppermute | solution.py:18
  (84 shorter events, 23.3 us)
Async XLA Ops:
  0.6 51.6 %copy-start.1 = (bf16[128,1024]{1,0:T(8,128)(2,1)S(1)}, bf16[128,1024]{1,0:T(8,128)(2,1)}, u32[]{:S(2)}) copy-start(bf16[128,1024]{1,0:T(8,128)(2,1)} %param.8) | copy-start | bytes 786436
  3.6 49.0 %copy-start.9 = (bf16[1,128,1024]{2,1,0:T(8,128)(2,1)S(1)}, bf16[1,128,1024]{2,1,0:T(8,128)(2,1)}, u32[]{:S(2)}) copy-start(bf16[1,128,1024]{2,1,0:T(8,128)(2,1)} %param.6) | copy-start | bytes 786436
  3.6 6.3 %collective-permute-start = (bf16[128,256]{0,1:T(8,128)(2,1)S(1)}, bf16[128,256]{0,1:T(8,128)(2,1)S(1)}, u32[]{:S(2)}, u32[]{:S(2)}) collective-permute-start(bf16[128,256]{0,1:T(8,128)(2,1)S(1)} %fusion.25), channel_id=1, source_target_pairs={{0,8},{8,0},{16,24},{24,16},{32,40},{40,32},{48,56},{56,48},{64,72... | collective-permute-start | bytes 196616 | tf_op jit(solution)/shard_map/ppermute | solution.py:18
  9.9 7.1 %collective-permute-start.1 = (bf16[128,256]{0,1:T(8,128)(2,1)S(1)}, bf16[128,256]{0,1:T(8,128)(2,1)S(1)}, u32[]{:S(2)}, u32[]{:S(2)}) collective-permute-start(bf16[128,256]{0,1:T(8,128)(2,1)S(1)} %fusion.60), channel_id=1, source_target_pairs={{0,16},{8,24},{16,0},{24,8},{32,48},{40,56},{48,32},{56,40},{64,80... | collective-permute-start | bytes 196616 | tf_op jit(solution)/shard_map/ppermute | solution.py:18
  17.0 11.7 %collective-permute-start.2 = (bf16[128,256]{0,1:T(8,128)(2,1)S(1)}, bf16[128,256]{0,1:T(8,128)(2,1)S(1)}, u32[]{:S(2)}, u32[]{:S(2)}) collective-permute-start(bf16[128,256]{0,1:T(8,128)(2,1)S(1)} %add.48), channel_id=1, source_target_pairs={{0,32},{8,40},{16,48},{24,56},{32,0},{40,8},{48,16},{56,24},{64,96... | collective-permute-start | bytes 196616 | tf_op jit(solution)/shard_map/ppermute | solution.py:18
  28.8 6.2 %collective-permute-start.3 = (bf16[128,256]{0,1:T(8,128)(2,1)S(1)}, bf16[128,256]{0,1:T(8,128)(2,1)S(1)}, u32[]{:S(2)}, u32[]{:S(2)}) collective-permute-start(bf16[128,256]{0,1:T(8,128)(2,1)S(1)} %add.49), channel_id=1, source_target_pairs={{0,64},{8,72},{16,80},{24,88},{32,96},{40,104},{48,112},{56,120},{... | collective-permute-start | bytes 196616 | tf_op jit(solution)/shard_map/ppermute | solution.py:18
  35.0 15.2 %collective-permute-start.4 = (bf16[1,128,256]{1,2,0:T(8,128)(2,1)S(1)}, bf16[1,128,256]{1,2,0:T(8,128)(2,1)S(1)}, u32[]{:S(2)}, u32[]{:S(2)}) collective-permute-start(bf16[1,128,256]{1,2,0:T(8,128)(2,1)S(1)} %bitcast.203), channel_id=1, source_target_pairs={{0,128},{8,136},{16,144},{24,152},{32,160},{40,168},{48,176},{56,1... | collective-permute-start | bytes 196616 | tf_op jit(solution)/shard_map/ppermute | solution.py:18
  50.1 12.2 %collective-permute-start.5 = (bf16[2,128,256]{1,2,0:T(8,128)(2,1)S(1)}, bf16[2,128,256]{1,2,0:T(8,128)(2,1)S(1)}, u32[]{:S(2)}, u32[]{:S(2)}) collective-permute-start(bf16[2,128,256]{1,2,0:T(8,128)(2,1)S(1)} %maximum_select_fusion.3), channel_id=1, source_target_pairs={{0,256},{8,264},{16,272},{24,280},{32,288},{40,296},{48,304},{56,3... | collective-permute-start | bytes 393224 | tf_op jit(solution)/shard_map/ppermute | solution.py:18
  65.4 2.5 %copy-start.4 = (f32[1,384,1,1,128]{1,4,3,2,0:T(8,128)}, f32[1,384,1,1,128]{1,4,3,2,0:T(8,128)S(1)}, u32[]{:S(2)}) copy-start(f32[1,384,1,1,128]{1,4,3,2,0:T(8,128)S(1)} %convolution_bitcast_fusion.3) | copy-start | bytes 589828
  66.2 3.0 %copy-start.2 = (bf16[128,8,128]{2,0,1:T(8,128)(2,1)}, bf16[128,8,128]{2,0,1:T(8,128)(2,1)S(1)}, u32[]{:S(2)}) copy-start(bf16[128,8,128]{2,0,1:T(8,128)(2,1)S(1)} %fusion.8) | copy-start | bytes 786436
  66.2 2.2 %copy-start.10 = (s32[1,2]{1,0:T(1,128)S(1)}, s32[1,2]{1,0:T(1,128)}, u32[]{:S(2)}) copy-start(s32[1,2]{1,0:T(1,128)} %param.11) | copy-start | bytes 28
  66.6 3.6 %collective-permute-start.6 = (bf16[128,1024]{0,1:T(8,128)(2,1)S(1)}, bf16[128,1024]{0,1:T(8,128)(2,1)}, u32[]{:S(2)}, u32[]{:S(2)}) collective-permute-start(bf16[128,1024]{0,1:T(8,128)(2,1)S(1)} %bitcast.199), channel_id=1, source_target_pairs={{512,0},{513,1},{514,2},{515,3},{516,4},{517,5},{518,6},{519,7},{5... | collective-permute-start | bytes 786440 | tf_op jit(solution)/shard_map/ppermute | solution.py:13
  70.2 1.4 %copy-start.8 = (f32[1,128,1,8,128]{1,4,3,2,0:T(8,128)S(1)}, f32[1,128,1,8,128]{1,4,3,2,0:T(8,128)}, u32[]{:S(2)}) copy-start(f32[1,128,1,8,128]{1,4,3,2,0:T(8,128)} %get-tuple-element.11) | copy-start | bytes 1572868
  71.6 2.9 %copy-start.6 = (f32[1,384,1,1,128]{1,4,3,2,0:T(8,128)}, f32[1,384,1,1,128]{1,4,3,2,0:T(8,128)S(1)}, u32[]{:S(2)}) copy-start(f32[1,384,1,1,128]{1,4,3,2,0:T(8,128)S(1)} %convolution_bitcast_fusion.1) | copy-start | bytes 589828
  75.9 51.3 %copy-start = (s32[4]{0:T(128)S(1)}, s32[4]{0:T(128)}, u32[]{:S(2)}) copy-start(s32[4]{0:T(128)} %param.10) | copy-start | bytes 52
  75.9 20.4 %collective-permute-start.7 = (f32[2,128,256]{2,0,1:T(2,128)S(1)}, f32[2,128,256]{2,0,1:T(2,128)S(1)}, u32[]{:S(2)}, u32[]{:S(2)}) collective-permute-start(f32[2,128,256]{2,0,1:T(2,128)S(1)} %broadcast_select_fusion), channel_id=1, source_target_pairs={{0,256},{8,264},{16,272},{24,280},{32,288},{40,296},{48,304},{56,3... | collective-permute-start | bytes 786440 | tf_op jit(solution)/shard_map/ppermute | solution.py:18
  77.9 60.4 %copy-start.3 = (bf16[128,8,128]{2,0,1:T(8,128)(2,1)S(1)}, bf16[128,8,128]{2,0,1:T(8,128)(2,1)}, u32[]{:S(2)}) copy-start(bf16[128,8,128]{2,0,1:T(8,128)(2,1)} %copy-done.2) | copy-start | bytes 786436
  96.7 11.0 %collective-permute-start.8 = (f32[1,128,256]{2,0,1:T(1,128)S(1)}, f32[1,128,256]{2,0,1:T(1,128)S(1)}, u32[]{:S(2)}, u32[]{:S(2)}) collective-permute-start(f32[1,128,256]{2,0,1:T(1,128)S(1)} %broadcast_select_fusion.1), channel_id=1, source_target_pairs={{0,128},{8,136},{16,144},{24,152},{32,160},{40,168},{48,176},{56,1... | collective-permute-start | bytes 393224 | tf_op jit(solution)/shard_map/ppermute | solution.py:18
  107.9 31.6 %copy-start.5 = (f32[1,384,1,1,128]{1,4,3,2,0:T(8,128)S(1)}, f32[1,384,1,1,128]{1,4,3,2,0:T(8,128)}, u32[]{:S(2)}) copy-start(f32[1,384,1,1,128]{1,4,3,2,0:T(8,128)} %copy-done.4) | copy-start | bytes 589828
  107.9 31.5 %copy-start.7 = (f32[1,384,1,1,128]{1,4,3,2,0:T(8,128)S(1)}, f32[1,384,1,1,128]{1,4,3,2,0:T(8,128)}, u32[]{:S(2)}) copy-start(f32[1,384,1,1,128]{1,4,3,2,0:T(8,128)} %copy-done.6) | copy-start | bytes 589828
  107.9 7.2 %collective-permute-start.9 = (f32[1,128,256]{2,0,1:T(1,128)S(1)}, f32[1,128,256]{2,0,1:T(1,128)S(1)}, u32[]{:S(2)}, u32[]{:S(2)}) collective-permute-start(f32[1,128,256]{2,0,1:T(1,128)S(1)} %fusion.20), channel_id=1, source_target_pairs={{0,8},{8,0},{16,24},{24,16},{32,40},{40,32},{48,56},{56,48},{64,72... | collective-permute-start | bytes 393224 | tf_op jit(solution)/shard_map/ppermute | solution.py:18
  115.2 10.0 %collective-permute-start.10 = (f32[1,128,256]{2,0,1:T(1,128)S(1)}, f32[1,128,256]{2,0,1:T(1,128)S(1)}, u32[]{:S(2)}, u32[]{:S(2)}) collective-permute-start(f32[1,128,256]{2,0,1:T(1,128)S(1)} %add.56), channel_id=1, source_target_pairs={{0,16},{8,24},{16,0},{24,8},{32,48},{40,56},{48,32},{56,40},{64,80... | collective-permute-start | bytes 393224 | tf_op jit(solution)/shard_map/ppermute | solution.py:18
  125.3 10.9 %collective-permute-start.11 = (f32[1,128,256]{2,0,1:T(1,128)S(1)}, f32[1,128,256]{2,0,1:T(1,128)S(1)}, u32[]{:S(2)}, u32[]{:S(2)}) collective-permute-start(f32[1,128,256]{2,0,1:T(1,128)S(1)} %add.57), channel_id=1, source_target_pairs={{0,32},{8,40},{16,48},{24,56},{32,0},{40,8},{48,16},{56,24},{64,96... | collective-permute-start | bytes 393224 | tf_op jit(solution)/shard_map/ppermute | solution.py:18
  136.3 6.9 %collective-permute-start.12 = (f32[1,128,256]{2,0,1:T(1,128)S(1)}, f32[1,128,256]{2,0,1:T(1,128)S(1)}, u32[]{:S(2)}, u32[]{:S(2)}) collective-permute-start(f32[1,128,256]{2,0,1:T(1,128)S(1)} %add.58), channel_id=1, source_target_pairs={{0,64},{8,72},{16,80},{24,88},{32,96},{40,104},{48,112},{56,120},{... | collective-permute-start | bytes 393224 | tf_op jit(solution)/shard_map/ppermute | solution.py:18

commit v2 on v0

--- a/solution.py
+++ b/solution.py
@@ -1,7 +1,7 @@
 import jax
 import jax.numpy as jnp
 from jax import lax
-from jax.sharding import PartitionSpec as P
+from jax.sharding import Mesh, PartitionSpec as P
 
 HEAD_SIZE = 128
 BLK = 128
@@ -65,23 +65,53 @@
     return (dq.reshape(rows, width), band_grad, anchor_term.reshape(nanch, BLK, feat))
 
 
+def spread_anchors(mine, rows_per_slot):
+    ny = lax.axis_size("cy")
+    nx = lax.axis_size("cx")
+    blk, feat = mine.shape
+    part = mine.reshape(ny, blk // ny, feat)
+    got = lax.all_to_all(part, "cy", 0, 0, tiled=True)
+    row = jnp.sum(got.astype(jnp.float32), axis=0).astype(mine.dtype)
+    got = lax.all_to_all(jnp.broadcast_to(row[None], (nx,) + row.shape), "cx", 0, 0, tiled=True)
+    nslot = nx // rows_per_slot
+    slots = jnp.sum(
+        got.reshape(nslot, rows_per_slot, *row.shape).astype(jnp.float32), axis=1
+    ).astype(mine.dtype)
+    got = lax.all_to_all(jnp.broadcast_to(slots[None], (ny,) + slots.shape), "cy", 0, 0, tiled=True)
+    return got.transpose(1, 0, 2, 3).reshape(nslot, blk, feat)
+
+
+def gather_grads(acc, rows_per_slot):
+    ny = lax.axis_size("cy")
+    nslot, blk, feat = acc.shape
+    part = acc.reshape(nslot, ny, blk // ny, feat).transpose(1, 0, 2, 3)
+    got = lax.all_to_all(part, "cy", 0, 0, tiled=True)
+    rowsum = jnp.sum(got, axis=0)
+    got = lax.all_to_all(jnp.repeat(rowsum, rows_per_slot, axis=0), "cx", 0, 0, tiled=True)
+    total = jnp.sum(got, axis=0)
+    got = lax.all_to_all(jnp.broadcast_to(total[None], (ny,) + total.shape), "cy", 0, 0, tiled=True)
+    return got.reshape(blk, feat)
+
+
 def body(layer_in, kv_in, out_grad, sentences, anchor_blocks, anchor_pick):
     query_rows = layer_in[0]
     keyvals = kv_in[0]
     rows, width = query_rows.shape
     feat = keyvals.shape[1]
     per_dev = rows // BLK
+    nanch = anchor_blocks.shape[0]
+    rows_per_slot = lax.axis_size("cx") // nanch
+    ctx = lax.axis_index("cx") * lax.axis_size("cy") + lax.axis_index("cy")
+    rank = lax.axis_index("cx") // rows_per_slot
     section_one = lax.axis_index("section") == 1
-    blocks = lax.axis_index("ctx") * per_dev + jnp.arange(per_dev, dtype=jnp.int32)
+    blocks = ctx * per_dev + jnp.arange(per_dev, dtype=jnp.int32)
     kv_blocks = keyvals.reshape(per_dev, BLK, feat)
     hit = anchor_blocks[None, :] == blocks[:, None]
-    hit_float = hit.astype(jnp.float32)
-    holder = jnp.sum(hit_float, axis=1).astype(jnp.bfloat16)
+    holder = jnp.sum(hit.astype(jnp.float32), axis=1).astype(jnp.bfloat16)
     mine = jnp.einsum("b,bmf->mf", holder, kv_blocks, preferred_element_type=jnp.float32).astype(
         jnp.bfloat16
     )
-    gathered = lax.all_gather(mine[None], "ctx", axis=0, tiled=True)
-    anchor_kv = gathered[anchor_blocks // per_dev]
+    anchor_kv = spread_anchors(mine, rows_per_slot)
     dq_first, band_first, term_first = attend(
         query_rows, keyvals, anchor_kv, out_grad, sentences, anchor_pick, anchor_blocks, blocks
     )
@@ -92,26 +122,34 @@
     )
     band_grad = jnp.where(section_one, band_first, band_second)
     anchor_term = jnp.where(section_one, term_first, term_second)
-    summed = lax.psum(anchor_term, "ctx")
-    owned = jnp.einsum("bn,nmf->bmf", hit_float, summed, precision=lax.Precision.HIGHEST)
+    total = gather_grads(anchor_term, rows_per_slot)
+    owner = (anchor_blocks[rank] == blocks).astype(jnp.float32)
+    owned = owner[:, None, None] * total[None]
     kv_grad = (band_grad + owned.reshape(band_grad.shape)).astype(jnp.bfloat16)
     input_grad = jnp.where(section_one, sent_back, dq_second.astype(jnp.bfloat16))
     return (input_grad[None], kv_grad[None])
 
 
 def solution(mesh):
+    ny = 8
+    devs = mesh.devices
+    grid = Mesh(
+        devs.reshape(devs.shape[0], devs.shape[1] // ny, ny, devs.shape[2]),
+        ("section", "cx", "cy", "head"),
+    )
+    ctx = ("cx", "cy")
     placed = (
-        P("section", "ctx", "head"),
-        P("section", "ctx", "head"),
-        P("ctx", "head"),
-        P("ctx"),
+        P("section", ctx, "head"),
+        P("section", ctx, "head"),
+        P(ctx, "head"),
+        P(ctx),
         P(),
-        P("ctx", None),
+        P(ctx, None),
     )
     return jax.shard_map(
         body,
-        mesh=mesh,
+        mesh=grid,
         in_specs=placed,
-        out_specs=(P("section", "ctx", "head"), P("section", "ctx", "head")),
+        out_specs=(P("section", ctx, "head"), P("section", ctx, "head")),
         check_vma=False,
     )

time: 310 us -> 118 us (0.38)
  waiting for transfers between devices: 267 us -> 38.2 us
  starting transfers between devices: 1.37 us -> 32.7 us
  blocking collectives: 0 us -> 21.3 us
  between operations: 15.1 us -> 2.39 us
    psum x1 -> x0, waiting for transfers between devices: 166 us -> none  [body(): summed = lax.psum(anchor_term, 'ctx')]
    all_gather x1 -> x0, waiting for transfers between devices: 99.9 us -> none  [body(): gathered = lax.all_gather(mine[None], 'ctx', axis=0, tiled=True)]
    all_to_all x0 -> x5, waiting for transfers between devices: none -> 37.2 us  [the longest x1 9.31 us: spread_anchors(): lax.all_to_all(jnp.broadcast_to(slots[None], (ny,) + slots.shape), 'cy',...]
    all_to_all x0 -> x5, starting transfers between devices: none -> 31.5 us  [the longest x1 12.3 us: spread_anchors(): lax.all_to_all(jnp.broadcast_to(row[None], (nx,) + row.shape), 'cx', 0, 0...]
    all_to_all x0 -> x1, blocking collectives: none -> 21.3 us  [gather_grads(): got = lax.all_to_all(part, 'cy', 0, 0, tiled=True)]
  transfers between devices with their start and end apart: 3 -> 6, of which waited for: 3 -> 6; matrix products, arithmetic and copies ran while one was open for 2% -> 5% of each run, Pallas kernels for 0% -> 0%
where the time goes in v2:
time: 118 us; the launch traced here: 117 us
  waiting for transfers between devices  38.2 us (32%)
  starting transfers between devices  32.7 us (28%)
  blocking collectives  21.3 us (18%)
  matrix products  8.22 us (7%)
  local copies, waits for them, and re-layouts  7.99 us (7%)
  other arithmetic  5.81 us (5%)
  between operations  2.39 us (2%)
    all_to_all x1, blocking collectives, gather_grads(): got = lax.all_to_all(part, 'cy', 0, 0, tiled=True)  21.3 us
    all_to_all x1, starting transfers between devices, spread_anchors(): lax.all_to_all(jnp.broadcast_to(row[None], (nx,) + row.shape), 'cx', 0, 0...  12.3 us
    all_to_all x1, waiting for transfers between devices, spread_anchors(): lax.all_to_all(jnp.broadcast_to(slots[None], (ny,) + slots.shape), 'cy',...  9.31 us
    all_to_all x1, starting transfers between devices, spread_anchors(): got = lax.all_to_all(part, 'cy', 0, 0, tiled=True)  7.69 us
    all_to_all x1, waiting for transfers between devices, gather_grads(): lax.all_to_all(jnp.broadcast_to(total[None], (ny,) + total.shape), 'cy',...  7.68 us
    all_to_all x1, waiting for transfers between devices, spread_anchors(): lax.all_to_all(jnp.broadcast_to(row[None], (nx,) + row.shape), 'cx', 0, 0...  6.94 us
    all_to_all x1, waiting for transfers between devices, gather_grads(): lax.all_to_all(jnp.repeat(rowsum, rows_per_slot, axis=0), 'cx', 0, 0, til...  6.92 us
    all_to_all x1, waiting for transfers between devices, spread_anchors(): got = lax.all_to_all(part, 'cy', 0, 0, tiled=True)  6.37 us
  transfers between devices with their start and end apart: 6, of which 6 were waited for; matrix products, arithmetic and copies ran while one was open for 5% of the time, Pallas kernels for 0%

profile of v2, /device:TPU:2, one launch (start us, length us, event | category | flops | bytes accessed | tf_op | source)
XLA Modules:
  0.0 116.7 jit_solution(7280412152265139591)
XLA Ops:
  0.6 1.3 %fusion.27 = bf16[]{:T(256)} fusion(s32[4]{0:T(128)} %param.10, s32[]{:T(128)} %add.26), kind=kLoop, calls=%fused_computation.60 | loop fusion | flops 11 | bytes 22 | tf_op jit(solution)/shard_map/reduce_sum | solution.py:110
  2.6 1.5 %multiply_convert_fusion = bf16[1,128,256]{2,1,0:T(8,128)(2,1)} fusion(bf16[1,128,256]{2,1,0:T(8,128)(2,1)} %param.7, f32[]{:T(128)S(6)} %convert.12), kind=kLoop, calls=%fused_computation.43 | loop fusion | flops 98304 | bytes 131076 | tf_op jit(solution)/shard_map/convert_element_type | solution.py:111
  4.1 7.7 %all-to-all-start = ((bf16[8,16,256]{2,1,0:T(8,128)(2,1)}), bf16[8,16,256]{2,1,0:T(8,128)(2,1)S(1)}, u32[]{:S(2)}, u32[]{:S(2)}) async-start(bf16[8,16,256]{2,1,0:T(8,128)(2,1)} %bitcast.1), calls=%async_computation | async-start | bytes 131072 | tf_op jit(solution)/shard_map/all_to_all | solution.py:73
  12.5 1.3 %gather_fusion.1 = s32[2]{0:T(128)S(1)} fusion(s32[4]{0:T(128)} %param.10, s32[1024]{0:T(1024)S(1)} %pad_clamp_fusion), kind=kCustom, calls=%fused_computation.1 | custom fusion | bytes 24 | tf_op jit(solution)/shard_map/gather | solution.py:39
  13.8 6.4 %all-to-all-done = bf16[8,16,256]{2,1,0:T(8,128)(2,1)S(1)} async-done(((bf16[8,16,256]{2,1,0:T(8,128)(2,1)}), bf16[8,16,256]{2,1,0:T(8,128)(2,1)S(1)}, u32[]{:S(2)}, u32[]{:S(2)}) %all-to-all-start) | async-done | bytes 65568 | tf_op jit(solution)/shard_map/all_to_all | solution.py:73
  20.8 12.3 %all-to-all-start.1 = ((bf16[8,16,256]{2,1,0:T(8,128)(2,1)}), bf16[8,16,256]{2,1,0:T(8,128)(2,1)S(1)}, u32[]{:S(2)}, u32[]{:S(2)}) async-start(bf16[8,16,256]{2,1,0:T(8,128)(2,1)} %broadcast_in_dim.34), calls=%async_computation.1 | async-start | bytes 131072 | tf_op jit(solution)/shard_map/all_to_all | solution.py:75
  33.1 6.9 %all-to-all-done.1 = bf16[8,16,256]{2,1,0:T(8,128)(2,1)S(1)} async-done(((bf16[8,16,256]{2,1,0:T(8,128)(2,1)}), bf16[8,16,256]{2,1,0:T(8,128)(2,1)S(1)}, u32[]{:S(2)}, u32[]{:S(2)}) %all-to-all-start.1) | async-done | bytes 65568 | tf_op jit(solution)/shard_map/all_to_all | solution.py:75
  40.0 0.7 broadcast_in_dim.35
  40.8 3.4 %all-to-all-start.2 = ((bf16[8,4,16,256]{3,2,1,0:T(8,128)(2,1)}), bf16[8,4,16,256]{3,2,1,0:T(8,128)(2,1)S(1)}, u32[]{:S(2)}, u32[]{:S(2)}) async-start(bf16[8,4,16,256]{3,2,1,0:T(8,128)(2,1)} %broadcast_in_dim.35), calls=%async_computation.2 | async-start | bytes 524288 | tf_op jit(solution)/shard_map/all_to_all | solution.py:80
  45.3 9.3 %all-to-all-done.2 = bf16[8,4,16,256]{3,2,1,0:T(8,128)(2,1)S(1)} async-done(((bf16[8,4,16,256]{3,2,1,0:T(8,128)(2,1)}), bf16[8,4,16,256]{3,2,1,0:T(8,128)(2,1)S(1)}, u32[]{:S(2)}, u32[]{:S(2)}) %all-to-all-start.2) | async-done | bytes 262176 | tf_op jit(solution)/shard_map/all_to_all | solution.py:80
  55.9 1.2 %multiply_reduce_fusion = (f32[128,8]{0,1:T(8,128)S(1)}, f32[1,128,1,8,128]{1,4,3,2,0:T(8,128)}) fusion(f32[1,128,1,8,128]{1,4,3,2,0:T(8,128)S(1)} %bitcast.208, f32[8,128]{1,0:T(8,128)S(1)} %fusion.5, f32[1,1,8,128,384]{3,4,2,1,0:T(8,128)S(1)} %get-tuple-element.11, f32[8,128]{1,0:T(8,128)S(1)} %get-tuple-element.10, ...), kind=kOutput, calls=%fused_computation.34 | convolution fusion | flops 102300672 | bytes 2830336 | tf_op jit(solution)/shard_map/bkgql,blkd->bqkgd/dot_general | solution.py:47
  58.8 1.3 %collective-permute-start = (bf16[128,1024]{0,1:T(8,128)(2,1)S(1)}, bf16[128,1024]{0,1:T(8,128)(2,1)}, u32[]{:S(2)}, u32[]{:S(2)}) collective-permute-start(bf16[128,1024]{0,1:T(8,128)(2,1)S(1)} %bitcast.202), channel_id=1, source_target_pairs={{512,0},{513,1},{514,2},{515,3},{516,4},{517,5},{518,6},{519,7},{5... | collective-permute-start | bytes 786440 | tf_op jit(solution)/shard_map/ppermute | solution.py:13
  60.6 0.8 fusion.25
  61.4 1.0 collective-permute-done
  62.3 1.4 %convolution_bitcast_fusion.1 = f32[1,384,1,1,128]{1,4,3,2,0:T(8,128)S(1)} fusion(bf16[128,8,128]{0,2,1:T(8,128)(2,1)} %bitcast.31, f32[1,1,8,128,384]{3,4,2,1,0:T(8,128)S(1)} %get-tuple-element.11, f32[8,128]{1,0:T(8,128)S(1)} %fusion.5, f32[8,128]{1,0:T(8,128)S(1)} %get-tuple-element.10), kind=kOutput, calls=%fused_computation.21 | convolution fusion | flops 101842944 | bytes 2039808 | tf_op jit(solution)/shard_map/bkgql,bqkgd->blkd/dot_general | solution.py:57
  63.8 1.1 fusion.18
  64.9 1.4 %fusion.7 = bf16[8,128,384]{1,2,0:T(8,128)(2,1)S(1)} fusion(bf16[128,8,128]{0,2,1:T(8,128)(2,1)} %bitcast.31, f32[8,128]{1,0:T(8,128)S(1)} %bitcast.213, bf16[1,256,1,2,128]{4,1,3,2,0:T(8,128)(2,1)S(1)} %bitcast.200, bf16[1,128,1,2,128]{4,1,3,2,0:T(8,128)(2,1)S(1)} %copy.83, f32[8,128]{1,0:T(8,128)S(1)} %fusion.5, ...), kind=kOutput, calls=%fused_computation.13 | convolution fusion | flops 102825984 | bytes 2830336 | tf_op jit(solution)/shard_map/bqkgd,blkd->bkgql/dot_general | solution.py:50
  67.2 0.8 convolution_select_fusion
  68.0 21.3 %all_to_all.30 = f32[8,4,16,256]{3,1,2,0:T(4,128)S(1)} all-to-all(f32[8,4,16,256]{3,1,2,0:T(4,128)S(1)} %bitcast.195), channel_id=1, replica_groups=mesh['section'=2,'cx'=8,'cy'=8,'head'=8] {'cy'}, dimensions={0} | all-to-all | bytes 1048576 | tf_op jit(solution)/shard_map/all_to_all | solution.py:88
  90.1 4.7 %all-to-all-start.4 = ((f32[8,16,256]{2,1,0:T(8,128)}), f32[8,16,256]{2,1,0:T(8,128)S(1)}, u32[]{:S(2)}, u32[]{:S(2)}) async-start(f32[8,16,256]{2,1,0:T(8,128)} %bitcast.75), calls=%async_computation.4 | async-start | bytes 262144 | tf_op jit(solution)/shard_map/all_to_all | solution.py:90
  96.1 6.9 %all-to-all-done.4 = f32[8,16,256]{2,1,0:T(8,128)S(1)} async-done(((f32[8,16,256]{2,1,0:T(8,128)}), f32[8,16,256]{2,1,0:T(8,128)S(1)}, u32[]{:S(2)}, u32[]{:S(2)}) %all-to-all-start.4) | async-done | bytes 131104 | tf_op jit(solution)/shard_map/all_to_all | solution.py:90
  103.6 3.4 %all-to-all-start.5 = ((f32[8,16,256]{2,1,0:T(8,128)}), f32[8,16,256]{2,1,0:T(8,128)S(1)}, u32[]{:S(2)}, u32[]{:S(2)}) async-start(f32[8,16,256]{2,1,0:T(8,128)} %broadcast_in_dim.44), calls=%async_computation.5 | async-start | bytes 262144 | tf_op jit(solution)/shard_map/all_to_all | solution.py:92
  107.4 0.9 copy.105
  108.3 7.7 %all-to-all-done.5 = f32[8,16,256]{2,1,0:T(8,128)S(1)} async-done(((f32[8,16,256]{2,1,0:T(8,128)}), f32[8,16,256]{2,1,0:T(8,128)S(1)}, u32[]{:S(2)}, u32[]{:S(2)}) %all-to-all-start.5) | async-done | bytes 131104 | tf_op jit(solution)/shard_map/all_to_all | solution.py:92
  (70 shorter events, 9.6 us)
Async XLA Ops:
  0.6 43.6 %copy-start.1 = (bf16[128,1024]{1,0:T(8,128)(2,1)S(1)}, bf16[128,1024]{1,0:T(8,128)(2,1)}, u32[]{:S(2)}) copy-start(bf16[128,1024]{1,0:T(8,128)(2,1)} %param.8) | copy-start | bytes 786436
  4.1 40.5 %copy-start.10 = (bf16[1,128,256]{2,1,0:T(8,128)(2,1)S(1)}, bf16[1,128,256]{2,1,0:T(8,128)(2,1)}, u32[]{:S(2)}) copy-start(bf16[1,128,256]{2,1,0:T(8,128)(2,1)} %param.7) | copy-start | bytes 196612
  4.1 16.1 %all-to-all-start = ((bf16[8,16,256]{2,1,0:T(8,128)(2,1)}), bf16[8,16,256]{2,1,0:T(8,128)(2,1)S(1)}, u32[]{:S(2)}, u32[]{:S(2)}) async-start(bf16[8,16,256]{2,1,0:T(8,128)(2,1)} %bitcast.1), calls=%async_computation | async-start | bytes 131072 | tf_op jit(solution)/shard_map/all_to_all | solution.py:73
  12.4 32.3 %copy-start.9 = (bf16[1,128,1024]{2,1,0:T(8,128)(2,1)S(1)}, bf16[1,128,1024]{2,1,0:T(8,128)(2,1)}, u32[]{:S(2)}) copy-start(bf16[1,128,1024]{2,1,0:T(8,128)(2,1)} %param.6) | copy-start | bytes 786436
  20.8 24.2 %copy-start.11 = (s32[128]{0:T(128)S(1)}, s32[128]{0:T(128)}, u32[]{:S(2)}) copy-start(s32[128]{0:T(128)} %param.9) | copy-start | bytes 1540
  20.8 19.2 %all-to-all-start.1 = ((bf16[8,16,256]{2,1,0:T(8,128)(2,1)}), bf16[8,16,256]{2,1,0:T(8,128)(2,1)S(1)}, u32[]{:S(2)}, u32[]{:S(2)}) async-start(bf16[8,16,256]{2,1,0:T(8,128)(2,1)} %broadcast_in_dim.34), calls=%async_computation.1 | async-start | bytes 131072 | tf_op jit(solution)/shard_map/all_to_all | solution.py:75
  40.8 13.8 %all-to-all-start.2 = ((bf16[8,4,16,256]{3,2,1,0:T(8,128)(2,1)}), bf16[8,4,16,256]{3,2,1,0:T(8,128)(2,1)S(1)}, u32[]{:S(2)}, u32[]{:S(2)}) async-start(bf16[8,4,16,256]{3,2,1,0:T(8,128)(2,1)} %broadcast_in_dim.35), calls=%async_computation.2 | async-start | bytes 524288 | tf_op jit(solution)/shard_map/all_to_all | solution.py:80
  57.6 2.5 %copy-start.4 = (f32[1,384,1,1,128]{1,4,3,2,0:T(8,128)}, f32[1,384,1,1,128]{1,4,3,2,0:T(8,128)S(1)}, u32[]{:S(2)}) copy-start(f32[1,384,1,1,128]{1,4,3,2,0:T(8,128)S(1)} %convolution_bitcast_fusion.3) | copy-start | bytes 589828
  58.4 3.0 %copy-start.2 = (bf16[128,8,128]{2,0,1:T(8,128)(2,1)}, bf16[128,8,128]{2,0,1:T(8,128)(2,1)S(1)}, u32[]{:S(2)}) copy-start(bf16[128,8,128]{2,0,1:T(8,128)(2,1)S(1)} %fusion.8) | copy-start | bytes 786436
  58.4 2.2 %copy-start.12 = (s32[1,2]{1,0:T(1,128)S(1)}, s32[1,2]{1,0:T(1,128)}, u32[]{:S(2)}) copy-start(s32[1,2]{1,0:T(1,128)} %param.11) | copy-start | bytes 28
  58.8 3.6 %collective-permute-start = (bf16[128,1024]{0,1:T(8,128)(2,1)S(1)}, bf16[128,1024]{0,1:T(8,128)(2,1)}, u32[]{:S(2)}, u32[]{:S(2)}) collective-permute-start(bf16[128,1024]{0,1:T(8,128)(2,1)S(1)} %bitcast.202), channel_id=1, source_target_pairs={{512,0},{513,1},{514,2},{515,3},{516,4},{517,5},{518,6},{519,7},{5... | collective-permute-start | bytes 786440 | tf_op jit(solution)/shard_map/ppermute | solution.py:13
  62.3 1.4 %copy-start.8 = (f32[1,128,1,8,128]{1,4,3,2,0:T(8,128)S(1)}, f32[1,128,1,8,128]{1,4,3,2,0:T(8,128)}, u32[]{:S(2)}) copy-start(f32[1,128,1,8,128]{1,4,3,2,0:T(8,128)} %get-tuple-element.13) | copy-start | bytes 1572868
  63.8 2.9 %copy-start.6 = (f32[1,384,1,1,128]{1,4,3,2,0:T(8,128)}, f32[1,384,1,1,128]{1,4,3,2,0:T(8,128)S(1)}, u32[]{:S(2)}) copy-start(f32[1,384,1,1,128]{1,4,3,2,0:T(8,128)S(1)} %convolution_bitcast_fusion.1) | copy-start | bytes 589828
  67.2 27.7 %copy-start = (s32[4]{0:T(128)S(1)}, s32[4]{0:T(128)}, u32[]{:S(2)}) copy-start(s32[4]{0:T(128)} %param.10) | copy-start | bytes 52
  68.0 39.1 %copy-start.3 = (bf16[128,8,128]{2,0,1:T(8,128)(2,1)S(1)}, bf16[128,8,128]{2,0,1:T(8,128)(2,1)}, u32[]{:S(2)}) copy-start(bf16[128,8,128]{2,0,1:T(8,128)(2,1)} %copy-done.2) | copy-start | bytes 786436
  89.4 18.8 %copy-start.5 = (f32[1,384,1,1,128]{1,4,3,2,0:T(8,128)S(1)}, f32[1,384,1,1,128]{1,4,3,2,0:T(8,128)}, u32[]{:S(2)}) copy-start(f32[1,384,1,1,128]{1,4,3,2,0:T(8,128)} %copy-done.4) | copy-start | bytes 589828
  89.4 18.8 %copy-start.7 = (f32[1,384,1,1,128]{1,4,3,2,0:T(8,128)S(1)}, f32[1,384,1,1,128]{1,4,3,2,0:T(8,128)}, u32[]{:S(2)}) copy-start(f32[1,384,1,1,128]{1,4,3,2,0:T(8,128)} %copy-done.6) | copy-start | bytes 589828
  90.1 12.9 %all-to-all-start.4 = ((f32[8,16,256]{2,1,0:T(8,128)}), f32[8,16,256]{2,1,0:T(8,128)S(1)}, u32[]{:S(2)}, u32[]{:S(2)}) async-start(f32[8,16,256]{2,1,0:T(8,128)} %bitcast.75), calls=%async_computation.4 | async-start | bytes 262144 | tf_op jit(solution)/shard_map/all_to_all | solution.py:90
  103.6 12.4 %all-to-all-start.5 = ((f32[8,16,256]{2,1,0:T(8,128)}), f32[8,16,256]{2,1,0:T(8,128)S(1)}, u32[]{:S(2)}, u32[]{:S(2)}) async-start(f32[8,16,256]{2,1,0:T(8,128)} %broadcast_in_dim.44), calls=%async_computation.5 | async-start | bytes 262144 | tf_op jit(solution)/shard_map/all_to_all | solution.py:92

commit v3 on v2

--- a/solution.py
+++ b/solution.py
@@ -57,12 +57,8 @@
     dv = jnp.einsum("bkgql,bqkgd->blkd", pb, c_blocks, preferred_element_type=jnp.float32)
     dkv = jnp.stack([dk, dv], axis=3)
     band_grad = dkv[:, :BLK].reshape(rows, feat)
-    far_grad = dkv[:, BLK:].reshape(per_dev, npick, BLK * feat)
-    onehot = (picks[:, :, None] == jnp.arange(nanch, dtype=jnp.int32)[None, None, :]).astype(
-        jnp.float32
-    )
-    anchor_term = jnp.einsum("ban,bam->nm", onehot, far_grad, precision=lax.Precision.HIGHEST)
-    return (dq.reshape(rows, width), band_grad, anchor_term.reshape(nanch, BLK, feat))
+    far_grad = dkv[:, BLK:].reshape(per_dev * npick, BLK, feat)
+    return (dq.reshape(rows, width), band_grad, far_grad)
 
 
 def spread_anchors(mine, rows_per_slot):
@@ -81,12 +77,21 @@
     return got.transpose(1, 0, 2, 3).reshape(nslot, blk, feat)
 
 
-def gather_grads(acc, rows_per_slot):
+def gather_grads(far, picks, nslot, rows_per_slot):
     ny = lax.axis_size("cy")
-    nslot, blk, feat = acc.shape
-    part = acc.reshape(nslot, ny, blk // ny, feat).transpose(1, 0, 2, 3)
-    got = lax.all_to_all(part, "cy", 0, 0, tiled=True)
-    rowsum = jnp.sum(got, axis=0)
+    npick, blk, feat = far.shape
+    size = (blk // ny) * feat
+    data = far.reshape(npick, ny, size)
+    tag = jnp.broadcast_to(picks.astype(jnp.float32)[:, None, None], (npick, ny, 128))
+    load = jnp.concatenate([data, tag], axis=2).transpose(1, 0, 2)
+    got = lax.all_to_all(load, "cy", 0, 0, tiled=True)
+    vals = got[:, :, :size]
+    ids = got[:, :, size]
+    slot_ids = jnp.arange(nslot, dtype=jnp.float32)
+    rowsum = jnp.sum(
+        jnp.where(ids[None, :, :, None] == slot_ids[:, None, None, None], vals[None], 0.0),
+        axis=(1, 2),
+    ).reshape(nslot, blk // ny, feat)
     got = lax.all_to_all(jnp.repeat(rowsum, rows_per_slot, axis=0), "cx", 0, 0, tiled=True)
     total = jnp.sum(got, axis=0)
     got = lax.all_to_all(jnp.broadcast_to(total[None], (ny,) + total.shape), "cy", 0, 0, tiled=True)
@@ -112,17 +117,27 @@
         jnp.bfloat16
     )
     anchor_kv = spread_anchors(mine, rows_per_slot)
-    dq_first, band_first, term_first = attend(
-        query_rows, keyvals, anchor_kv, out_grad, sentences, anchor_pick, anchor_blocks, blocks
-    )
+    npick = anchor_pick.shape[1]
+
+    def run(cot):
+        return attend(
+            query_rows, keyvals, anchor_kv, cot, sentences, anchor_pick, anchor_blocks, blocks
+        )
+
+    def idle(cot):
+        return (
+            jnp.zeros((rows, query_rows.shape[1]), jnp.float32),
+            jnp.zeros((rows, feat), jnp.float32),
+            jnp.zeros((per_dev * npick, BLK, feat), jnp.float32),
+        )
+
+    dq_first, band_first, far_first = lax.cond(section_one, run, idle, out_grad)
     sent_back = dq_first.astype(jnp.bfloat16)
     arrived = from_behind(sent_back, "section", -1)
-    dq_second, band_second, term_second = attend(
-        query_rows, keyvals, anchor_kv, arrived, sentences, anchor_pick, anchor_blocks, blocks
-    )
+    dq_second, band_second, far_second = lax.cond(section_one, idle, run, arrived)
     band_grad = jnp.where(section_one, band_first, band_second)
-    anchor_term = jnp.where(section_one, term_first, term_second)
-    total = gather_grads(anchor_term, rows_per_slot)
+    far = jnp.where(section_one, far_first, far_second)
+    total = gather_grads(far, anchor_pick.reshape(-1), nanch, rows_per_slot)
     owner = (anchor_blocks[rank] == blocks).astype(jnp.float32)
     owned = owner[:, None, None] * total[None]
     kv_grad = (band_grad + owned.reshape(band_grad.shape)).astype(jnp.bfloat16)

time: 118 us -> 108 us (0.915)
  the two profiles are of different devices: /device:TPU:2 before, /device:TPU:896 now
where the time goes in v3:
time: 108 us
  blocking collectives  43.7 us (40%)
  waiting for transfers between devices  33.2 us (31%)
  starting transfers between devices  11.4 us (11%)
  local copies, waits for them, and re-layouts  8.83 us (8%)
  other arithmetic  6.03 us (6%)
  matrix products  2.23 us (2%)
  between operations  2.12 us (2%)
    all_to_all x1, blocking collectives, spread_anchors(): got = lax.all_to_all(part, 'cy', 0, 0, tiled=True)  15.8 us
    all_to_all x1, blocking collectives, spread_anchors(): lax.all_to_all(jnp.broadcast_to(row[None], (nx,) + row.shape), 'cx', 0, 0...  14.9 us
    all_to_all x1, blocking collectives, gather_grads(): got = lax.all_to_all(load, 'cy', 0, 0, tiled=True)  13 us
    all_to_all x1, waiting for transfers between devices, spread_anchors(): lax.all_to_all(jnp.broadcast_to(slots[None], (ny,) + slots.shape), 'cy',...  10.4 us
    all_to_all x1, waiting for transfers between devices, gather_grads(): lax.all_to_all(jnp.broadcast_to(total[None], (ny,) + total.shape), 'cy',...  8.26 us
    all_to_all x1, waiting for transfers between devices, gather_grads(): lax.all_to_all(jnp.repeat(rowsum, rows_per_slot, axis=0), 'cx', 0, 0, til...  7.73 us
    ppermute x1, waiting for transfers between devices, from_behind(): return lax.ppermute(x, axis, pairs)  6.84 us
    all_to_all x1, starting transfers between devices, spread_anchors(): lax.all_to_all(jnp.broadcast_to(slots[None], (ny,) + slots.shape), 'cy',...  3.41 us
  transfers between devices with their start and end apart: 4, of which 4 were waited for; matrix products, arithmetic and copies ran while one was open for 2% of the time, Pallas kernels for 0%

profile of v3, /device:TPU:896, one launch (start us, length us, event | category | flops | bytes accessed | tf_op | source)
XLA Modules:
  0.0 107.7 jit_solution(10866444587634288471)
XLA Ops:
  0.6 1.3 %fusion.51 = bf16[]{:T(256)} fusion(s32[4]{0:T(128)} %param.14, s32[]{:T(128)} %add.21), kind=kLoop, calls=%fused_computation.96 | loop fusion | flops 11 | bytes 22 | tf_op jit(solution)/shard_map/reduce_sum | solution.py:115
  2.6 0.9 multiply_convert_fusion
  3.4 15.8 %all_to_all.30 = bf16[8,16,256]{2,1,0:T(8,128)(2,1)S(1)} all-to-all(bf16[8,16,256]{2,1,0:T(8,128)(2,1)S(1)} %bitcast.262), channel_id=1, replica_groups=mesh['section'=2,'cx'=8,'cy'=8,'head'=8] {'cy'}, dimensions={0} | all-to-all | bytes 131072 | tf_op jit(solution)/shard_map/all_to_all | solution.py:69
  19.2 14.9 %all_to_all.31 = bf16[8,16,256]{2,1,0:T(8,128)(2,1)S(1)} all-to-all(bf16[8,16,256]{2,1,0:T(8,128)(2,1)S(1)} %broadcast_in_dim.121), channel_id=1, replica_groups=mesh['section'=2,'cx'=8,'cy'=8,'head'=8] {'cx'}, dimensions={0} | all-to-all | bytes 131072 | tf_op jit(solution)/shard_map/all_to_all | solution.py:71
  34.1 0.7 broadcast_in_dim.122
  34.9 3.4 %all-to-all-start.2 = ((bf16[8,4,16,256]{3,2,1,0:T(8,128)(2,1)}), bf16[8,4,16,256]{3,2,1,0:T(8,128)(2,1)S(1)}, u32[]{:S(2)}, u32[]{:S(2)}) async-start(bf16[8,4,16,256]{3,2,1,0:T(8,128)(2,1)} %broadcast_in_dim.122), calls=%async_computation.2 | async-start | bytes 524288 | tf_op jit(solution)/shard_map/all_to_all | solution.py:76
  38.3 10.4 %all-to-all-done.2 = bf16[8,4,16,256]{3,2,1,0:T(8,128)(2,1)S(1)} async-done(((bf16[8,4,16,256]{3,2,1,0:T(8,128)(2,1)}), bf16[8,4,16,256]{3,2,1,0:T(8,128)(2,1)S(1)}, u32[]{:S(2)}, u32[]{:S(2)}) %all-to-all-start.2) | async-done | bytes 262176 | tf_op jit(solution)/shard_map/all_to_all | solution.py:76
  48.7 0.9 conditional.2
  48.8 0.7 broadcast.230
  49.5 1.3 %collective-permute-start = (bf16[128,1024]{0,1:T(8,128)(2,1)}, bf16[128,1024]{0,1:T(8,128)(2,1)S(1)}, u32[]{:S(2)}, u32[]{:S(2)}) collective-permute-start(bf16[128,1024]{0,1:T(8,128)(2,1)} %get-tuple-element.58), channel_id=1, source_target_pairs={{512,0},{513,1},{514,2},{515,3},{516,4},{517,5},{518,6},{519,7},{5... | collective-permute-start | bytes 786440 | tf_op jit(solution)/shard_map/ppermute | solution.py:13
  51.5 6.8 %collective-permute-done = bf16[128,1024]{0,1:T(8,128)(2,1)S(1)} collective-permute-done((bf16[128,1024]{0,1:T(8,128)(2,1)}, bf16[128,1024]{0,1:T(8,128)(2,1)S(1)}, u32[]{:S(2)}, u32[]{:S(2)}) %collective-permute-start) | collective-permute-done | bytes 262176 | tf_op jit(solution)/shard_map/ppermute | solution.py:13
  58.3 8.5 %conditional.3 = (f32[2,128,256]{1,0,2:T(2,128)S(1)}, bf16[128,1024]{1,0:T(8,128)(2,1)S(1)}, f32[128,256]{1,0:T(8,128)S(1)}) conditional(s32[]{:T(128)} %convert_element_type.104, (s32[128]{0:T(128)}, s32[1,2]{1,0:T(1,128)S(1)}, s32[4]{0:T(128)}, s32[]{:T(128)}, bf16[1,128,256]{2,1,0:T(8,128)(2,1)}, ...), branch_computations={%region_8.12_spmd, %region_12.13_spmd} | conditional | flops 610777088 | bytes 19310432 | solution.py:137
  58.4 1.3 %gather_fusion.2 = s32[2]{0:T(128)S(1)} fusion(s32[4]{0:T(128)} %get-tuple-element.43, s32[1024]{0:T(1024)S(1)} %pad_clamp_fusion.1), kind=kCustom, calls=%fused_computation.2 | custom fusion | bytes 24 | tf_op jit(solution)/shard_map/cond/branch_0_fun/gather | solution.py:39
  59.7 0.8 fusion.42
  60.7 1.0 copy.163
  61.8 1.1 %copy.165 = bf16[1,128,1024]{1,2,0:T(8,128)(2,1)S(1)} copy(bf16[1,128,1024]{2,1,0:T(8,128)(2,1)} %get-tuple-element.144) | data formatting | bytes 524288 | tf_op jit(solution)/shard_map
  67.4 13.0 %all_to_all.32 = f32[8,2,4224]{2,1,0:T(2,128)S(1)} all-to-all(f32[8,2,4224]{2,1,0:T(2,128)S(1)} %copy.171), channel_id=1, replica_groups=mesh['section'=2,'cx'=8,'cy'=8,'head'=8] {'cy'}, dimensions={0} | all-to-all | bytes 540672 | tf_op jit(solution)/shard_map/all_to_all | solution.py:87
  81.0 0.7 broadcast_in_dim.128
  81.6 3.4 %all-to-all-start.4 = ((f32[8,16,256]{2,1,0:T(8,128)}), f32[8,16,256]{2,1,0:T(8,128)S(1)}, u32[]{:S(2)}, u32[]{:S(2)}) async-start(f32[8,16,256]{2,1,0:T(8,128)} %bitcast.87), calls=%async_computation.4 | async-start | bytes 262144 | tf_op jit(solution)/shard_map/all_to_all | solution.py:95
  86.3 7.7 %all-to-all-done.4 = f32[8,16,256]{2,1,0:T(8,128)S(1)} async-done(((f32[8,16,256]{2,1,0:T(8,128)}), f32[8,16,256]{2,1,0:T(8,128)S(1)}, u32[]{:S(2)}, u32[]{:S(2)}) %all-to-all-start.4) | async-done | bytes 131104 | tf_op jit(solution)/shard_map/all_to_all | solution.py:95
  94.7 3.4 %all-to-all-start.5 = ((f32[8,16,256]{2,1,0:T(8,128)}), f32[8,16,256]{2,1,0:T(8,128)S(1)}, u32[]{:S(2)}, u32[]{:S(2)}) async-start(f32[8,16,256]{2,1,0:T(8,128)} %broadcast_in_dim.129), calls=%async_computation.5 | async-start | bytes 262144 | tf_op jit(solution)/shard_map/all_to_all | solution.py:97
  98.0 0.7 select_bitcast_fusion
  98.8 8.3 %all-to-all-done.5 = f32[8,16,256]{2,1,0:T(8,128)S(1)} async-done(((f32[8,16,256]{2,1,0:T(8,128)}), f32[8,16,256]{2,1,0:T(8,128)S(1)}, u32[]{:S(2)}, u32[]{:S(2)}) %all-to-all-start.5) | async-done | bytes 131104 | tf_op jit(solution)/shard_map/all_to_all | solution.py:97
  107.1 0.7 fusion.50
  (53 shorter events, 7.3 us)
Async XLA Ops:
  34.9 13.8 %all-to-all-start.2 = ((bf16[8,4,16,256]{3,2,1,0:T(8,128)(2,1)}), bf16[8,4,16,256]{3,2,1,0:T(8,128)(2,1)S(1)}, u32[]{:S(2)}, u32[]{:S(2)}) async-start(bf16[8,4,16,256]{3,2,1,0:T(8,128)(2,1)} %broadcast_in_dim.122), calls=%async_computation.2 | async-start | bytes 524288 | tf_op jit(solution)/shard_map/all_to_all | solution.py:76
  48.7 9.7 %copy-start.2 = (s32[1,2]{1,0:T(1,128)S(1)}, s32[1,2]{1,0:T(1,128)}, u32[]{:S(2)}) copy-start(s32[1,2]{1,0:T(1,128)} %param.15) | copy-start | bytes 28
  49.5 8.8 %collective-permute-start = (bf16[128,1024]{0,1:T(8,128)(2,1)}, bf16[128,1024]{0,1:T(8,128)(2,1)S(1)}, u32[]{:S(2)}, u32[]{:S(2)}) collective-permute-start(bf16[128,1024]{0,1:T(8,128)(2,1)} %get-tuple-element.58), channel_id=1, source_target_pairs={{512,0},{513,1},{514,2},{515,3},{516,4},{517,5},{518,6},{519,7},{5... | collective-permute-start | bytes 786440 | tf_op jit(solution)/shard_map/ppermute | solution.py:13
  67.2 17.8 %copy-start = (s32[4]{0:T(128)S(1)}, s32[4]{0:T(128)}, u32[]{:S(2)}) copy-start(s32[4]{0:T(128)} %param.14) | copy-start | bytes 52
  81.6 12.4 %all-to-all-start.4 = ((f32[8,16,256]{2,1,0:T(8,128)}), f32[8,16,256]{2,1,0:T(8,128)S(1)}, u32[]{:S(2)}, u32[]{:S(2)}) async-start(f32[8,16,256]{2,1,0:T(8,128)} %bitcast.87), calls=%async_computation.4 | async-start | bytes 262144 | tf_op jit(solution)/shard_map/all_to_all | solution.py:95
  94.7 12.4 %all-to-all-start.5 = ((f32[8,16,256]{2,1,0:T(8,128)}), f32[8,16,256]{2,1,0:T(8,128)S(1)}, u32[]{:S(2)}, u32[]{:S(2)}) async-start(f32[8,16,256]{2,1,0:T(8,128)} %broadcast_in_dim.129), calls=%async_computation.5 | async-start | bytes 262144 | tf_op jit(solution)/shard_map/all_to_all | solution.py:97

commit v4 on v3

--- a/solution.py
+++ b/solution.py
@@ -13,23 +13,28 @@
     return lax.ppermute(x, axis, pairs)
 
 
-def attend(query_rows, keyvals, anchor_kv, cot, sentences, picks, anchor_blocks, blocks):
-    rows, width = query_rows.shape
-    feat = keyvals.shape[1]
+def gather_keys(keyvals, anchor_kv, picks):
+    rows, feat = keyvals.shape
     kvh = feat // (2 * HEAD_SIZE)
-    group_size = width // (kvh * HEAD_SIZE)
     per_dev = rows // BLK
     npick = picks.shape[1]
     nanch = anchor_kv.shape[0]
-    scale = HEAD_SIZE ** (-0.5)
-    q_blocks = query_rows.reshape(per_dev, BLK, kvh, group_size, HEAD_SIZE)
     own = keyvals.reshape(per_dev, BLK, kvh, 2, HEAD_SIZE)
     far = anchor_kv.reshape(nanch, BLK, kvh, 2, HEAD_SIZE)[picks].reshape(
         per_dev, npick * BLK, kvh, 2, HEAD_SIZE
     )
     keys = jnp.concatenate([own, far], axis=1)
-    kk = keys[:, :, :, 0]
-    vv = keys[:, :, :, 1]
+    return keys[:, :, :, 0], keys[:, :, :, 1]
+
+
+def forward(query_rows, kk, sentences, picks, anchor_blocks, blocks):
+    rows, width = query_rows.shape
+    kvh = kk.shape[2]
+    group_size = width // (kvh * HEAD_SIZE)
+    per_dev = rows // BLK
+    npick = picks.shape[1]
+    scale = HEAD_SIZE ** (-0.5)
+    q_blocks = query_rows.reshape(per_dev, BLK, kvh, group_size, HEAD_SIZE)
     score = (
         jnp.einsum("bqkgd,blkd->bkgql", q_blocks, kk, preferred_element_type=jnp.float32) * scale
     )
@@ -42,7 +47,17 @@
     score = jnp.where(mask, score, jnp.float32(-1e30))
     top = jnp.max(score, axis=-1, keepdims=True)
     expo = jnp.exp(score - top)
-    probs = expo / jnp.sum(expo, axis=-1, keepdims=True)
+    return expo / jnp.sum(expo, axis=-1, keepdims=True)
+
+
+def backward(query_rows, kk, vv, probs, cot):
+    rows, width = query_rows.shape
+    kvh = kk.shape[2]
+    feat = 2 * kvh * HEAD_SIZE
+    group_size = width // (kvh * HEAD_SIZE)
+    per_dev = rows // BLK
+    scale = HEAD_SIZE ** (-0.5)
+    q_blocks = query_rows.reshape(per_dev, BLK, kvh, group_size, HEAD_SIZE)
     pb = probs.astype(jnp.bfloat16)
     outp = jnp.einsum("bkgql,blkd->bqkgd", pb, vv, preferred_element_type=jnp.float32)
     c_blocks = cot.reshape(per_dev, BLK, kvh, group_size, HEAD_SIZE)
@@ -57,7 +72,7 @@
     dv = jnp.einsum("bkgql,bqkgd->blkd", pb, c_blocks, preferred_element_type=jnp.float32)
     dkv = jnp.stack([dk, dv], axis=3)
     band_grad = dkv[:, :BLK].reshape(rows, feat)
-    far_grad = dkv[:, BLK:].reshape(per_dev * npick, BLK, feat)
+    far_grad = dkv[:, BLK:].reshape(-1, BLK, feat)
     return (dq.reshape(rows, width), band_grad, far_grad)
 
 
@@ -112,29 +127,41 @@
     blocks = ctx * per_dev + jnp.arange(per_dev, dtype=jnp.int32)
     kv_blocks = keyvals.reshape(per_dev, BLK, feat)
     hit = anchor_blocks[None, :] == blocks[:, None]
-    holder = jnp.sum(hit.astype(jnp.float32), axis=1).astype(jnp.bfloat16)
-    mine = jnp.einsum("b,bmf->mf", holder, kv_blocks, preferred_element_type=jnp.float32).astype(
-        jnp.bfloat16
-    )
+    holder = jnp.any(hit, axis=1)[:, None, None]
+    mine = jnp.where(holder, kv_blocks, jnp.zeros_like(kv_blocks)).sum(axis=0, dtype=jnp.float32)
+    mine = mine.astype(jnp.bfloat16)
     anchor_kv = spread_anchors(mine, rows_per_slot)
     npick = anchor_pick.shape[1]
+    kk, vv = gather_keys(keyvals, anchor_kv, anchor_pick)
 
-    def run(cot):
-        return attend(
-            query_rows, keyvals, anchor_kv, cot, sentences, anchor_pick, anchor_blocks, blocks
-        )
-
-    def idle(cot):
+    def zeros():
         return (
             jnp.zeros((rows, query_rows.shape[1]), jnp.float32),
             jnp.zeros((rows, feat), jnp.float32),
             jnp.zeros((per_dev * npick, BLK, feat), jnp.float32),
         )
 
-    dq_first, band_first, far_first = lax.cond(section_one, run, idle, out_grad)
+    def probs_of():
+        return forward(query_rows, kk, sentences, anchor_pick, anchor_blocks, blocks)
+
+    def second_layer(cot):
+        probs = probs_of()
+        return (probs,) + backward(query_rows, kk, vv, probs, cot)
+
+    def first_layer_probs(cot):
+        return (probs_of(),) + zeros()
+
+    probs, dq_first, band_first, far_first = lax.cond(
+        section_one, second_layer, first_layer_probs, out_grad
+    )
     sent_back = dq_first.astype(jnp.bfloat16)
     arrived = from_behind(sent_back, "section", -1)
-    dq_second, band_second, far_second = lax.cond(section_one, idle, run, arrived)
+    dq_second, band_second, far_second = lax.cond(
+        section_one,
+        lambda cot: zeros(),
+        lambda cot: backward(query_rows, kk, vv, probs, cot),
+        arrived,
+    )
     band_grad = jnp.where(section_one, band_first, band_second)
     far = jnp.where(section_one, far_first, far_second)
     total = gather_grads(far, anchor_pick.reshape(-1), nanch, rows_per_slot)

time: 108 us -> 104 us (0.963)
  the two profiles are of different devices: /device:TPU:896 before, /device:TPU:2 now
where the time goes in v4:
time: 104 us
  blocking collectives  46.3 us (45%)
  waiting for transfers between devices  26.3 us (25%)
  starting transfers between devices  12.9 us (12%)
  local copies, waits for them, and re-layouts  8.76 us (8%)
  other arithmetic  4.48 us (4%)
  matrix products  3.07 us (3%)
  between operations  1.57 us (2%)
    all_to_all x1, blocking collectives, spread_anchors(): lax.all_to_all(jnp.broadcast_to(row[None], (nx,) + row.shape), 'cx', 0, 0...  16.7 us
    all_to_all x1, blocking collectives, spread_anchors(): got = lax.all_to_all(part, 'cy', 0, 0, tiled=True)  16.5 us
    all_to_all x1, blocking collectives, gather_grads(): got = lax.all_to_all(load, 'cy', 0, 0, tiled=True)  13.1 us
    all_to_all x1, waiting for transfers between devices, spread_anchors(): lax.all_to_all(jnp.broadcast_to(slots[None], (ny,) + slots.shape), 'cy',...  9.25 us
    all_to_all x1, waiting for transfers between devices, gather_grads(): lax.all_to_all(jnp.broadcast_to(total[None], (ny,) + total.shape), 'cy',...  8.25 us
    all_to_all x1, waiting for transfers between devices, gather_grads(): lax.all_to_all(jnp.repeat(rowsum, rows_per_slot, axis=0), 'cx', 0, 0, til...  6.41 us
    all_to_all x1, starting transfers between devices, gather_grads(): lax.all_to_all(jnp.repeat(rowsum, rows_per_slot, axis=0), 'cx', 0, 0, til...  4.73 us
    all_to_all x1, starting transfers between devices, spread_anchors(): lax.all_to_all(jnp.broadcast_to(slots[None], (ny,) + slots.shape), 'cy',...  3.56 us
  transfers between devices with their start and end apart: 4, of which 4 were waited for; matrix products, arithmetic and copies ran while one was open for 2% of the time, Pallas kernels for 0%

profile of v4, /device:TPU:2, one launch (start us, length us, event | category | flops | bytes accessed | tf_op | source)
XLA Modules:
  0.0 103.5 jit_solution(16153529942214928546)
XLA Ops:
  0.6 1.3 %compare_reduce_fusion = pred[]{:T(512)} fusion(s32[4]{0:T(128)} %param.14, s32[]{:T(128)} %add.22), kind=kLoop, calls=%fused_computation.96 | loop fusion | flops 7 | bytes 21 | tf_op jit(solution)/shard_map/reduce_or | solution.py:130
  1.9 0.7 broadcast_select_fusion.1
  2.6 16.5 %all_to_all.30 = bf16[8,16,256]{2,1,0:T(8,128)(2,1)S(1)} all-to-all(bf16[8,16,256]{2,1,0:T(8,128)(2,1)S(1)} %bitcast.277), channel_id=1, replica_groups=mesh['section'=2,'cx'=8,'cy'=8,'head'=8] {'cy'}, dimensions={0} | all-to-all | bytes 131072 | tf_op jit(solution)/shard_map/all_to_all | solution.py:84
  19.2 16.7 %all_to_all.31 = bf16[8,16,256]{2,1,0:T(8,128)(2,1)S(1)} all-to-all(bf16[8,16,256]{2,1,0:T(8,128)(2,1)S(1)} %broadcast_in_dim.136), channel_id=1, replica_groups=mesh['section'=2,'cx'=8,'cy'=8,'head'=8] {'cx'}, dimensions={0} | all-to-all | bytes 131072 | tf_op jit(solution)/shard_map/all_to_all | solution.py:86
  35.9 0.7 broadcast_in_dim.137
  36.6 3.6 %all-to-all-start.2 = ((bf16[8,4,16,256]{3,2,1,0:T(8,128)(2,1)}), bf16[8,4,16,256]{3,2,1,0:T(8,128)(2,1)S(1)}, u32[]{:S(2)}, u32[]{:S(2)}) async-start(bf16[8,4,16,256]{3,2,1,0:T(8,128)(2,1)} %broadcast_in_dim.137), calls=%async_computation.2 | async-start | bytes 524288 | tf_op jit(solution)/shard_map/all_to_all | solution.py:91
  40.2 1.0 copy.180
  41.3 9.3 %all-to-all-done.2 = bf16[8,4,16,256]{3,2,1,0:T(8,128)(2,1)S(1)} async-done(((bf16[8,4,16,256]{3,2,1,0:T(8,128)(2,1)}), bf16[8,4,16,256]{3,2,1,0:T(8,128)(2,1)S(1)}, u32[]{:S(2)}, u32[]{:S(2)}) %all-to-all-start.2) | async-done | bytes 262176 | tf_op jit(solution)/shard_map/all_to_all | solution.py:91
  51.4 3.5 %conditional.2 = (f32[1,1,8,128,384]{3,4,2,1,0:T(8,128)S(1)}, f32[2,128,256]{1,0,2:T(2,128)S(1)}, bf16[128,1024]{0,1:T(8,128)(2,1)}, bf16[128,1024]{1,0:T(8,128)(2,1)S(1)}, f32[128,256]{1,0:T(8,128)}) conditional(s32[]{:T(128)} %convert_element_type.104, (s32[128]{0:T(128)S(1)}, s32[1,2]{1,0:T(1,128)S(1)}, s32[4]{0:T(128)S(1)}, s32[]{:T(128)}, ...), branch_computations={%region_3.6_spmd, %region_6.0_spmd} | conditional | flops 609597440 | bytes 32016288 | solution.py:154
  53.4 0.7 broadcast.240
  54.9 1.3 %collective-permute-start = (bf16[128,1024]{0,1:T(8,128)(2,1)}, bf16[128,1024]{0,1:T(8,128)(2,1)S(1)}, u32[]{:S(2)}, u32[]{:S(2)}) collective-permute-start(bf16[128,1024]{0,1:T(8,128)(2,1)} %get-tuple-element.68), channel_id=1, source_target_pairs={{512,0},{513,1},{514,2},{515,3},{516,4},{517,5},{518,6},{519,7},{5... | collective-permute-start | bytes 786440 | tf_op jit(solution)/shard_map/ppermute | solution.py:13
  56.2 2.3 %collective-permute-done = bf16[128,1024]{0,1:T(8,128)(2,1)S(1)} collective-permute-done((bf16[128,1024]{0,1:T(8,128)(2,1)}, bf16[128,1024]{0,1:T(8,128)(2,1)S(1)}, u32[]{:S(2)}, u32[]{:S(2)}) %collective-permute-start) | collective-permute-done | bytes 262176 | tf_op jit(solution)/shard_map/ppermute | solution.py:13
  58.5 4.0 %conditional.3 = (f32[2,128,256]{1,0,2:T(2,128)S(1)}, bf16[128,1024]{1,0:T(8,128)(2,1)S(1)}, f32[128,256]{1,0:T(8,128)S(1)}) conditional(s32[]{:T(128)} %convert_element_type.104, (bf16[1,384,1,128]{3,1,2,0:T(8,128)(2,1)S(1)}, bf16[128,1024]{0,1:T(8,128)(2,1)S(1)}, f32[1,1,8,128,384]{3,4,2,1,0:T(8,128)S(1)}, bf16[1,128,1024]{2,1,0:T(8,128)(2,1)S(1)}, ...), branch_computations={%region_10.12_spmd, %region_12.13_spmd} | conditional | flops 506084352 | bytes 12099608 | solution.py:159
  59.2 0.8 copy.191
  60.0 1.3 %fusion.7 = f32[1,384,1,1,128]{1,4,3,2,0:T(8,128)S(1)} fusion(bf16[8,128,384]{1,2,0:T(8,128)(2,1)S(1)} %fusion.2, bf16[128,8,128]{0,2,1:T(8,128)(2,1)} %bitcast.266), kind=kOutput, calls=%fused_computation.15 | convolution fusion | flops 100712448 | bytes 1245184 | tf_op jit(solution)/shard_map/cond/branch_0_fun/bkgql,bqkgd->blkd/dot_general | solution.py:69
  63.1 13.1 %all_to_all.32 = f32[8,2,4224]{2,1,0:T(2,128)S(1)} all-to-all(f32[8,2,4224]{2,1,0:T(2,128)S(1)} %copy.198), channel_id=1, replica_groups=mesh['section'=2,'cx'=8,'cy'=8,'head'=8] {'cy'}, dimensions={0} | all-to-all | bytes 540672 | tf_op jit(solution)/shard_map/all_to_all | solution.py:102
  76.8 0.7 broadcast_in_dim.144
  77.4 4.7 %all-to-all-start.4 = ((f32[8,16,256]{2,1,0:T(8,128)}), f32[8,16,256]{2,1,0:T(8,128)S(1)}, u32[]{:S(2)}, u32[]{:S(2)}) async-start(f32[8,16,256]{2,1,0:T(8,128)} %bitcast.95), calls=%async_computation.4 | async-start | bytes 262144 | tf_op jit(solution)/shard_map/all_to_all | solution.py:110
  83.4 6.4 %all-to-all-done.4 = f32[8,16,256]{2,1,0:T(8,128)S(1)} async-done(((f32[8,16,256]{2,1,0:T(8,128)}), f32[8,16,256]{2,1,0:T(8,128)S(1)}, u32[]{:S(2)}, u32[]{:S(2)}) %all-to-all-start.4) | async-done | bytes 131104 | tf_op jit(solution)/shard_map/all_to_all | solution.py:110
  89.8 0.7 broadcast_in_dim.145
  90.5 3.4 %all-to-all-start.5 = ((f32[8,16,256]{2,1,0:T(8,128)}), f32[8,16,256]{2,1,0:T(8,128)S(1)}, u32[]{:S(2)}, u32[]{:S(2)}) async-start(f32[8,16,256]{2,1,0:T(8,128)} %broadcast_in_dim.145), calls=%async_computation.5 | async-start | bytes 262144 | tf_op jit(solution)/shard_map/all_to_all | solution.py:112
  93.9 0.7 select_bitcast_fusion
  94.6 8.3 %all-to-all-done.5 = f32[8,16,256]{2,1,0:T(8,128)S(1)} async-done(((f32[8,16,256]{2,1,0:T(8,128)}), f32[8,16,256]{2,1,0:T(8,128)S(1)}, u32[]{:S(2)}, u32[]{:S(2)}) %all-to-all-start.5) | async-done | bytes 131104 | tf_op jit(solution)/shard_map/all_to_all | solution.py:112
  102.9 0.7 fusion.42
  (68 shorter events, 7.0 us)
Async XLA Ops:
  0.6 40.6 %copy-start.9 = (s32[1,2]{1,0:T(1,128)S(1)}, s32[1,2]{1,0:T(1,128)}, u32[]{:S(2)}) copy-start(s32[1,2]{1,0:T(1,128)} %param.15) | copy-start | bytes 28
  36.6 14.7 %copy-start = (s32[4]{0:T(128)S(1)}, s32[4]{0:T(128)}, u32[]{:S(2)}) copy-start(s32[4]{0:T(128)} %param.14) | copy-start | bytes 52
  36.6 14.7 %copy-start.3 = (bf16[1,128,1024]{2,1,0:T(8,128)(2,1)S(1)}, bf16[1,128,1024]{2,1,0:T(8,128)(2,1)}, u32[]{:S(2)}) copy-start(bf16[1,128,1024]{2,1,0:T(8,128)(2,1)} %param.10) | copy-start | bytes 786436
  36.6 14.7 %copy-start.7 = (bf16[128,1024]{1,0:T(8,128)(2,1)S(1)}, bf16[128,1024]{1,0:T(8,128)(2,1)}, u32[]{:S(2)}) copy-start(bf16[128,1024]{1,0:T(8,128)(2,1)} %param.12) | copy-start | bytes 786436
  36.6 14.8 %copy-start.8 = (s32[128]{0:T(128)S(1)}, s32[128]{0:T(128)}, u32[]{:S(2)}) copy-start(s32[128]{0:T(128)} %param.13) | copy-start | bytes 1540
  36.6 14.0 %all-to-all-start.2 = ((bf16[8,4,16,256]{3,2,1,0:T(8,128)(2,1)}), bf16[8,4,16,256]{3,2,1,0:T(8,128)(2,1)S(1)}, u32[]{:S(2)}, u32[]{:S(2)}) async-start(bf16[8,4,16,256]{3,2,1,0:T(8,128)(2,1)} %broadcast_in_dim.137), calls=%async_computation.2 | async-start | bytes 524288 | tf_op jit(solution)/shard_map/all_to_all | solution.py:91
  54.9 3.6 %copy-start.5 = (bf16[128,1024]{1,0:T(8,128)(2,1)}, bf16[128,1024]{1,0:T(8,128)(2,1)S(1)}, u32[]{:S(2)}) copy-start(bf16[128,1024]{1,0:T(8,128)(2,1)S(1)} %get-tuple-element.191) | copy-start | bytes 786436
  54.9 3.6 %copy-start.4 = (f32[2,128,256]{1,0,2:T(2,128)}, f32[2,128,256]{1,0,2:T(2,128)S(1)}, u32[]{:S(2)}) copy-start(f32[2,128,256]{1,0,2:T(2,128)S(1)} %get-tuple-element.73) | copy-start | bytes 786436
  54.9 3.6 %collective-permute-start = (bf16[128,1024]{0,1:T(8,128)(2,1)}, bf16[128,1024]{0,1:T(8,128)(2,1)S(1)}, u32[]{:S(2)}, u32[]{:S(2)}) collective-permute-start(bf16[128,1024]{0,1:T(8,128)(2,1)} %get-tuple-element.68), channel_id=1, source_target_pairs={{512,0},{513,1},{514,2},{515,3},{516,4},{517,5},{518,6},{519,7},{5... | collective-permute-start | bytes 786440 | tf_op jit(solution)/shard_map/ppermute | solution.py:13
  63.0 30.8 %copy-start.6 = (bf16[128,1024]{1,0:T(8,128)(2,1)S(1)}, bf16[128,1024]{1,0:T(8,128)(2,1)}, u32[]{:S(2)}) copy-start(bf16[128,1024]{1,0:T(8,128)(2,1)} %copy-done.5) | copy-start | bytes 786436
  77.4 12.4 %all-to-all-start.4 = ((f32[8,16,256]{2,1,0:T(8,128)}), f32[8,16,256]{2,1,0:T(8,128)S(1)}, u32[]{:S(2)}, u32[]{:S(2)}) async-start(f32[8,16,256]{2,1,0:T(8,128)} %bitcast.95), calls=%async_computation.4 | async-start | bytes 262144 | tf_op jit(solution)/shard_map/all_to_all | solution.py:110
  90.5 12.4 %all-to-all-start.5 = ((f32[8,16,256]{2,1,0:T(8,128)}), f32[8,16,256]{2,1,0:T(8,128)S(1)}, u32[]{:S(2)}, u32[]{:S(2)}) async-start(f32[8,16,256]{2,1,0:T(8,128)} %broadcast_in_dim.145), calls=%async_computation.5 | async-start | bytes 262144 | tf_op jit(solution)/shard_map/all_to_all | solution.py:112

commit v5 on v4

--- a/solution.py
+++ b/solution.py
@@ -134,41 +134,22 @@
     npick = anchor_pick.shape[1]
     kk, vv = gather_keys(keyvals, anchor_kv, anchor_pick)
 
-    def zeros():
-        return (
-            jnp.zeros((rows, query_rows.shape[1]), jnp.float32),
-            jnp.zeros((rows, feat), jnp.float32),
-            jnp.zeros((per_dev * npick, BLK, feat), jnp.float32),
-        )
+    probs = forward(query_rows, kk, sentences, anchor_pick, anchor_blocks, blocks)
 
-    def probs_of():
-        return forward(query_rows, kk, sentences, anchor_pick, anchor_blocks, blocks)
-
-    def second_layer(cot):
-        probs = probs_of()
-        return (probs,) + backward(query_rows, kk, vv, probs, cot)
-
-    def first_layer_probs(cot):
-        return (probs_of(),) + zeros()
-
-    probs, dq_first, band_first, far_first = lax.cond(
-        section_one, second_layer, first_layer_probs, out_grad
+    sent_back = lax.cond(
+        section_one,
+        lambda cot: backward(query_rows, kk, vv, probs, cot)[0].astype(jnp.bfloat16),
+        lambda cot: cot,
+        out_grad,
     )
-    sent_back = dq_first.astype(jnp.bfloat16)
     arrived = from_behind(sent_back, "section", -1)
-    dq_second, band_second, far_second = lax.cond(
-        section_one,
-        lambda cot: zeros(),
-        lambda cot: backward(query_rows, kk, vv, probs, cot),
-        arrived,
-    )
-    band_grad = jnp.where(section_one, band_first, band_second)
-    far = jnp.where(section_one, far_first, far_second)
+    cot = jnp.where(section_one, out_grad, arrived)
+    dq, band_grad, far = backward(query_rows, kk, vv, probs, cot)
     total = gather_grads(far, anchor_pick.reshape(-1), nanch, rows_per_slot)
     owner = (anchor_blocks[rank] == blocks).astype(jnp.float32)
     owned = owner[:, None, None] * total[None]
     kv_grad = (band_grad + owned.reshape(band_grad.shape)).astype(jnp.bfloat16)
-    input_grad = jnp.where(section_one, sent_back, dq_second.astype(jnp.bfloat16))
+    input_grad = jnp.where(section_one, sent_back, dq.astype(jnp.bfloat16))
     return (input_grad[None], kv_grad[None])
 
 

time: 104 us -> 110 us (1.058)
  blocking collectives: 46.3 us -> 0 us
  waiting for transfers between devices: 26.3 us -> 51.4 us
  starting transfers between devices: 12.9 us -> 35.9 us
  other arithmetic: 4.48 us -> 7.95 us
    all_to_all x3 -> x0, blocking collectives: 46.3 us -> none  [the longest x1 16.7 us: spread_anchors(): lax.all_to_all(jnp.broadcast_to(row[None], (nx,) + row.shape), 'cx', 0, 0...]
    all_to_all x0 -> x3, waiting for transfers between devices: none -> 25.4 us  [the longest x1 12.1 us: gather_grads(): got = lax.all_to_all(load, 'cy', 0, 0, tiled=True)]
    all_to_all x0 -> x3, starting transfers between devices: none -> 23.1 us  [the longest x1 12.1 us: spread_anchors(): lax.all_to_all(jnp.broadcast_to(row[None], (nx,) + row.shape), 'cx', 0, 0...]
    ppermute x1, waiting for transfers between devices: 2.34 us -> 0.6 us  [from_behind(): return lax.ppermute(x, axis, pairs)]
    another operation x6 -> x3, local copies, waits for them, and re-layouts: 2.5 us -> 0.9 us
    all_to_all x1, waiting for transfers between devices: 6.41 us -> 7.55 us  [gather_grads(): lax.all_to_all(jnp.repeat(rowsum, rows_per_slot, axis=0), 'cx', 0, 0, til...]
    reduce_sum x0 -> x1, other arithmetic: none -> 1.1 us  [backward(): jnp.sum(c_blocks.astype(jnp.float32) * outp, axis=-1).transpose(0, 2, 3, 1)]
  transfers between devices with their start and end apart: 4 -> 7, of which waited for: 4 -> 7; matrix products, arithmetic and copies ran while one was open for 2% -> 6% of each run, Pallas kernels for 0% -> 0%
where the time goes in v5:
time: 110 us; the launch traced here: 109 us
  waiting for transfers between devices  51.4 us (47%)
  starting transfers between devices  35.9 us (33%)
  local copies, waits for them, and re-layouts  9.47 us (9%)
  other arithmetic  7.95 us (7%)
  matrix products  2.92 us (3%)
  between operations  1.74 us (2%)
    all_to_all x1, starting transfers between devices, spread_anchors(): lax.all_to_all(jnp.broadcast_to(row[None], (nx,) + row.shape), 'cx', 0, 0...  12.1 us
    all_to_all x1, waiting for transfers between devices, gather_grads(): got = lax.all_to_all(load, 'cy', 0, 0, tiled=True)  12.1 us
    all_to_all x1, waiting for transfers between devices, spread_anchors(): lax.all_to_all(jnp.broadcast_to(slots[None], (ny,) + slots.shape), 'cy',...  9.63 us
    all_to_all x1, waiting for transfers between devices, gather_grads(): lax.all_to_all(jnp.broadcast_to(total[None], (ny,) + total.shape), 'cy',...  8.25 us
    all_to_all x1, starting transfers between devices, spread_anchors(): got = lax.all_to_all(part, 'cy', 0, 0, tiled=True)  7.56 us
    all_to_all x1, waiting for transfers between devices, gather_grads(): lax.all_to_all(jnp.repeat(rowsum, rows_per_slot, axis=0), 'cx', 0, 0, til...  7.55 us
    all_to_all x1, waiting for transfers between devices, spread_anchors(): lax.all_to_all(jnp.broadcast_to(row[None], (nx,) + row.shape), 'cx', 0, 0...  6.94 us
    all_to_all x1, waiting for transfers between devices, spread_anchors(): got = lax.all_to_all(part, 'cy', 0, 0, tiled=True)  6.34 us
  transfers between devices with their start and end apart: 7, of which 7 were waited for; matrix products, arithmetic and copies ran while one was open for 6% of the time, Pallas kernels for 0%

profile of v5, /device:TPU:2, one launch (start us, length us, event | category | flops | bytes accessed | tf_op | source)
XLA Modules:
  0.0 109.4 jit_solution(5547894110318741779)
XLA Ops:
  0.7 1.3 %compare_reduce_fusion = pred[]{:T(512)} fusion(s32[4]{0:T(128)} %param.12, s32[]{:T(128)} %add.24), kind=kLoop, calls=%fused_computation.62 | loop fusion | flops 7 | bytes 21 | tf_op jit(solution)/shard_map/reduce_or | solution.py:130
  2.0 1.3 %broadcast_select_fusion.1 = bf16[1,128,256]{2,1,0:T(8,128)(2,1)} fusion(bf16[1,128,256]{2,1,0:T(8,128)(2,1)} %param.9, pred[]{:T(512)} %compare_reduce_fusion), kind=kLoop, calls=%fused_computation.58 | loop fusion | flops 32768 | bytes 131073 | tf_op jit(solution)/shard_map/jit(_where)/select_n | solution.py:131
  3.3 7.6 %all-to-all-start = ((bf16[8,16,256]{2,1,0:T(8,128)(2,1)}), bf16[8,16,256]{2,1,0:T(8,128)(2,1)S(1)}, u32[]{:S(2)}, u32[]{:S(2)}) async-start(bf16[8,16,256]{2,1,0:T(8,128)(2,1)} %bitcast.22), calls=%async_computation | async-start | bytes 131072 | tf_op jit(solution)/shard_map/all_to_all | solution.py:84
  10.9 0.7 convert_bitcast_fusion.1
  11.6 1.3 %gather_fusion.1 = s32[2]{0:T(128)S(1)} fusion(s32[4]{0:T(128)} %param.12, s32[1024]{0:T(1024)S(1)} %pad_clamp_fusion), kind=kCustom, calls=%fused_computation.1 | custom fusion | bytes 24 | tf_op jit(solution)/shard_map/gather | solution.py:44
  12.9 6.3 %all-to-all-done = bf16[8,16,256]{2,1,0:T(8,128)(2,1)S(1)} async-done(((bf16[8,16,256]{2,1,0:T(8,128)(2,1)}), bf16[8,16,256]{2,1,0:T(8,128)(2,1)S(1)}, u32[]{:S(2)}, u32[]{:S(2)}) %all-to-all-start) | async-done | bytes 65568 | tf_op jit(solution)/shard_map/all_to_all | solution.py:84
  19.9 12.1 %all-to-all-start.1 = ((bf16[8,16,256]{2,1,0:T(8,128)(2,1)}), bf16[8,16,256]{2,1,0:T(8,128)(2,1)S(1)}, u32[]{:S(2)}, u32[]{:S(2)}) async-start(bf16[8,16,256]{2,1,0:T(8,128)(2,1)} %broadcast_in_dim.104), calls=%async_computation.1 | async-start | bytes 131072 | tf_op jit(solution)/shard_map/all_to_all | solution.py:86
  32.0 6.9 %all-to-all-done.1 = bf16[8,16,256]{2,1,0:T(8,128)(2,1)S(1)} async-done(((bf16[8,16,256]{2,1,0:T(8,128)(2,1)}), bf16[8,16,256]{2,1,0:T(8,128)(2,1)S(1)}, u32[]{:S(2)}, u32[]{:S(2)}) %all-to-all-start.1) | async-done | bytes 65568 | tf_op jit(solution)/shard_map/all_to_all | solution.py:86
  39.0 0.7 broadcast_in_dim.105
  39.7 3.4 %all-to-all-start.2 = ((bf16[8,4,16,256]{3,2,1,0:T(8,128)(2,1)}), bf16[8,4,16,256]{3,2,1,0:T(8,128)(2,1)S(1)}, u32[]{:S(2)}, u32[]{:S(2)}) async-start(bf16[8,4,16,256]{3,2,1,0:T(8,128)(2,1)} %broadcast_in_dim.105), calls=%async_computation.2 | async-start | bytes 524288 | tf_op jit(solution)/shard_map/all_to_all | solution.py:91
  43.9 9.6 %all-to-all-done.2 = bf16[8,4,16,256]{3,2,1,0:T(8,128)(2,1)S(1)} async-done(((bf16[8,4,16,256]{3,2,1,0:T(8,128)(2,1)}), bf16[8,4,16,256]{3,2,1,0:T(8,128)(2,1)S(1)}, u32[]{:S(2)}, u32[]{:S(2)}) %all-to-all-start.2) | async-done | bytes 262176 | tf_op jit(solution)/shard_map/all_to_all | solution.py:91
  55.9 1.3 %collective-permute-start = (bf16[128,1024]{1,0:T(8,128)(2,1)S(1)}, bf16[128,1024]{1,0:T(8,128)(2,1)}, u32[]{:S(2)}, u32[]{:S(2)}) collective-permute-start(bf16[128,1024]{1,0:T(8,128)(2,1)S(1)} %get-tuple-element.40), channel_id=1, source_target_pairs={{512,0},{513,1},{514,2},{515,3},{516,4},{517,5},{518,6},{519,7},{5... | collective-permute-start | bytes 786440 | tf_op jit(solution)/shard_map/ppermute | solution.py:13
  57.7 1.1 %convolution_bitcast_fusion.1 = f32[1,128,1,8,128]{1,4,3,2,0:T(8,128)} fusion(bf16[8,128,384]{1,2,0:T(8,128)(2,1)S(1)} %get-tuple-element.42, bf16[1,384,1,1,128]{4,1,3,2,0:T(8,128)(2,1)S(1)} %get-tuple-element.45), kind=kOutput, calls=%fused_computation.26 | convolution fusion | flops 100663296 | bytes 1409024 | tf_op jit(solution)/shard_map/bkgql,blkd->bqkgd/dot_general | solution.py:62
  59.5 1.0 broadcast_select_fusion
  60.6 1.1 %multiply_reduce_fusion = f32[128,8]{0,1:T(8,128)S(1)} fusion(f32[1,128,1,8,128]{1,4,3,2,0:T(8,128)S(1)} %bitcast.192, f32[1,128,1,8,128]{1,4,3,2,0:T(8,128)} %convolution_bitcast_fusion.1), kind=kLoop, calls=%fused_computation.34 | loop fusion | flops 261120 | bytes 1052672 | tf_op jit(solution)/shard_map/reduce_sum | solution.py:64
  63.9 0.8 copy.150
  64.8 3.4 %all-to-all-start.3 = ((f32[8,2,4224]{2,1,0:T(2,128)}), f32[8,2,4224]{2,1,0:T(2,128)S(1)}, u32[]{:S(2)}, u32[]{:S(2)}) async-start(f32[8,2,4224]{2,1,0:T(2,128)} %copy.150), calls=%async_computation.3 | async-start | bytes 540672 | tf_op jit(solution)/shard_map/all_to_all | solution.py:102
  69.4 12.1 %all-to-all-done.3 = f32[8,2,4224]{2,1,0:T(2,128)S(1)} async-done(((f32[8,2,4224]{2,1,0:T(2,128)}), f32[8,2,4224]{2,1,0:T(2,128)S(1)}, u32[]{:S(2)}, u32[]{:S(2)}) %all-to-all-start.3) | async-done | bytes 270368 | tf_op jit(solution)/shard_map/all_to_all | solution.py:102
  82.8 4.7 %all-to-all-start.4 = ((f32[8,16,256]{2,1,0:T(8,128)}), f32[8,16,256]{2,1,0:T(8,128)S(1)}, u32[]{:S(2)}, u32[]{:S(2)}) async-start(f32[8,16,256]{2,1,0:T(8,128)} %bitcast.66), calls=%async_computation.4 | async-start | bytes 262144 | tf_op jit(solution)/shard_map/all_to_all | solution.py:110
  88.1 7.6 %all-to-all-done.4 = f32[8,16,256]{2,1,0:T(8,128)S(1)} async-done(((f32[8,16,256]{2,1,0:T(8,128)}), f32[8,16,256]{2,1,0:T(8,128)S(1)}, u32[]{:S(2)}, u32[]{:S(2)}) %all-to-all-start.4) | async-done | bytes 131104 | tf_op jit(solution)/shard_map/all_to_all | solution.py:110
  95.7 0.7 broadcast_in_dim.119
  96.3 3.4 %all-to-all-start.5 = ((f32[8,16,256]{2,1,0:T(8,128)}), f32[8,16,256]{2,1,0:T(8,128)S(1)}, u32[]{:S(2)}, u32[]{:S(2)}) async-start(f32[8,16,256]{2,1,0:T(8,128)} %broadcast_in_dim.119), calls=%async_computation.5 | async-start | bytes 262144 | tf_op jit(solution)/shard_map/all_to_all | solution.py:112
  99.7 0.7 select_bitcast_fusion
  100.5 8.3 %all-to-all-done.5 = f32[8,16,256]{2,1,0:T(8,128)S(1)} async-done(((f32[8,16,256]{2,1,0:T(8,128)}), f32[8,16,256]{2,1,0:T(8,128)S(1)}, u32[]{:S(2)}, u32[]{:S(2)}) %all-to-all-start.5) | async-done | bytes 131104 | tf_op jit(solution)/shard_map/all_to_all | solution.py:112
  (73 shorter events, 10.1 us)
Async XLA Ops:
  0.6 42.6 %copy-start.9 = (bf16[1,128,256]{2,1,0:T(8,128)(2,1)S(1)}, bf16[1,128,256]{2,1,0:T(8,128)(2,1)}, u32[]{:S(2)}) copy-start(bf16[1,128,256]{2,1,0:T(8,128)(2,1)} %param.9) | copy-start | bytes 196612
  0.6 42.8 %copy-start.8 = (bf16[1,128,1024]{2,1,0:T(8,128)(2,1)S(1)}, bf16[1,128,1024]{2,1,0:T(8,128)(2,1)}, u32[]{:S(2)}) copy-start(bf16[1,128,1024]{2,1,0:T(8,128)(2,1)} %param.8) | copy-start | bytes 786436
  0.7 43.0 %copy-start.10 = (s32[128]{0:T(128)S(1)}, s32[128]{0:T(128)}, u32[]{:S(2)}) copy-start(s32[128]{0:T(128)} %param.11) | copy-start | bytes 1540
  3.3 15.9 %all-to-all-start = ((bf16[8,16,256]{2,1,0:T(8,128)(2,1)}), bf16[8,16,256]{2,1,0:T(8,128)(2,1)S(1)}, u32[]{:S(2)}, u32[]{:S(2)}) async-start(bf16[8,16,256]{2,1,0:T(8,128)(2,1)} %bitcast.22), calls=%async_computation | async-start | bytes 131072 | tf_op jit(solution)/shard_map/all_to_all | solution.py:84
  19.9 19.1 %all-to-all-start.1 = ((bf16[8,16,256]{2,1,0:T(8,128)(2,1)}), bf16[8,16,256]{2,1,0:T(8,128)(2,1)S(1)}, u32[]{:S(2)}, u32[]{:S(2)}) async-start(bf16[8,16,256]{2,1,0:T(8,128)(2,1)} %broadcast_in_dim.104), calls=%async_computation.1 | async-start | bytes 131072 | tf_op jit(solution)/shard_map/all_to_all | solution.py:86
  39.7 13.8 %all-to-all-start.2 = ((bf16[8,4,16,256]{3,2,1,0:T(8,128)(2,1)}), bf16[8,4,16,256]{3,2,1,0:T(8,128)(2,1)S(1)}, u32[]{:S(2)}, u32[]{:S(2)}) async-start(bf16[8,4,16,256]{3,2,1,0:T(8,128)(2,1)} %broadcast_in_dim.105), calls=%async_computation.2 | async-start | bytes 524288 | tf_op jit(solution)/shard_map/all_to_all | solution.py:91
  43.6 11.0 %copy-start.1 = (bf16[1,128,1024]{1,2,0:T(8,128)(2,1)}, bf16[1,128,1024]{1,2,0:T(8,128)(2,1)S(1)}, u32[]{:S(2)}) copy-start(bf16[1,128,1024]{1,2,0:T(8,128)(2,1)S(1)} %copy.169) | copy-start | bytes 786436
  54.3 1.6 %copy-start.4 = (bf16[1,384,1,1,128]{4,1,3,2,0:T(8,128)(2,1)}, bf16[1,384,1,1,128]{4,1,3,2,0:T(8,128)(2,1)S(1)}, u32[]{:S(2)}) copy-start(bf16[1,384,1,1,128]{4,1,3,2,0:T(8,128)(2,1)S(1)} %get-tuple-element.44) | copy-start | bytes 294916
  54.9 1.0 copy-start.3
  55.9 3.0 %copy-start.6 = (bf16[128,1024]{1,0:T(8,128)(2,1)}, bf16[128,1024]{1,0:T(8,128)(2,1)S(1)}, u32[]{:S(2)}) copy-start(bf16[128,1024]{1,0:T(8,128)(2,1)S(1)} %get-tuple-element.40) | copy-start | bytes 786436
  55.9 3.6 %collective-permute-start = (bf16[128,1024]{1,0:T(8,128)(2,1)S(1)}, bf16[128,1024]{1,0:T(8,128)(2,1)}, u32[]{:S(2)}, u32[]{:S(2)}) collective-permute-start(bf16[128,1024]{1,0:T(8,128)(2,1)S(1)} %get-tuple-element.40), channel_id=1, source_target_pairs={{512,0},{513,1},{514,2},{515,3},{516,4},{517,5},{518,6},{519,7},{5... | collective-permute-start | bytes 786440 | tf_op jit(solution)/shard_map/ppermute | solution.py:13
  61.7 1.0 copy-start.2
  63.4 4.8 %copy-start = (s32[4]{0:T(128)S(1)}, s32[4]{0:T(128)}, u32[]{:S(2)}) copy-start(s32[4]{0:T(128)} %param.12) | copy-start | bytes 52
  63.9 23.6 %copy-start.5 = (bf16[1,384,1,1,128]{4,1,3,2,0:T(8,128)(2,1)S(1)}, bf16[1,384,1,1,128]{4,1,3,2,0:T(8,128)(2,1)}, u32[]{:S(2)}) copy-start(bf16[1,384,1,1,128]{4,1,3,2,0:T(8,128)(2,1)} %copy-done.4) | copy-start | bytes 294916
  64.8 16.8 %all-to-all-start.3 = ((f32[8,2,4224]{2,1,0:T(2,128)}), f32[8,2,4224]{2,1,0:T(2,128)S(1)}, u32[]{:S(2)}, u32[]{:S(2)}) async-start(f32[8,2,4224]{2,1,0:T(2,128)} %copy.150), calls=%async_computation.3 | async-start | bytes 540672 | tf_op jit(solution)/shard_map/all_to_all | solution.py:102
  82.8 12.9 %all-to-all-start.4 = ((f32[8,16,256]{2,1,0:T(8,128)}), f32[8,16,256]{2,1,0:T(8,128)S(1)}, u32[]{:S(2)}, u32[]{:S(2)}) async-start(f32[8,16,256]{2,1,0:T(8,128)} %bitcast.66), calls=%async_computation.4 | async-start | bytes 262144 | tf_op jit(solution)/shard_map/all_to_all | solution.py:110
  87.5 12.2 %copy-start.7 = (bf16[128,1024]{1,0:T(8,128)(2,1)S(1)}, bf16[128,1024]{1,0:T(8,128)(2,1)}, u32[]{:S(2)}) copy-start(bf16[128,1024]{1,0:T(8,128)(2,1)} %copy-done.6) | copy-start | bytes 786436
  96.3 12.4 %all-to-all-start.5 = ((f32[8,16,256]{2,1,0:T(8,128)}), f32[8,16,256]{2,1,0:T(8,128)S(1)}, u32[]{:S(2)}, u32[]{:S(2)}) async-start(f32[8,16,256]{2,1,0:T(8,128)} %broadcast_in_dim.119), calls=%async_computation.5 | async-start | bytes 262144 | tf_op jit(solution)/shard_map/all_to_all | solution.py:112

commit v6 on v5

--- a/solution.py
+++ b/solution.py
@@ -134,22 +134,40 @@
     npick = anchor_pick.shape[1]
     kk, vv = gather_keys(keyvals, anchor_kv, anchor_pick)
 
-    probs = forward(query_rows, kk, sentences, anchor_pick, anchor_blocks, blocks)
+    def probs_of():
+        return forward(query_rows, kk, sentences, anchor_pick, anchor_blocks, blocks)
 
-    sent_back = lax.cond(
-        section_one,
-        lambda cot: backward(query_rows, kk, vv, probs, cot)[0].astype(jnp.bfloat16),
-        lambda cot: cot,
-        out_grad,
+    def relayed(probs, cot):
+        dq, band, far = backward(query_rows, kk, vv, probs, cot)
+        return dq.astype(jnp.bfloat16), band, far
+
+    def second_layer(cot):
+        probs = probs_of()
+        return (probs,) + relayed(probs, cot)
+
+    def first_layer_probs(cot):
+        return (
+            probs_of(),
+            cot,
+            jnp.zeros((rows, feat), jnp.float32),
+            jnp.zeros((per_dev * npick, BLK, feat), jnp.float32),
+        )
+
+    probs, sent_back, band_first, far_first = lax.cond(
+        section_one, second_layer, first_layer_probs, out_grad
     )
     arrived = from_behind(sent_back, "section", -1)
-    cot = jnp.where(section_one, out_grad, arrived)
-    dq, band_grad, far = backward(query_rows, kk, vv, probs, cot)
+    dq_out, band_grad, far = lax.cond(
+        section_one,
+        lambda cot: (sent_back, band_first, far_first),
+        lambda cot: relayed(probs, cot),
+        arrived,
+    )
     total = gather_grads(far, anchor_pick.reshape(-1), nanch, rows_per_slot)
     owner = (anchor_blocks[rank] == blocks).astype(jnp.float32)
     owned = owner[:, None, None] * total[None]
     kv_grad = (band_grad + owned.reshape(band_grad.shape)).astype(jnp.bfloat16)
-    input_grad = jnp.where(section_one, sent_back, dq.astype(jnp.bfloat16))
+    input_grad = dq_out
     return (input_grad[None], kv_grad[None])
 
 

time: 110 us -> 103 us (0.936)
  blocking collectives: 0 us -> 57.8 us
  waiting for transfers between devices: 51.4 us -> 19.1 us
  starting transfers between devices: 35.9 us -> 8.21 us
  other arithmetic: 7.95 us -> 3.79 us
  local copies, waits for them, and re-layouts: 9.47 us -> 8.28 us
    all_to_all x0 -> x4, blocking collectives: none -> 57.8 us  [the longest x1 17.5 us: spread_anchors(): lax.all_to_all(jnp.broadcast_to(row[None], (nx,) + row.shape), 'cx', 0, 0...]
    all_to_all x4 -> x0, waiting for transfers between devices: 32.9 us -> none  [the longest x1 12.1 us: gather_grads(): got = lax.all_to_all(load, 'cy', 0, 0, tiled=True)]
    all_to_all x4 -> x0, starting transfers between devices: 27.8 us -> none  [the longest x1 12.1 us: spread_anchors(): lax.all_to_all(jnp.broadcast_to(row[None], (nx,) + row.shape), 'cx', 0, 0...]
    another operation x3 -> x5, local copies, waits for them, and re-layouts: 0.9 us -> 2.61 us
    ppermute x1, waiting for transfers between devices: 0.6 us -> 2.13 us  [from_behind(): return lax.ppermute(x, axis, pairs)]
    reduce_sum x1 -> x0, other arithmetic: 1.1 us -> none  [backward(): jnp.sum(c_blocks.astype(jnp.float32) * outp, axis=-1).transpose(0, 2, 3, 1)]
  transfers between devices with their start and end apart: 7 -> 3, of which waited for: 7 -> 3; matrix products, arithmetic and copies ran while one was open for 6% -> 2% of each run, Pallas kernels for 0% -> 0%
where the time goes in v6:
time: 103 us; the launch traced here: 102 us
  blocking collectives  57.8 us (56%)
  waiting for transfers between devices  19.1 us (19%)
  local copies, waits for them, and re-layouts  8.28 us (8%)
  starting transfers between devices  8.21 us (8%)
  other arithmetic  3.79 us (4%)
  matrix products  3.06 us (3%)
  between operations  1.56 us (2%)
    all_to_all x1, blocking collectives, spread_anchors(): lax.all_to_all(jnp.broadcast_to(row[None], (nx,) + row.shape), 'cx', 0, 0...  17.5 us
    all_to_all x1, blocking collectives, spread_anchors(): got = lax.all_to_all(part, 'cy', 0, 0, tiled=True)  15.7 us
    all_to_all x1, blocking collectives, gather_grads(): got = lax.all_to_all(load, 'cy', 0, 0, tiled=True)  13.1 us
    all_to_all x1, blocking collectives, gather_grads(): lax.all_to_all(jnp.repeat(rowsum, rows_per_slot, axis=0), 'cx', 0, 0, til...  11.5 us
    all_to_all x1, waiting for transfers between devices, spread_anchors(): lax.all_to_all(jnp.broadcast_to(slots[None], (ny,) + slots.shape), 'cy',...  9.25 us
    all_to_all x1, waiting for transfers between devices, gather_grads(): lax.all_to_all(jnp.broadcast_to(total[None], (ny,) + total.shape), 'cy',...  7.74 us
    all_to_all x1, starting transfers between devices, spread_anchors(): lax.all_to_all(jnp.broadcast_to(slots[None], (ny,) + slots.shape), 'cy',...  3.56 us
    all_to_all x1, starting transfers between devices, gather_grads(): lax.all_to_all(jnp.broadcast_to(total[None], (ny,) + total.shape), 'cy',...  3.37 us
  transfers between devices with their start and end apart: 3, of which 3 were waited for; matrix products, arithmetic and copies ran while one was open for 2% of the time, Pallas kernels for 0%

profile of v6, /device:TPU:2, one launch (start us, length us, event | category | flops | bytes accessed | tf_op | source)
XLA Modules:
  0.0 102.0 jit_solution(4550673940248178950)
XLA Ops:
  0.6 1.3 %compare_reduce_fusion = pred[]{:T(512)} fusion(s32[4]{0:T(128)} %param.14, s32[]{:T(128)} %add.22), kind=kLoop, calls=%fused_computation.90 | loop fusion | flops 7 | bytes 21 | tf_op jit(solution)/shard_map/reduce_or | solution.py:130
  1.9 0.7 broadcast_select_fusion
  2.6 15.7 %all_to_all.30 = bf16[8,16,256]{2,1,0:T(8,128)(2,1)S(1)} all-to-all(bf16[8,16,256]{2,1,0:T(8,128)(2,1)S(1)} %bitcast.270), channel_id=1, replica_groups=mesh['section'=2,'cx'=8,'cy'=8,'head'=8] {'cy'}, dimensions={0} | all-to-all | bytes 131072 | tf_op jit(solution)/shard_map/all_to_all | solution.py:84
  18.4 17.5 %all_to_all.31 = bf16[8,16,256]{2,1,0:T(8,128)(2,1)S(1)} all-to-all(bf16[8,16,256]{2,1,0:T(8,128)(2,1)S(1)} %broadcast_in_dim.138), channel_id=1, replica_groups=mesh['section'=2,'cx'=8,'cy'=8,'head'=8] {'cx'}, dimensions={0} | all-to-all | bytes 131072 | tf_op jit(solution)/shard_map/all_to_all | solution.py:86
  35.9 0.7 broadcast_in_dim.139
  36.6 3.6 %all-to-all-start.2 = ((bf16[8,4,16,256]{3,2,1,0:T(8,128)(2,1)}), bf16[8,4,16,256]{3,2,1,0:T(8,128)(2,1)S(1)}, u32[]{:S(2)}, u32[]{:S(2)}) async-start(bf16[8,4,16,256]{3,2,1,0:T(8,128)(2,1)} %broadcast_in_dim.139), calls=%async_computation.2 | async-start | bytes 524288 | tf_op jit(solution)/shard_map/all_to_all | solution.py:91
  40.2 1.0 copy.180
  41.3 9.3 %all-to-all-done.2 = bf16[8,4,16,256]{3,2,1,0:T(8,128)(2,1)S(1)} async-done(((bf16[8,4,16,256]{3,2,1,0:T(8,128)(2,1)}), bf16[8,4,16,256]{3,2,1,0:T(8,128)(2,1)S(1)}, u32[]{:S(2)}, u32[]{:S(2)}) %all-to-all-start.2) | async-done | bytes 262176 | tf_op jit(solution)/shard_map/all_to_all | solution.py:91
  51.4 3.6 %conditional.2 = (f32[1,1,8,128,384]{3,4,2,1,0:T(8,128)S(1)}, bf16[128,1024]{0,1:T(8,128)(2,1)S(1)}, f32[128,256]{0,1:T(8,128)}, f32[2,128,256]{1,0,2:T(2,128)}) conditional(s32[]{:T(128)} %convert_element_type.103, (s32[128]{0:T(128)S(1)}, s32[1,2]{1,0:T(1,128)S(1)}, s32[4]{0:T(128)S(1)}, s32[]{:T(128)}, bf16[1,384,1,128]{3,1,2,0:T(8,128)(2,1)S(1)}, ...), branch_computations={%region_3.6_spmd, %region_6.0_spmd} | conditional | flops 609597440 | bytes 31229848 | solution.py:156
  51.7 0.6 gather_fusion
  53.5 0.8 broadcast.227
  54.3 0.7 broadcast.226
  55.0 1.3 %collective-permute-start = (bf16[128,1024]{0,1:T(8,128)(2,1)S(1)}, bf16[128,1024]{0,1:T(8,128)(2,1)S(1)}, u32[]{:S(2)}, u32[]{:S(2)}) collective-permute-start(bf16[128,1024]{0,1:T(8,128)(2,1)S(1)} %get-tuple-element.83), channel_id=1, source_target_pairs={{512,0},{513,1},{514,2},{515,3},{516,4},{517,5},{518,6},{519,7},{5... | collective-permute-start | bytes 786440 | tf_op jit(solution)/shard_map/ppermute | solution.py:13
  56.3 2.1 %collective-permute-done = bf16[128,1024]{0,1:T(8,128)(2,1)S(1)} collective-permute-done((bf16[128,1024]{0,1:T(8,128)(2,1)S(1)}, bf16[128,1024]{0,1:T(8,128)(2,1)S(1)}, u32[]{:S(2)}, u32[]{:S(2)}) %collective-permute-start) | collective-permute-done | bytes 262176 | tf_op jit(solution)/shard_map/ppermute | solution.py:13
  58.4 4.5 %conditional.3 = (bf16[1,128,1024]{2,1,0:T(8,128)(2,1)S(1)}, f32[128,256]{1,0:T(8,128)S(1)}, f32[2,8,4096]{2,0,1:T(2,128)S(1)}) conditional(s32[]{:T(128)} %convert_element_type.103, (bf16[1,384,1,128]{3,1,2,0:T(8,128)(2,1)S(1)}, bf16[128,1024]{0,1:T(8,128)(2,1)S(1)}, f32[1,1,8,128,384]{3,4,2,1,0:T(8,128)S(1)}, ...), branch_computations={%region_10.12_spmd, %region_12.13_spmd} | conditional | flops 506084352 | bytes 13148184 | solution.py:160
  59.1 0.8 copy.192
  59.9 1.3 %fusion.7 = f32[1,384,1,1,128]{1,4,3,2,0:T(8,128)S(1)} fusion(bf16[8,128,384]{1,2,0:T(8,128)(2,1)S(1)} %fusion.2, bf16[128,8,128]{0,2,1:T(8,128)(2,1)} %bitcast.260), kind=kOutput, calls=%fused_computation.15 | convolution fusion | flops 100712448 | bytes 1245184 | tf_op jit(solution)/shard_map/cond/branch_0_fun/bkgql,bqkgd->blkd/dot_general | solution.py:69
  63.1 13.1 %all_to_all.32 = f32[8,2,4224]{2,1,0:T(2,128)S(1)} all-to-all(f32[8,2,4224]{2,1,0:T(2,128)S(1)} %maximum_bitcast_fusion), channel_id=1, replica_groups=mesh['section'=2,'cx'=8,'cy'=8,'head'=8] {'cy'}, dimensions={0} | all-to-all | bytes 540672 | tf_op jit(solution)/shard_map/all_to_all | solution.py:102
  76.8 11.5 %all_to_all.33 = f32[8,16,256]{2,1,0:T(8,128)S(1)} all-to-all(f32[8,16,256]{2,1,0:T(8,128)S(1)} %bitcast.266), channel_id=1, replica_groups=mesh['section'=2,'cx'=8,'cy'=8,'head'=8] {'cx'}, dimensions={0} | all-to-all | bytes 262144 | tf_op jit(solution)/shard_map/all_to_all | solution.py:110
  88.3 0.6 broadcast_in_dim.146
  88.9 3.4 %all-to-all-start.5 = ((f32[8,16,256]{2,1,0:T(8,128)}), f32[8,16,256]{2,1,0:T(8,128)S(1)}, u32[]{:S(2)}, u32[]{:S(2)}) async-start(f32[8,16,256]{2,1,0:T(8,128)} %broadcast_in_dim.146), calls=%async_computation.5 | async-start | bytes 262144 | tf_op jit(solution)/shard_map/all_to_all | solution.py:112
  92.3 0.6 dynamic_slice.3
  93.5 7.7 %all-to-all-done.5 = f32[8,16,256]{2,1,0:T(8,128)S(1)} async-done(((f32[8,16,256]{2,1,0:T(8,128)}), f32[8,16,256]{2,1,0:T(8,128)S(1)}, u32[]{:S(2)}, u32[]{:S(2)}) %all-to-all-start.5) | async-done | bytes 131104 | tf_op jit(solution)/shard_map/all_to_all | solution.py:112
  101.3 0.6 fusion.40
  (59 shorter events, 5.4 us)
Async XLA Ops:
  0.6 40.6 %copy-start.7 = (s32[1,2]{1,0:T(1,128)S(1)}, s32[1,2]{1,0:T(1,128)}, u32[]{:S(2)}) copy-start(s32[1,2]{1,0:T(1,128)} %param.15) | copy-start | bytes 28
  36.6 14.7 %copy-start = (s32[4]{0:T(128)S(1)}, s32[4]{0:T(128)}, u32[]{:S(2)}) copy-start(s32[4]{0:T(128)} %param.14) | copy-start | bytes 52
  36.6 14.7 %copy-start.3 = (bf16[1,128,1024]{2,1,0:T(8,128)(2,1)S(1)}, bf16[1,128,1024]{2,1,0:T(8,128)(2,1)}, u32[]{:S(2)}) copy-start(bf16[1,128,1024]{2,1,0:T(8,128)(2,1)} %param.10) | copy-start | bytes 786436
  36.6 14.7 %copy-start.4 = (bf16[128,1024]{1,0:T(8,128)(2,1)S(1)}, bf16[128,1024]{1,0:T(8,128)(2,1)}, u32[]{:S(2)}) copy-start(bf16[128,1024]{1,0:T(8,128)(2,1)} %param.12) | copy-start | bytes 786436
  36.6 14.8 %copy-start.6 = (s32[128]{0:T(128)S(1)}, s32[128]{0:T(128)}, u32[]{:S(2)}) copy-start(s32[128]{0:T(128)} %param.13) | copy-start | bytes 1540
  36.6 14.0 %all-to-all-start.2 = ((bf16[8,4,16,256]{3,2,1,0:T(8,128)(2,1)}), bf16[8,4,16,256]{3,2,1,0:T(8,128)(2,1)S(1)}, u32[]{:S(2)}, u32[]{:S(2)}) async-start(bf16[8,4,16,256]{3,2,1,0:T(8,128)(2,1)} %broadcast_in_dim.139), calls=%async_computation.2 | async-start | bytes 524288 | tf_op jit(solution)/shard_map/all_to_all | solution.py:91
  55.0 3.4 %collective-permute-start = (bf16[128,1024]{0,1:T(8,128)(2,1)S(1)}, bf16[128,1024]{0,1:T(8,128)(2,1)S(1)}, u32[]{:S(2)}, u32[]{:S(2)}) collective-permute-start(bf16[128,1024]{0,1:T(8,128)(2,1)S(1)} %get-tuple-element.83), channel_id=1, source_target_pairs={{512,0},{513,1},{514,2},{515,3},{516,4},{517,5},{518,6},{519,7},{5... | collective-permute-start | bytes 786440 | tf_op jit(solution)/shard_map/ppermute | solution.py:13
  62.9 25.4 %copy-start.5 = (bf16[1,128,1024]{2,1,0:T(8,128)(2,1)}, bf16[1,128,1024]{2,1,0:T(8,128)(2,1)S(1)}, u32[]{:S(2)}) copy-start(bf16[1,128,1024]{2,1,0:T(8,128)(2,1)S(1)} %get-tuple-element.240) | copy-start | bytes 786436
  88.9 12.4 %all-to-all-start.5 = ((f32[8,16,256]{2,1,0:T(8,128)}), f32[8,16,256]{2,1,0:T(8,128)S(1)}, u32[]{:S(2)}, u32[]{:S(2)}) async-start(f32[8,16,256]{2,1,0:T(8,128)} %broadcast_in_dim.146), calls=%async_computation.5 | async-start | bytes 262144 | tf_op jit(solution)/shard_map/all_to_all | solution.py:112

commit v7 on v6

--- a/solution.py
+++ b/solution.py
@@ -126,8 +126,7 @@
     section_one = lax.axis_index("section") == 1
     blocks = ctx * per_dev + jnp.arange(per_dev, dtype=jnp.int32)
     kv_blocks = keyvals.reshape(per_dev, BLK, feat)
-    hit = anchor_blocks[None, :] == blocks[:, None]
-    holder = jnp.any(hit, axis=1)[:, None, None]
+    holder = (anchor_blocks[rank] == blocks)[:, None, None]
     mine = jnp.where(holder, kv_blocks, jnp.zeros_like(kv_blocks)).sum(axis=0, dtype=jnp.float32)
     mine = mine.astype(jnp.bfloat16)
     anchor_kv = spread_anchors(mine, rows_per_slot)

time: 103 us -> 103 us (level)
  other arithmetic: 3.79 us -> 1.85 us
  waiting for transfers between devices: 19.1 us -> 20.4 us
    reduce_or x1 -> x0, other arithmetic: 1.3 us -> none  [body(): holder = jnp.any(hit, axis=1)[:, None, None]]
    all_to_all x1, waiting for transfers between devices: 7.74 us -> 8.99 us  [gather_grads(): lax.all_to_all(jnp.broadcast_to(total[None], (ny,) + total.shape), 'cy',...]
  transfers between devices with their start and end apart: 3 -> 3, of which waited for: 3 -> 3; matrix products, arithmetic and copies ran while one was open for 2% -> 1% of each run, Pallas kernels for 0% -> 0%
where the time goes in v7:
time: 103 us; the launch traced here: 102 us
  blocking collectives  57.8 us (56%)
  waiting for transfers between devices  20.4 us (20%)
  local copies, waits for them, and re-layouts  8.94 us (9%)
  starting transfers between devices  8.21 us (8%)
  matrix products  3.06 us (3%)
  other arithmetic  1.85 us (2%)
  between operations  1.56 us (2%)
    all_to_all x1, blocking collectives, spread_anchors(): lax.all_to_all(jnp.broadcast_to(row[None], (nx,) + row.shape), 'cx', 0, 0...  17.5 us
    all_to_all x1, blocking collectives, spread_anchors(): got = lax.all_to_all(part, 'cy', 0, 0, tiled=True)  15.7 us
    all_to_all x1, blocking collectives, gather_grads(): got = lax.all_to_all(load, 'cy', 0, 0, tiled=True)  13.1 us
    all_to_all x1, blocking collectives, gather_grads(): lax.all_to_all(jnp.repeat(rowsum, rows_per_slot, axis=0), 'cx', 0, 0, til...  11.5 us
    all_to_all x1, waiting for transfers between devices, spread_anchors(): lax.all_to_all(jnp.broadcast_to(slots[None], (ny,) + slots.shape), 'cy',...  9.25 us
    all_to_all x1, waiting for transfers between devices, gather_grads(): lax.all_to_all(jnp.broadcast_to(total[None], (ny,) + total.shape), 'cy',...  8.99 us
    all_to_all x1, starting transfers between devices, spread_anchors(): lax.all_to_all(jnp.broadcast_to(slots[None], (ny,) + slots.shape), 'cy',...  3.56 us
    all_to_all x1, starting transfers between devices, gather_grads(): lax.all_to_all(jnp.broadcast_to(total[None], (ny,) + total.shape), 'cy',...  3.37 us
  transfers between devices with their start and end apart: 3, of which 3 were waited for; matrix products, arithmetic and copies ran while one was open for 1% of the time, Pallas kernels for 0%

profile of v7, /device:TPU:2, one launch (start us, length us, event | category | flops | bytes accessed | tf_op | source)
XLA Modules:
  0.0 101.9 jit_solution(14949408719003407723)
XLA Ops:
  0.7 1.2 %dynamic_slice.4 = s32[1]{0:T(128)} dynamic-slice(s32[4]{0:T(128)} %param.14, s32[]{:T(128)S(6)} %select_n.34), dynamic_slice_sizes={1} | dynamic-slice | bytes 12 | tf_op jit(solution)/shard_map/dynamic_slice | solution.py:129
  2.6 15.7 %all_to_all.30 = bf16[8,16,256]{2,1,0:T(8,128)(2,1)S(1)} all-to-all(bf16[8,16,256]{2,1,0:T(8,128)(2,1)S(1)} %bitcast.270), channel_id=1, replica_groups=mesh['section'=2,'cx'=8,'cy'=8,'head'=8] {'cy'}, dimensions={0} | all-to-all | bytes 131072 | tf_op jit(solution)/shard_map/all_to_all | solution.py:84
  18.3 17.5 %all_to_all.31 = bf16[8,16,256]{2,1,0:T(8,128)(2,1)S(1)} all-to-all(bf16[8,16,256]{2,1,0:T(8,128)(2,1)S(1)} %broadcast_in_dim.140), channel_id=1, replica_groups=mesh['section'=2,'cx'=8,'cy'=8,'head'=8] {'cx'}, dimensions={0} | all-to-all | bytes 131072 | tf_op jit(solution)/shard_map/all_to_all | solution.py:86
  35.8 0.7 broadcast_in_dim.141
  36.6 3.6 %all-to-all-start.2 = ((bf16[8,4,16,256]{3,2,1,0:T(8,128)(2,1)}), bf16[8,4,16,256]{3,2,1,0:T(8,128)(2,1)S(1)}, u32[]{:S(2)}, u32[]{:S(2)}) async-start(bf16[8,4,16,256]{3,2,1,0:T(8,128)(2,1)} %broadcast_in_dim.141), calls=%async_computation.2 | async-start | bytes 524288 | tf_op jit(solution)/shard_map/all_to_all | solution.py:91
  40.1 1.0 copy.180
  41.3 9.3 %all-to-all-done.2 = bf16[8,4,16,256]{3,2,1,0:T(8,128)(2,1)S(1)} async-done(((bf16[8,4,16,256]{3,2,1,0:T(8,128)(2,1)}), bf16[8,4,16,256]{3,2,1,0:T(8,128)(2,1)S(1)}, u32[]{:S(2)}, u32[]{:S(2)}) %all-to-all-start.2) | async-done | bytes 262176 | tf_op jit(solution)/shard_map/all_to_all | solution.py:91
  50.7 0.6 gather_fusion.2
  51.3 3.6 %conditional.2 = (f32[1,1,8,128,384]{3,4,2,1,0:T(8,128)S(1)}, bf16[128,1024]{0,1:T(8,128)(2,1)S(1)}, f32[128,256]{0,1:T(8,128)}, f32[2,128,256]{1,0,2:T(2,128)}) conditional(s32[]{:T(128)} %convert_element_type.103, (s32[128]{0:T(128)S(1)}, s32[1,2]{1,0:T(1,128)S(1)}, s32[4]{0:T(128)S(1)}, s32[]{:T(128)}, bf16[1,384,1,128]{3,1,2,0:T(8,128)(2,1)S(1)}, ...), branch_computations={%region_2.5_spmd, %region_5.0_spmd} | conditional | flops 609597440 | bytes 31229848 | solution.py:155
  51.6 0.6 gather_fusion
  53.5 0.8 broadcast.223
  54.3 0.7 broadcast.222
  54.9 1.3 %collective-permute-start = (bf16[128,1024]{0,1:T(8,128)(2,1)S(1)}, bf16[128,1024]{0,1:T(8,128)(2,1)S(1)}, u32[]{:S(2)}, u32[]{:S(2)}) collective-permute-start(bf16[128,1024]{0,1:T(8,128)(2,1)S(1)} %get-tuple-element.83), channel_id=1, source_target_pairs={{512,0},{513,1},{514,2},{515,3},{516,4},{517,5},{518,6},{519,7},{5... | collective-permute-start | bytes 786440 | tf_op jit(solution)/shard_map/ppermute | solution.py:13
  56.2 2.1 %collective-permute-done = bf16[128,1024]{0,1:T(8,128)(2,1)S(1)} collective-permute-done((bf16[128,1024]{0,1:T(8,128)(2,1)S(1)}, bf16[128,1024]{0,1:T(8,128)(2,1)S(1)}, u32[]{:S(2)}, u32[]{:S(2)}) %collective-permute-start) | collective-permute-done | bytes 262176 | tf_op jit(solution)/shard_map/ppermute | solution.py:13
  58.4 4.5 %conditional.3 = (bf16[1,128,1024]{2,1,0:T(8,128)(2,1)S(1)}, f32[128,256]{1,0:T(8,128)S(1)}, f32[2,8,4096]{2,0,1:T(2,128)S(1)}) conditional(s32[]{:T(128)} %convert_element_type.103, (bf16[1,384,1,128]{3,1,2,0:T(8,128)(2,1)S(1)}, bf16[128,1024]{0,1:T(8,128)(2,1)S(1)}, f32[1,1,8,128,384]{3,4,2,1,0:T(8,128)S(1)}, ...), branch_computations={%region_9.11_spmd, %region_11.12_spmd} | conditional | flops 506084352 | bytes 13148184 | solution.py:159
  59.1 0.8 copy.192
  59.9 1.3 %fusion.7 = f32[1,384,1,1,128]{1,4,3,2,0:T(8,128)S(1)} fusion(bf16[8,128,384]{1,2,0:T(8,128)(2,1)S(1)} %fusion.2, bf16[128,8,128]{0,2,1:T(8,128)(2,1)} %bitcast.260), kind=kOutput, calls=%fused_computation.15 | convolution fusion | flops 100712448 | bytes 1245184 | tf_op jit(solution)/shard_map/cond/branch_0_fun/bkgql,bqkgd->blkd/dot_general | solution.py:69
  61.2 0.4 convolution_bitcast_fusion.1
  63.0 13.1 %all_to_all.32 = f32[8,2,4224]{2,1,0:T(2,128)S(1)} all-to-all(f32[8,2,4224]{2,1,0:T(2,128)S(1)} %maximum_bitcast_fusion), channel_id=1, replica_groups=mesh['section'=2,'cx'=8,'cy'=8,'head'=8] {'cy'}, dimensions={0} | all-to-all | bytes 540672 | tf_op jit(solution)/shard_map/all_to_all | solution.py:102
  76.7 11.5 %all_to_all.33 = f32[8,16,256]{2,1,0:T(8,128)S(1)} all-to-all(f32[8,16,256]{2,1,0:T(8,128)S(1)} %bitcast.266), channel_id=1, replica_groups=mesh['section'=2,'cx'=8,'cy'=8,'head'=8] {'cx'}, dimensions={0} | all-to-all | bytes 262144 | tf_op jit(solution)/shard_map/all_to_all | solution.py:110
  88.2 0.6 broadcast_in_dim.148
  88.9 3.4 %all-to-all-start.5 = ((f32[8,16,256]{2,1,0:T(8,128)}), f32[8,16,256]{2,1,0:T(8,128)S(1)}, u32[]{:S(2)}, u32[]{:S(2)}) async-start(f32[8,16,256]{2,1,0:T(8,128)} %broadcast_in_dim.148), calls=%async_computation.5 | async-start | bytes 262144 | tf_op jit(solution)/shard_map/all_to_all | solution.py:112
  92.3 9.0 %all-to-all-done.5 = f32[8,16,256]{2,1,0:T(8,128)S(1)} async-done(((f32[8,16,256]{2,1,0:T(8,128)}), f32[8,16,256]{2,1,0:T(8,128)S(1)}, u32[]{:S(2)}, u32[]{:S(2)}) %all-to-all-start.5) | async-done | bytes 131104 | tf_op jit(solution)/shard_map/all_to_all | solution.py:112
  101.3 0.6 fusion.40
  (58 shorter events, 4.5 us)
Async XLA Ops:
  0.6 40.6 %copy-start.7 = (s32[1,2]{1,0:T(1,128)S(1)}, s32[1,2]{1,0:T(1,128)}, u32[]{:S(2)}) copy-start(s32[1,2]{1,0:T(1,128)} %param.15) | copy-start | bytes 28
  36.6 14.7 %copy-start = (s32[4]{0:T(128)S(1)}, s32[4]{0:T(128)}, u32[]{:S(2)}) copy-start(s32[4]{0:T(128)} %param.14) | copy-start | bytes 52
  36.6 14.7 %copy-start.3 = (bf16[1,128,1024]{2,1,0:T(8,128)(2,1)S(1)}, bf16[1,128,1024]{2,1,0:T(8,128)(2,1)}, u32[]{:S(2)}) copy-start(bf16[1,128,1024]{2,1,0:T(8,128)(2,1)} %param.10) | copy-start | bytes 786436
  36.6 14.7 %copy-start.4 = (bf16[128,1024]{1,0:T(8,128)(2,1)S(1)}, bf16[128,1024]{1,0:T(8,128)(2,1)}, u32[]{:S(2)}) copy-start(bf16[128,1024]{1,0:T(8,128)(2,1)} %param.12) | copy-start | bytes 786436
  36.6 14.8 %copy-start.6 = (s32[128]{0:T(128)S(1)}, s32[128]{0:T(128)}, u32[]{:S(2)}) copy-start(s32[128]{0:T(128)} %param.13) | copy-start | bytes 1540
  36.6 14.0 %all-to-all-start.2 = ((bf16[8,4,16,256]{3,2,1,0:T(8,128)(2,1)}), bf16[8,4,16,256]{3,2,1,0:T(8,128)(2,1)S(1)}, u32[]{:S(2)}, u32[]{:S(2)}) async-start(bf16[8,4,16,256]{3,2,1,0:T(8,128)(2,1)} %broadcast_in_dim.141), calls=%async_computation.2 | async-start | bytes 524288 | tf_op jit(solution)/shard_map/all_to_all | solution.py:91
  54.9 3.4 %collective-permute-start = (bf16[128,1024]{0,1:T(8,128)(2,1)S(1)}, bf16[128,1024]{0,1:T(8,128)(2,1)S(1)}, u32[]{:S(2)}, u32[]{:S(2)}) collective-permute-start(bf16[128,1024]{0,1:T(8,128)(2,1)S(1)} %get-tuple-element.83), channel_id=1, source_target_pairs={{512,0},{513,1},{514,2},{515,3},{516,4},{517,5},{518,6},{519,7},{5... | collective-permute-start | bytes 786440 | tf_op jit(solution)/shard_map/ppermute | solution.py:13
  62.8 25.4 %copy-start.5 = (bf16[1,128,1024]{2,1,0:T(8,128)(2,1)}, bf16[1,128,1024]{2,1,0:T(8,128)(2,1)S(1)}, u32[]{:S(2)}) copy-start(bf16[1,128,1024]{2,1,0:T(8,128)(2,1)S(1)} %get-tuple-element.240) | copy-start | bytes 786436
  88.9 12.4 %all-to-all-start.5 = ((f32[8,16,256]{2,1,0:T(8,128)}), f32[8,16,256]{2,1,0:T(8,128)S(1)}, u32[]{:S(2)}, u32[]{:S(2)}) async-start(f32[8,16,256]{2,1,0:T(8,128)} %broadcast_in_dim.148), calls=%async_computation.5 | async-start | bytes 262144 | tf_op jit(solution)/shard_map/all_to_all | solution.py:112

commit v8 on v7

--- a/solution.py
+++ b/solution.py
@@ -29,22 +29,22 @@
 
 def forward(query_rows, kk, sentences, picks, anchor_blocks, blocks):
     rows, width = query_rows.shape
-    kvh = kk.shape[2]
-    group_size = width // (kvh * HEAD_SIZE)
-    per_dev = rows // BLK
+    assert rows == BLK and kk.shape[0] == 1 and kk.shape[2] == 1
+    group_size = width // HEAD_SIZE
     npick = picks.shape[1]
     scale = HEAD_SIZE ** (-0.5)
-    q_blocks = query_rows.reshape(per_dev, BLK, kvh, group_size, HEAD_SIZE)
-    score = (
-        jnp.einsum("bqkgd,blkd->bkgql", q_blocks, kk, preferred_element_type=jnp.float32) * scale
-    )
-    sent = sentences.reshape(per_dev, BLK)
+    q2 = query_rows.reshape(rows * group_size, HEAD_SIZE)
+    keys = kk.reshape(-1, HEAD_SIZE)
+    score = lax.dot_general(
+        q2, keys, (((1,), (1,)), ((), ())), preferred_element_type=jnp.float32
+    ) * scale
+    sent = sentences.reshape(BLK)
     idx = jnp.arange(BLK, dtype=jnp.int32)
-    band = (idx[None, :, None] >= idx[None, None, :]) & (sent[:, :, None] == sent[:, None, :])
-    valid = jnp.repeat(anchor_blocks[picks] < blocks[:, None], BLK, axis=1)
-    far_mask = jnp.broadcast_to(valid[:, None, :], (per_dev, BLK, npick * BLK))
-    mask = jnp.concatenate([band, far_mask], axis=2)[:, None, None]
-    score = jnp.where(mask, score, jnp.float32(-1e30))
+    band = (idx[:, None] >= idx[None, :]) & (sent[:, None] == sent[None, :])
+    valid = jnp.repeat(anchor_blocks[picks[0]] < blocks[0], BLK)
+    mask = jnp.concatenate([band, jnp.broadcast_to(valid[None, :], (BLK, npick * BLK))], axis=1)
+    mask = jnp.broadcast_to(mask[:, None, :], (BLK, group_size, mask.shape[1]))
+    score = jnp.where(mask.reshape(score.shape), score, jnp.float32(-1e30))
     top = jnp.max(score, axis=-1, keepdims=True)
     expo = jnp.exp(score - top)
     return expo / jnp.sum(expo, axis=-1, keepdims=True)
@@ -52,27 +52,24 @@
 
 def backward(query_rows, kk, vv, probs, cot):
     rows, width = query_rows.shape
-    kvh = kk.shape[2]
-    feat = 2 * kvh * HEAD_SIZE
-    group_size = width // (kvh * HEAD_SIZE)
-    per_dev = rows // BLK
+    feat = 2 * HEAD_SIZE
     scale = HEAD_SIZE ** (-0.5)
-    q_blocks = query_rows.reshape(per_dev, BLK, kvh, group_size, HEAD_SIZE)
+    q2 = query_rows.reshape(-1, HEAD_SIZE)
+    c2 = cot.reshape(-1, HEAD_SIZE)
+    keys = kk.reshape(-1, HEAD_SIZE)
+    vals = vv.reshape(-1, HEAD_SIZE)
+    f32 = jnp.float32
     pb = probs.astype(jnp.bfloat16)
-    outp = jnp.einsum("bkgql,blkd->bqkgd", pb, vv, preferred_element_type=jnp.float32)
-    c_blocks = cot.reshape(per_dev, BLK, kvh, group_size, HEAD_SIZE)
-    delta = jnp.sum(c_blocks.astype(jnp.float32) * outp, axis=-1).transpose(0, 2, 3, 1)[..., None]
-    dprob = jnp.einsum("bqkgd,blkd->bkgql", c_blocks, vv, preferred_element_type=jnp.float32)
+    outp = lax.dot_general(pb, vals, (((1,), (0,)), ((), ())), preferred_element_type=f32)
+    delta = jnp.sum(c2.astype(f32) * outp, axis=-1, keepdims=True)
+    dprob = lax.dot_general(c2, vals, (((1,), (1,)), ((), ())), preferred_element_type=f32)
     dscore = (probs * (dprob - delta)).astype(jnp.bfloat16)
-    dq = jnp.einsum("bkgql,blkd->bqkgd", dscore, kk, preferred_element_type=jnp.float32) * scale
-    dk = (
-        jnp.einsum("bkgql,bqkgd->blkd", dscore, q_blocks, preferred_element_type=jnp.float32)
-        * scale
-    )
-    dv = jnp.einsum("bkgql,bqkgd->blkd", pb, c_blocks, preferred_element_type=jnp.float32)
-    dkv = jnp.stack([dk, dv], axis=3)
-    band_grad = dkv[:, :BLK].reshape(rows, feat)
-    far_grad = dkv[:, BLK:].reshape(-1, BLK, feat)
+    dq = lax.dot_general(dscore, keys, (((1,), (0,)), ((), ())), preferred_element_type=f32) * scale
+    dk = lax.dot_general(dscore, q2, (((0,), (0,)), ((), ())), preferred_element_type=f32) * scale
+    dv = lax.dot_general(pb, c2, (((0,), (0,)), ((), ())), preferred_element_type=f32)
+    dkv = jnp.stack([dk, dv], axis=1).reshape(-1, feat)
+    band_grad = dkv[:BLK]
+    far_grad = dkv[BLK:].reshape(-1, BLK, feat)
     return (dq.reshape(rows, width), band_grad, far_grad)
 
 

time: 103 us -> 105 us (1.019)
  local copies, waits for them, and re-layouts: 8.94 us -> 11.6 us
    reshape x0 -> x5, local copies, waits for them, and re-layouts: none -> 1.9 us  [the longest x2 1.21 us: backward(): c2 = cot.reshape(-1, HEAD_SIZE)]
    cond x1 -> x6, local copies, waits for them, and re-layouts: 0.14 us -> 1.92 us
  transfers between devices with their start and end apart: 3 -> 3, of which waited for: 3 -> 3; matrix products, arithmetic and copies ran while one was open for 1% -> 0% of each run, Pallas kernels for 0% -> 0%
where the time goes in v8:
time: 105 us; the launch traced here: 104 us
  blocking collectives  57.6 us (55%)
  waiting for transfers between devices  21.2 us (20%)
  local copies, waits for them, and re-layouts  11.6 us (11%)
  starting transfers between devices  8.06 us (8%)
  matrix products  2.32 us (2%)
  other arithmetic  1.77 us (2%)
  between operations  1.57 us (1%)
    all_to_all x1, blocking collectives, spread_anchors(): lax.all_to_all(jnp.broadcast_to(row[None], (nx,) + row.shape), 'cx', 0, 0...  17.5 us
    all_to_all x1, blocking collectives, spread_anchors(): got = lax.all_to_all(part, 'cy', 0, 0, tiled=True)  15.7 us
    all_to_all x1, blocking collectives, gather_grads(): got = lax.all_to_all(load, 'cy', 0, 0, tiled=True)  13 us
    all_to_all x1, blocking collectives, gather_grads(): lax.all_to_all(jnp.repeat(rowsum, rows_per_slot, axis=0), 'cx', 0, 0, til...  11.5 us
    all_to_all x1, waiting for transfers between devices, spread_anchors(): lax.all_to_all(jnp.broadcast_to(slots[None], (ny,) + slots.shape), 'cy',...  10.1 us
    all_to_all x1, waiting for transfers between devices, gather_grads(): lax.all_to_all(jnp.broadcast_to(total[None], (ny,) + total.shape), 'cy',...  8.99 us
    all_to_all x1, starting transfers between devices, spread_anchors(): lax.all_to_all(jnp.broadcast_to(slots[None], (ny,) + slots.shape), 'cy',...  3.41 us
    all_to_all x1, starting transfers between devices, gather_grads(): lax.all_to_all(jnp.broadcast_to(total[None], (ny,) + total.shape), 'cy',...  3.37 us
  transfers between devices with their start and end apart: 3, of which 3 were waited for; matrix products, arithmetic and copies ran while one was open for 0% of the time, Pallas kernels for 0%

profile of v8, /device:TPU:2, one launch (start us, length us, event | category | flops | bytes accessed | tf_op | source)
XLA Modules:
  0.0 104.4 jit_solution(6622742861505802496)
XLA Ops:
  0.7 1.2 %dynamic_slice.4 = s32[1]{0:T(128)} dynamic-slice(s32[4]{0:T(128)} %param.14, s32[]{:T(128)S(6)} %select_n.48), dynamic_slice_sizes={1} | dynamic-slice | bytes 12 | tf_op jit(solution)/shard_map/dynamic_slice | solution.py:126
  2.6 15.7 %all_to_all.30 = bf16[8,16,256]{2,1,0:T(8,128)(2,1)S(1)} all-to-all(bf16[8,16,256]{2,1,0:T(8,128)(2,1)S(1)} %bitcast.100), channel_id=1, replica_groups=mesh['section'=2,'cx'=8,'cy'=8,'head'=8] {'cy'}, dimensions={0} | all-to-all | bytes 131072 | tf_op jit(solution)/shard_map/all_to_all | solution.py:81
  18.4 17.5 %all_to_all.31 = bf16[8,16,256]{2,1,0:T(8,128)(2,1)S(1)} all-to-all(bf16[8,16,256]{2,1,0:T(8,128)(2,1)S(1)} %broadcast_in_dim.108), channel_id=1, replica_groups=mesh['section'=2,'cx'=8,'cy'=8,'head'=8] {'cx'}, dimensions={0} | all-to-all | bytes 131072 | tf_op jit(solution)/shard_map/all_to_all | solution.py:83
  35.9 0.7 broadcast_in_dim.109
  36.6 3.4 %all-to-all-start.2 = ((bf16[8,4,16,256]{3,2,1,0:T(8,128)(2,1)}), bf16[8,4,16,256]{3,2,1,0:T(8,128)(2,1)S(1)}, u32[]{:S(2)}, u32[]{:S(2)}) async-start(bf16[8,4,16,256]{3,2,1,0:T(8,128)(2,1)} %broadcast_in_dim.109), calls=%async_computation.2 | async-start | bytes 524288 | tf_op jit(solution)/shard_map/all_to_all | solution.py:88
  40.3 10.1 %all-to-all-done.2 = bf16[8,4,16,256]{3,2,1,0:T(8,128)(2,1)S(1)} async-done(((bf16[8,4,16,256]{3,2,1,0:T(8,128)(2,1)}), bf16[8,4,16,256]{3,2,1,0:T(8,128)(2,1)S(1)}, u32[]{:S(2)}, u32[]{:S(2)}) %all-to-all-start.2) | async-done | bytes 262176 | tf_op jit(solution)/shard_map/all_to_all | solution.py:88
  50.5 0.8 gather_fusion.2
  51.4 4.0 %conditional.2 = (f32[1024,384]{0,1:T(8,128)S(1)}, bf16[128,1024]{1,0:T(8,128)(2,1)S(1)}, f32[128,256]{0,1:T(8,128)}, f32[2,128,256]{1,0,2:T(2,128)}) conditional(s32[]{:T(128)} %convert_element_type.63, (s32[128]{0:T(128)S(1)}, s32[1,2]{1,0:T(1,128)S(1)}, s32[4]{0:T(128)S(1)}, s32[]{:T(128)}, bf16[1,128,1024]{2,1,0:T(8,128)(2,1)S(1)}, ...), branch_computations={%region_2.5_spmd, %region_5.0_spmd} | conditional | flops 609597440 | bytes 33851288 | solution.py:152
  51.5 0.6 gather_fusion
  54.0 0.8 broadcast.93
  54.8 0.7 broadcast.92
  55.4 1.3 %collective-permute-start = (bf16[128,1024]{1,0:T(8,128)(2,1)S(1)}, bf16[128,1024]{1,0:T(8,128)(2,1)S(1)}, u32[]{:S(2)}, u32[]{:S(2)}) collective-permute-start(bf16[128,1024]{1,0:T(8,128)(2,1)S(1)} %get-tuple-element.83), channel_id=1, source_target_pairs={{512,0},{513,1},{514,2},{515,3},{516,4},{517,5},{518,6},{519,7},{5... | collective-permute-start | bytes 786440 | tf_op jit(solution)/shard_map/ppermute | solution.py:13
  56.7 2.1 %collective-permute-done = bf16[128,1024]{1,0:T(8,128)(2,1)S(1)} collective-permute-done((bf16[128,1024]{1,0:T(8,128)(2,1)S(1)}, bf16[128,1024]{1,0:T(8,128)(2,1)S(1)}, u32[]{:S(2)}, u32[]{:S(2)}) %collective-permute-start) | collective-permute-done | bytes 262176 | tf_op jit(solution)/shard_map/ppermute | solution.py:13
  58.8 6.5 %conditional.3 = (bf16[1,128,1024]{2,1,0:T(8,128)(2,1)S(1)}, f32[128,256]{1,0:T(8,128)S(1)}, f32[2,8,4096]{2,0,1:T(2,128)S(1)}) conditional(s32[]{:T(128)} %convert_element_type.63, (bf16[128,1024]{1,0:T(8,128)(2,1)S(1)}, bf16[1,384,1,1,128]{4,1,3,2,0:T(8,128)(2,1)S(1)}, f32[1024,384]{0,1:T(8,128)S(1)}, bf16[1,128,1024]{2,1,0:T(8,128)(2,1)S(1)}, ...), branch_computations={%region_9.11_spmd, %region_11.12_spmd} | conditional | flops 506084352 | bytes 20488300 | solution.py:156
  58.8 0.7 copy-done.4
  59.5 0.7 copy-done.7
  60.7 1.1 %reshape.161 = bf16[1024,128]{1,0:T(8,128)(2,1)S(1)} reshape(bf16[128,1024]{1,0:T(8,128)(2,1)} %copy-done.7) | data formatting | bytes 524288 | tf_op jit(solution)/shard_map/cond/branch_0_fun/reshape | solution.py:58
  62.8 0.5 copy-done.5
  65.6 13.0 %all_to_all.32 = f32[8,2,4224]{2,1,0:T(2,128)S(1)} all-to-all(f32[8,2,4224]{2,1,0:T(2,128)S(1)} %maximum_bitcast_fusion), channel_id=1, replica_groups=mesh['section'=2,'cx'=8,'cy'=8,'head'=8] {'cy'}, dimensions={0} | all-to-all | bytes 540672 | tf_op jit(solution)/shard_map/all_to_all | solution.py:99
  79.2 11.5 %all_to_all.33 = f32[8,16,256]{2,1,0:T(8,128)S(1)} all-to-all(f32[8,16,256]{2,1,0:T(8,128)S(1)} %bitcast.96), channel_id=1, replica_groups=mesh['section'=2,'cx'=8,'cy'=8,'head'=8] {'cx'}, dimensions={0} | all-to-all | bytes 262144 | tf_op jit(solution)/shard_map/all_to_all | solution.py:107
  90.7 0.6 broadcast_in_dim.141
  91.3 3.4 %all-to-all-start.5 = ((f32[8,16,256]{2,1,0:T(8,128)}), f32[8,16,256]{2,1,0:T(8,128)S(1)}, u32[]{:S(2)}, u32[]{:S(2)}) async-start(f32[8,16,256]{2,1,0:T(8,128)} %broadcast_in_dim.141), calls=%async_computation.5 | async-start | bytes 262144 | tf_op jit(solution)/shard_map/all_to_all | solution.py:109
  94.7 9.0 %all-to-all-done.5 = f32[8,16,256]{2,1,0:T(8,128)S(1)} async-done(((f32[8,16,256]{2,1,0:T(8,128)}), f32[8,16,256]{2,1,0:T(8,128)S(1)}, u32[]{:S(2)}, u32[]{:S(2)}) %all-to-all-start.5) | async-done | bytes 131104 | tf_op jit(solution)/shard_map/all_to_all | solution.py:109
  103.7 0.6 fusion.26
  (69 shorter events, 6.6 us)
Async XLA Ops:
  0.6 39.4 %copy-start.9 = (bf16[1,128,256]{2,1,0:T(8,128)(2,1)S(1)}, bf16[1,128,256]{2,1,0:T(8,128)(2,1)}, u32[]{:S(2)}) copy-start(bf16[1,128,256]{2,1,0:T(8,128)(2,1)} %param.11) | copy-start | bytes 196612
  0.6 39.6 %copy-start.11 = (s32[1,2]{1,0:T(1,128)S(1)}, s32[1,2]{1,0:T(1,128)}, u32[]{:S(2)}) copy-start(s32[1,2]{1,0:T(1,128)} %param.15) | copy-start | bytes 28
  35.8 15.5 %copy-start = (s32[4]{0:T(128)S(1)}, s32[4]{0:T(128)}, u32[]{:S(2)}) copy-start(s32[4]{0:T(128)} %param.14) | copy-start | bytes 52
  35.8 15.5 %copy-start.3 = (bf16[1,128,1024]{2,1,0:T(8,128)(2,1)S(1)}, bf16[1,128,1024]{2,1,0:T(8,128)(2,1)}, u32[]{:S(2)}) copy-start(bf16[1,128,1024]{2,1,0:T(8,128)(2,1)} %param.10) | copy-start | bytes 786436
  35.8 15.5 %copy-start.6 = (bf16[128,1024]{1,0:T(8,128)(2,1)S(1)}, bf16[128,1024]{1,0:T(8,128)(2,1)}, u32[]{:S(2)}) copy-start(bf16[128,1024]{1,0:T(8,128)(2,1)} %param.12) | copy-start | bytes 786436
  35.8 15.6 %copy-start.10 = (s32[128]{0:T(128)S(1)}, s32[128]{0:T(128)}, u32[]{:S(2)}) copy-start(s32[128]{0:T(128)} %param.13) | copy-start | bytes 1540
  36.6 13.8 %all-to-all-start.2 = ((bf16[8,4,16,256]{3,2,1,0:T(8,128)(2,1)}), bf16[8,4,16,256]{3,2,1,0:T(8,128)(2,1)S(1)}, u32[]{:S(2)}, u32[]{:S(2)}) async-start(bf16[8,4,16,256]{3,2,1,0:T(8,128)(2,1)} %broadcast_in_dim.109), calls=%async_computation.2 | async-start | bytes 524288 | tf_op jit(solution)/shard_map/all_to_all | solution.py:88
  55.4 3.4 %collective-permute-start = (bf16[128,1024]{1,0:T(8,128)(2,1)S(1)}, bf16[128,1024]{1,0:T(8,128)(2,1)S(1)}, u32[]{:S(2)}, u32[]{:S(2)}) collective-permute-start(bf16[128,1024]{1,0:T(8,128)(2,1)S(1)} %get-tuple-element.83), channel_id=1, source_target_pairs={{512,0},{513,1},{514,2},{515,3},{516,4},{517,5},{518,6},{519,7},{5... | collective-permute-start | bytes 786440 | tf_op jit(solution)/shard_map/ppermute | solution.py:13
  58.8 0.7 copy-start.4
  59.5 0.7 copy-start.7
  62.3 1.0 copy-start.5
  65.4 25.3 %copy-start.8 = (bf16[1,128,1024]{2,1,0:T(8,128)(2,1)}, bf16[1,128,1024]{2,1,0:T(8,128)(2,1)S(1)}, u32[]{:S(2)}) copy-start(bf16[1,128,1024]{2,1,0:T(8,128)(2,1)S(1)} %get-tuple-element.81) | copy-start | bytes 786436
  91.3 12.4 %all-to-all-start.5 = ((f32[8,16,256]{2,1,0:T(8,128)}), f32[8,16,256]{2,1,0:T(8,128)S(1)}, u32[]{:S(2)}, u32[]{:S(2)}) async-start(f32[8,16,256]{2,1,0:T(8,128)} %broadcast_in_dim.141), calls=%async_computation.5 | async-start | bytes 262144 | tf_op jit(solution)/shard_map/all_to_all | solution.py:109

commit v9 on v7

--- a/solution.py
+++ b/solution.py
@@ -80,16 +80,13 @@
     ny = lax.axis_size("cy")
     nx = lax.axis_size("cx")
     blk, feat = mine.shape
-    part = mine.reshape(ny, blk // ny, feat)
-    got = lax.all_to_all(part, "cy", 0, 0, tiled=True)
+    got = lax.all_to_all(jnp.broadcast_to(mine[None], (ny, blk, feat)), "cy", 0, 0, tiled=True)
     row = jnp.sum(got.astype(jnp.float32), axis=0).astype(mine.dtype)
-    got = lax.all_to_all(jnp.broadcast_to(row[None], (nx,) + row.shape), "cx", 0, 0, tiled=True)
+    got = lax.all_to_all(jnp.broadcast_to(row[None], (nx, blk, feat)), "cx", 0, 0, tiled=True)
     nslot = nx // rows_per_slot
-    slots = jnp.sum(
-        got.reshape(nslot, rows_per_slot, *row.shape).astype(jnp.float32), axis=1
+    return jnp.sum(
+        got.reshape(nslot, rows_per_slot, blk, feat).astype(jnp.float32), axis=1
     ).astype(mine.dtype)
-    got = lax.all_to_all(jnp.broadcast_to(slots[None], (ny,) + slots.shape), "cy", 0, 0, tiled=True)
-    return got.transpose(1, 0, 2, 3).reshape(nslot, blk, feat)
 
 
 def gather_grads(far, picks, nslot, rows_per_slot):

time: 103 us -> 104 us (level)
  the two profiles are of different devices: /device:TPU:2 before, /device:TPU:896 now
where the time goes in v9:
time: 104 us; the launch traced here: 103 us
  blocking collectives  50.1 us (48%)
  waiting for transfers between devices  26.6 us (26%)
  starting transfers between devices  11 us (11%)
  local copies, waits for them, and re-layouts  8.5 us (8%)
  matrix products  3.06 us (3%)
  other arithmetic  1.96 us (2%)
  between operations  1.58 us (2%)
    all_to_all x1, blocking collectives, spread_anchors(): lax.all_to_all(jnp.broadcast_to(mine[None], (ny, blk, feat)), 'cy', 0, 0,...  25.4 us
    all_to_all x1, waiting for transfers between devices, spread_anchors(): lax.all_to_all(jnp.broadcast_to(row[None], (nx, blk, feat)), 'cx', 0, 0,...  15.5 us
    all_to_all x1, blocking collectives, gather_grads(): got = lax.all_to_all(load, 'cy', 0, 0, tiled=True)  13.2 us
    all_to_all x1, blocking collectives, gather_grads(): lax.all_to_all(jnp.repeat(rowsum, rows_per_slot, axis=0), 'cx', 0, 0, til...  11.5 us
    all_to_all x1, waiting for transfers between devices, gather_grads(): lax.all_to_all(jnp.broadcast_to(total[None], (ny,) + total.shape), 'cy',...  8.99 us
    all_to_all x1, starting transfers between devices, spread_anchors(): lax.all_to_all(jnp.broadcast_to(row[None], (nx, blk, feat)), 'cx', 0, 0,...  6.35 us
    all_to_all x1, starting transfers between devices, gather_grads(): lax.all_to_all(jnp.broadcast_to(total[None], (ny,) + total.shape), 'cy',...  3.37 us
    another operation x5, local copies, waits for them, and re-layouts  2.61 us
  transfers between devices with their start and end apart: 3, of which 3 were waited for; matrix products, arithmetic and copies ran while one was open for 0% of the time, Pallas kernels for 0%

profile of v9, /device:TPU:896, one launch (start us, length us, event | category | flops | bytes accessed | tf_op | source)
XLA Modules:
  0.0 103.0 jit_solution(9416217578272367604)
XLA Ops:
  0.7 1.2 %dynamic_slice.4 = s32[1]{0:T(128)} dynamic-slice(s32[4]{0:T(128)} %param.14, s32[]{:T(128)S(6)} %select_n.34), dynamic_slice_sizes={1} | dynamic-slice | bytes 12 | tf_op jit(solution)/shard_map/dynamic_slice | solution.py:126
  2.6 25.4 %all_to_all.25 = bf16[8,128,256]{2,1,0:T(8,128)(2,1)S(1)} all-to-all(bf16[8,128,256]{2,1,0:T(8,128)(2,1)S(1)} %broadcast_in_dim.143), channel_id=1, replica_groups=mesh['section'=2,'cx'=8,'cy'=8,'head'=8] {'cy'}, dimensions={0} | all-to-all | bytes 1048576 | tf_op jit(solution)/shard_map/all_to_all | solution.py:83
  28.1 0.8 broadcast_in_dim.144
  29.0 6.4 %all-to-all-start.1 = ((bf16[8,128,256]{2,1,0:T(8,128)(2,1)}), bf16[8,128,256]{2,1,0:T(8,128)(2,1)S(1)}, u32[]{:S(2)}, u32[]{:S(2)}) async-start(bf16[8,128,256]{2,1,0:T(8,128)(2,1)} %broadcast_in_dim.144), calls=%async_computation.1 | async-start | bytes 1048576 | tf_op jit(solution)/shard_map/all_to_all | solution.py:85
  35.7 15.5 %all-to-all-done.1 = bf16[8,128,256]{2,1,0:T(8,128)(2,1)S(1)} async-done(((bf16[8,128,256]{2,1,0:T(8,128)(2,1)}), bf16[8,128,256]{2,1,0:T(8,128)(2,1)S(1)}, u32[]{:S(2)}, u32[]{:S(2)}) %all-to-all-start.1) | async-done | bytes 524320 | tf_op jit(solution)/shard_map/all_to_all | solution.py:85
  51.6 0.6 gather_fusion.2
  52.3 3.6 %conditional.2 = (f32[1,1,8,128,384]{3,4,2,1,0:T(8,128)S(1)}, bf16[128,1024]{0,1:T(8,128)(2,1)S(1)}, f32[128,256]{0,1:T(8,128)}, f32[2,128,256]{1,0,2:T(2,128)}) conditional(s32[]{:T(128)} %convert_element_type.100, (s32[128]{0:T(128)S(1)}, s32[1,2]{1,0:T(1,128)S(1)}, s32[4]{0:T(128)S(1)}, s32[]{:T(128)}, bf16[1,384,1,128]{3,1,2,0:T(8,128)(2,1)S(1)}, ...), branch_computations={%region_2.5_spmd, %region_5.0_spmd} | conditional | flops 609597440 | bytes 31229848 | solution.py:152
  52.6 0.6 gather_fusion
  53.5 0.4 fusion.45
  54.5 0.8 broadcast.222
  55.3 0.7 broadcast.221
  55.9 1.3 %collective-permute-start = (bf16[128,1024]{0,1:T(8,128)(2,1)S(1)}, bf16[128,1024]{0,1:T(8,128)(2,1)S(1)}, u32[]{:S(2)}, u32[]{:S(2)}) collective-permute-start(bf16[128,1024]{0,1:T(8,128)(2,1)S(1)} %get-tuple-element.83), channel_id=1, source_target_pairs={{512,0},{513,1},{514,2},{515,3},{516,4},{517,5},{518,6},{519,7},{5... | collective-permute-start | bytes 786440 | tf_op jit(solution)/shard_map/ppermute | solution.py:13
  57.2 2.1 %collective-permute-done = bf16[128,1024]{0,1:T(8,128)(2,1)S(1)} collective-permute-done((bf16[128,1024]{0,1:T(8,128)(2,1)S(1)}, bf16[128,1024]{0,1:T(8,128)(2,1)S(1)}, u32[]{:S(2)}, u32[]{:S(2)}) %collective-permute-start) | collective-permute-done | bytes 262176 | tf_op jit(solution)/shard_map/ppermute | solution.py:13
  59.3 4.5 %conditional.3 = (bf16[1,128,1024]{2,1,0:T(8,128)(2,1)S(1)}, f32[128,256]{1,0:T(8,128)S(1)}, f32[2,8,4096]{2,0,1:T(2,128)S(1)}) conditional(s32[]{:T(128)} %convert_element_type.100, (bf16[1,384,1,128]{3,1,2,0:T(8,128)(2,1)S(1)}, bf16[128,1024]{0,1:T(8,128)(2,1)S(1)}, f32[1,1,8,128,384]{3,4,2,1,0:T(8,128)S(1)}, ...), branch_computations={%region_9.11_spmd, %region_11.12_spmd} | conditional | flops 506084352 | bytes 13148184 | solution.py:156
  59.7 0.4 fusion.2
  60.0 0.8 copy.190
  60.9 1.3 %fusion.7 = f32[1,384,1,1,128]{1,4,3,2,0:T(8,128)S(1)} fusion(bf16[8,128,384]{1,2,0:T(8,128)(2,1)S(1)} %fusion.2, bf16[128,8,128]{0,2,1:T(8,128)(2,1)} %bitcast.259), kind=kOutput, calls=%fused_computation.15 | convolution fusion | flops 100712448 | bytes 1245184 | tf_op jit(solution)/shard_map/cond/branch_0_fun/bkgql,bqkgd->blkd/dot_general | solution.py:69
  62.2 0.4 convolution_bitcast_fusion.1
  64.0 13.2 %all_to_all.26 = f32[8,2,4224]{2,1,0:T(2,128)S(1)} all-to-all(f32[8,2,4224]{2,1,0:T(2,128)S(1)} %maximum_bitcast_fusion), channel_id=1, replica_groups=mesh['section'=2,'cx'=8,'cy'=8,'head'=8] {'cy'}, dimensions={0} | all-to-all | bytes 540672 | tf_op jit(solution)/shard_map/all_to_all | solution.py:99
  77.8 11.5 %all_to_all.27 = f32[8,16,256]{2,1,0:T(8,128)S(1)} all-to-all(f32[8,16,256]{2,1,0:T(8,128)S(1)} %bitcast.265), channel_id=1, replica_groups=mesh['section'=2,'cx'=8,'cy'=8,'head'=8] {'cx'}, dimensions={0} | all-to-all | bytes 262144 | tf_op jit(solution)/shard_map/all_to_all | solution.py:107
  89.3 0.6 broadcast_in_dim.151
  90.0 3.4 %all-to-all-start.4 = ((f32[8,16,256]{2,1,0:T(8,128)}), f32[8,16,256]{2,1,0:T(8,128)S(1)}, u32[]{:S(2)}, u32[]{:S(2)}) async-start(f32[8,16,256]{2,1,0:T(8,128)} %broadcast_in_dim.151), calls=%async_computation.4 | async-start | bytes 262144 | tf_op jit(solution)/shard_map/all_to_all | solution.py:109
  93.4 9.0 %all-to-all-done.4 = f32[8,16,256]{2,1,0:T(8,128)S(1)} async-done(((f32[8,16,256]{2,1,0:T(8,128)}), f32[8,16,256]{2,1,0:T(8,128)S(1)}, u32[]{:S(2)}, u32[]{:S(2)}) %all-to-all-start.4) | async-done | bytes 131104 | tf_op jit(solution)/shard_map/all_to_all | solution.py:109
  102.4 0.6 fusion.40
  (58 shorter events, 4.3 us)
Async XLA Ops:
  2.6 32.7 %copy-start.6 = (bf16[1,128,256]{2,1,0:T(8,128)(2,1)S(1)}, bf16[1,128,256]{2,1,0:T(8,128)(2,1)}, u32[]{:S(2)}) copy-start(bf16[1,128,256]{2,1,0:T(8,128)(2,1)} %param.11) | copy-start | bytes 196612
  2.6 33.0 %copy-start.8 = (s32[1,2]{1,0:T(1,128)S(1)}, s32[1,2]{1,0:T(1,128)}, u32[]{:S(2)}) copy-start(s32[1,2]{1,0:T(1,128)} %param.15) | copy-start | bytes 28
  29.0 22.2 %all-to-all-start.1 = ((bf16[8,128,256]{2,1,0:T(8,128)(2,1)}), bf16[8,128,256]{2,1,0:T(8,128)(2,1)S(1)}, u32[]{:S(2)}, u32[]{:S(2)}) async-start(bf16[8,128,256]{2,1,0:T(8,128)(2,1)} %broadcast_in_dim.144), calls=%async_computation.1 | async-start | bytes 1048576 | tf_op jit(solution)/shard_map/all_to_all | solution.py:85
  35.3 16.9 %copy-start = (s32[4]{0:T(128)S(1)}, s32[4]{0:T(128)}, u32[]{:S(2)}) copy-start(s32[4]{0:T(128)} %param.14) | copy-start | bytes 52
  35.3 16.9 %copy-start.3 = (bf16[1,128,1024]{2,1,0:T(8,128)(2,1)S(1)}, bf16[1,128,1024]{2,1,0:T(8,128)(2,1)}, u32[]{:S(2)}) copy-start(bf16[1,128,1024]{2,1,0:T(8,128)(2,1)} %param.10) | copy-start | bytes 786436
  35.4 16.9 %copy-start.4 = (bf16[128,1024]{1,0:T(8,128)(2,1)S(1)}, bf16[128,1024]{1,0:T(8,128)(2,1)}, u32[]{:S(2)}) copy-start(bf16[128,1024]{1,0:T(8,128)(2,1)} %param.12) | copy-start | bytes 786436
  35.4 16.9 %copy-start.7 = (s32[128]{0:T(128)S(1)}, s32[128]{0:T(128)}, u32[]{:S(2)}) copy-start(s32[128]{0:T(128)} %param.13) | copy-start | bytes 1540
  55.9 3.4 %collective-permute-start = (bf16[128,1024]{0,1:T(8,128)(2,1)S(1)}, bf16[128,1024]{0,1:T(8,128)(2,1)S(1)}, u32[]{:S(2)}, u32[]{:S(2)}) collective-permute-start(bf16[128,1024]{0,1:T(8,128)(2,1)S(1)} %get-tuple-element.83), channel_id=1, source_target_pairs={{512,0},{513,1},{514,2},{515,3},{516,4},{517,5},{518,6},{519,7},{5... | collective-permute-start | bytes 786440 | tf_op jit(solution)/shard_map/ppermute | solution.py:13
  63.8 25.5 %copy-start.5 = (bf16[1,128,1024]{2,1,0:T(8,128)(2,1)}, bf16[1,128,1024]{2,1,0:T(8,128)(2,1)S(1)}, u32[]{:S(2)}) copy-start(bf16[1,128,1024]{2,1,0:T(8,128)(2,1)S(1)} %get-tuple-element.240) | copy-start | bytes 786436
  90.0 12.4 %all-to-all-start.4 = ((f32[8,16,256]{2,1,0:T(8,128)}), f32[8,16,256]{2,1,0:T(8,128)S(1)}, u32[]{:S(2)}, u32[]{:S(2)}) async-start(f32[8,16,256]{2,1,0:T(8,128)} %broadcast_in_dim.151), calls=%async_computation.4 | async-start | bytes 262144 | tf_op jit(solution)/shard_map/all_to_all | solution.py:109

commit v10 on v8

--- a/solution.py
+++ b/solution.py
@@ -1,6 +1,8 @@
 import jax
 import jax.numpy as jnp
 from jax import lax
+from jax.experimental import pallas as pl
+from jax.experimental.pallas import tpu as pltpu
 from jax.sharding import Mesh, PartitionSpec as P
 
 HEAD_SIZE = 128
@@ -27,50 +29,64 @@
     return keys[:, :, :, 0], keys[:, :, :, 1]
 
 
-def forward(query_rows, kk, sentences, picks, anchor_blocks, blocks):
+def attn_kernel(q_ref, k_ref, v_ref, c_ref, m_ref, dq_ref, dk_ref, dv_ref):
+    f32 = jnp.float32
+    scale = HEAD_SIZE ** (-0.5)
+    keys = k_ref[...]
+    vals = v_ref[...]
+    keep = m_ref[...] > 0.5
+    nt = (((1,), (1,)), ((), ()))
+    nn = (((1,), (0,)), ((), ()))
+    tn = (((0,), (0,)), ((), ()))
+    dk = jnp.zeros(dk_ref.shape, f32)
+    dv = jnp.zeros(dv_ref.shape, f32)
+    for g in range(q_ref.shape[1] // HEAD_SIZE):
+        cols = slice(g * HEAD_SIZE, (g + 1) * HEAD_SIZE)
+        qg = q_ref[:, cols]
+        cg = c_ref[:, cols]
+        score = lax.dot_general(qg, keys, nt, preferred_element_type=f32) * scale
+        score = jnp.where(keep, score, f32(-1e30))
+        top = jnp.max(score, axis=-1, keepdims=True)
+        expo = jnp.exp(score - top)
+        probs = expo / jnp.sum(expo, axis=-1, keepdims=True)
+        pb = probs.astype(jnp.bfloat16)
+        outp = lax.dot_general(pb, vals, nn, preferred_element_type=f32)
+        delta = jnp.sum(cg.astype(f32) * outp, axis=-1, keepdims=True)
+        dprob = lax.dot_general(cg, vals, nt, preferred_element_type=f32)
+        dscore = (probs * (dprob - delta)).astype(jnp.bfloat16)
+        dq_ref[:, cols] = lax.dot_general(dscore, keys, nn, preferred_element_type=f32) * scale
+        dk = dk + lax.dot_general(dscore, qg, tn, preferred_element_type=f32)
+        dv = dv + lax.dot_general(pb, cg, tn, preferred_element_type=f32)
+    dk_ref[...] = dk * scale
+    dv_ref[...] = dv
+
+
+def attend(query_rows, kk, vv, mask, cot):
     rows, width = query_rows.shape
-    assert rows == BLK and kk.shape[0] == 1 and kk.shape[2] == 1
-    group_size = width // HEAD_SIZE
+    nkeys = kk.shape[0]
+    vmem = pl.BlockSpec(memory_space=pltpu.VMEM)
+    dq, dk, dv = pl.pallas_call(
+        attn_kernel,
+        out_shape=(
+            jax.ShapeDtypeStruct((rows, width), jnp.float32),
+            jax.ShapeDtypeStruct((nkeys, HEAD_SIZE), jnp.float32),
+            jax.ShapeDtypeStruct((nkeys, HEAD_SIZE), jnp.float32),
+        ),
+        in_specs=[vmem] * 5,
+        out_specs=(vmem, vmem, vmem),
+    )(query_rows, kk, vv, cot, mask)
+    dkv = jnp.stack([dk, dv], axis=1).reshape(nkeys, 2 * HEAD_SIZE)
+    return dq, dkv[:BLK], dkv[BLK:].reshape(-1, BLK, 2 * HEAD_SIZE)
+
+
+def mask_of(sentences, picks, anchor_blocks, blocks):
     npick = picks.shape[1]
-    scale = HEAD_SIZE ** (-0.5)
-    q2 = query_rows.reshape(rows * group_size, HEAD_SIZE)
-    keys = kk.reshape(-1, HEAD_SIZE)
-    score = lax.dot_general(
-        q2, keys, (((1,), (1,)), ((), ())), preferred_element_type=jnp.float32
-    ) * scale
     sent = sentences.reshape(BLK)
     idx = jnp.arange(BLK, dtype=jnp.int32)
     band = (idx[:, None] >= idx[None, :]) & (sent[:, None] == sent[None, :])
     valid = jnp.repeat(anchor_blocks[picks[0]] < blocks[0], BLK)
     mask = jnp.concatenate([band, jnp.broadcast_to(valid[None, :], (BLK, npick * BLK))], axis=1)
-    mask = jnp.broadcast_to(mask[:, None, :], (BLK, group_size, mask.shape[1]))
-    score = jnp.where(mask.reshape(score.shape), score, jnp.float32(-1e30))
-    top = jnp.max(score, axis=-1, keepdims=True)
-    expo = jnp.exp(score - top)
-    return expo / jnp.sum(expo, axis=-1, keepdims=True)
-
-
-def backward(query_rows, kk, vv, probs, cot):
-    rows, width = query_rows.shape
-    feat = 2 * HEAD_SIZE
-    scale = HEAD_SIZE ** (-0.5)
-    q2 = query_rows.reshape(-1, HEAD_SIZE)
-    c2 = cot.reshape(-1, HEAD_SIZE)
-    keys = kk.reshape(-1, HEAD_SIZE)
-    vals = vv.reshape(-1, HEAD_SIZE)
-    f32 = jnp.float32
-    pb = probs.astype(jnp.bfloat16)
-    outp = lax.dot_general(pb, vals, (((1,), (0,)), ((), ())), preferred_element_type=f32)
-    delta = jnp.sum(c2.astype(f32) * outp, axis=-1, keepdims=True)
-    dprob = lax.dot_general(c2, vals, (((1,), (1,)), ((), ())), preferred_element_type=f32)
-    dscore = (probs * (dprob - delta)).astype(jnp.bfloat16)
-    dq = lax.dot_general(dscore, keys, (((1,), (0,)), ((), ())), preferred_element_type=f32) * scale
-    dk = lax.dot_general(dscore, q2, (((0,), (0,)), ((), ())), preferred_element_type=f32) * scale
-    dv = lax.dot_general(pb, c2, (((0,), (0,)), ((), ())), preferred_element_type=f32)
-    dkv = jnp.stack([dk, dv], axis=1).reshape(-1, feat)
-    band_grad = dkv[:BLK]
-    far_grad = dkv[BLK:].reshape(-1, BLK, feat)
-    return (dq.reshape(rows, width), band_grad, far_grad)
+    return mask.astype(jnp.float32)
 
 
 def spread_anchors(mine, rows_per_slot):
@@ -123,40 +139,36 @@
     section_one = lax.axis_index("section") == 1
     blocks = ctx * per_dev + jnp.arange(per_dev, dtype=jnp.int32)
     kv_blocks = keyvals.reshape(per_dev, BLK, feat)
-    holder = (anchor_blocks[rank] == blocks)[:, None, None]
+    hit = anchor_blocks[None, :] == blocks[:, None]
+    holder = jnp.any(hit, axis=1)[:, None, None]
     mine = jnp.where(holder, kv_blocks, jnp.zeros_like(kv_blocks)).sum(axis=0, dtype=jnp.float32)
     mine = mine.astype(jnp.bfloat16)
     anchor_kv = spread_anchors(mine, rows_per_slot)
     npick = anchor_pick.shape[1]
     kk, vv = gather_keys(keyvals, anchor_kv, anchor_pick)
 
-    def probs_of():
-        return forward(query_rows, kk, sentences, anchor_pick, anchor_blocks, blocks)
-
-    def relayed(probs, cot):
-        dq, band, far = backward(query_rows, kk, vv, probs, cot)
+    assert per_dev == 1 and feat == 2 * HEAD_SIZE
+    keys = kk.reshape(-1, HEAD_SIZE)
+    vals = vv.reshape(-1, HEAD_SIZE)
+    mask = mask_of(sentences, anchor_pick, anchor_blocks, blocks)
+
+    def relayed(cot):
+        dq, band, far = attend(query_rows, keys, vals, mask, cot)
         return dq.astype(jnp.bfloat16), band, far
 
-    def second_layer(cot):
-        probs = probs_of()
-        return (probs,) + relayed(probs, cot)
-
-    def first_layer_probs(cot):
+    def waiting(cot):
         return (
-            probs_of(),
             cot,
             jnp.zeros((rows, feat), jnp.float32),
             jnp.zeros((per_dev * npick, BLK, feat), jnp.float32),
         )
 
-    probs, sent_back, band_first, far_first = lax.cond(
-        section_one, second_layer, first_layer_probs, out_grad
-    )
+    sent_back, band_first, far_first = lax.cond(section_one, relayed, waiting, out_grad)
     arrived = from_behind(sent_back, "section", -1)
     dq_out, band_grad, far = lax.cond(
         section_one,
         lambda cot: (sent_back, band_first, far_first),
-        lambda cot: relayed(probs, cot),
+        relayed,
         arrived,
     )
     total = gather_grads(far, anchor_pick.reshape(-1), nanch, rows_per_slot)

time: 105 us -> 107 us (1.019)
  blocking collectives: 57.6 us -> 24.4 us
  starting transfers between devices: 8.06 us -> 27.9 us
  waiting for transfers between devices: 21.2 us -> 33.8 us
  Pallas kernels: 0 us -> 6.03 us
  local copies, waits for them, and re-layouts: 11.6 us -> 8.32 us
  other arithmetic: 1.77 us -> 4.31 us
  matrix products: 2.32 us -> 0 us
    all_to_all x2 -> x0, blocking collectives: 33.2 us -> none  [the longest x1 17.5 us: spread_anchors(): lax.all_to_all(jnp.broadcast_to(row[None], (nx,) + row.shape), 'cx', 0, 0...]
    all_to_all x0 -> x2, starting transfers between devices: none -> 19.8 us  [the longest x1 12.1 us: spread_anchors(): lax.all_to_all(jnp.broadcast_to(row[None], (nx,) + row.shape), 'cx', 0, 0...]
    all_to_all x0 -> x2, waiting for transfers between devices: none -> 14.6 us  [the longest x1 7.69 us: spread_anchors(): got = lax.all_to_all(part, 'cy', 0, 0, tiled=True)]
    pallas_call x0 -> x1, Pallas kernels: none -> 6.03 us  [attend(): pl.pallas_call(attn_kernel, out_shape=(jax.ShapeDtypeStruct((rows, width)...]
    unnamed x16, local copies, waits for them, and re-layouts: 0.16 us -> 2.93 us
    dot_general x6 -> x0, matrix products: 2.32 us -> none  [the longest x1 0.43 us: forward(): lax.dot_general(q2, keys, (((1,), (1,)), ((), ())), preferred_element_typ...]
    another operation x5 -> x2, local copies, waits for them, and re-layouts: 2.12 us -> 0.03 us
    reshape x5 -> x0, local copies, waits for them, and re-layouts: 1.9 us -> none  [the longest x2 1.21 us: backward(): c2 = cot.reshape(-1, HEAD_SIZE)]
  transfers between devices with their start and end apart: 3 -> 5, of which waited for: 3 -> 5; matrix products, arithmetic and copies ran while one was open for 0% -> 2% of each run, Pallas kernels for 0% -> 0%
where the time goes in v10:
time: 107 us; the launch traced here: 106 us
  waiting for transfers between devices  33.8 us (32%)
  starting transfers between devices  27.9 us (26%)
  blocking collectives  24.4 us (23%)
  local copies, waits for them, and re-layouts  8.32 us (8%)
  Pallas kernels  6.03 us (6%)
  other arithmetic  4.31 us (4%)
  between operations  1.58 us (1%)
    all_to_all x1, blocking collectives, gather_grads(): got = lax.all_to_all(load, 'cy', 0, 0, tiled=True)  13 us
    all_to_all x1, starting transfers between devices, spread_anchors(): lax.all_to_all(jnp.broadcast_to(row[None], (nx,) + row.shape), 'cx', 0, 0...  12.1 us
    all_to_all x1, blocking collectives, gather_grads(): lax.all_to_all(jnp.repeat(rowsum, rows_per_slot, axis=0), 'cx', 0, 0, til...  11.5 us
    all_to_all x1, waiting for transfers between devices, spread_anchors(): lax.all_to_all(jnp.broadcast_to(slots[None], (ny,) + slots.shape), 'cy',...  9.34 us
    all_to_all x1, waiting for transfers between devices, gather_grads(): lax.all_to_all(jnp.broadcast_to(total[None], (ny,) + total.shape), 'cy',...  7.74 us
    all_to_all x1, waiting for transfers between devices, spread_anchors(): got = lax.all_to_all(part, 'cy', 0, 0, tiled=True)  7.69 us
    all_to_all x1, starting transfers between devices, spread_anchors(): got = lax.all_to_all(part, 'cy', 0, 0, tiled=True)  7.69 us
    all_to_all x1, waiting for transfers between devices, spread_anchors(): lax.all_to_all(jnp.broadcast_to(row[None], (nx,) + row.shape), 'cx', 0, 0...  6.87 us
  transfers between devices with their start and end apart: 5, of which 5 were waited for; matrix products, arithmetic and copies ran while one was open for 2% of the time, Pallas kernels for 0%

profile of v10, /device:TPU:2, one launch (start us, length us, event | category | flops | bytes accessed | tf_op | source)
XLA Modules:
  0.0 106.4 jit_solution(3308189342715072041)
XLA Ops:
  0.7 0.7 copy-done
  2.0 1.3 %broadcast_select_fusion = bf16[1,128,256]{2,1,0:T(8,128)(2,1)} fusion(bf16[1,128,256]{2,1,0:T(8,128)(2,1)S(1)} %copy-done.8, pred[]{:T(512)} %compare_reduce_fusion), kind=kLoop, calls=%fused_computation.23 | loop fusion | flops 32768 | bytes 131073 | tf_op jit(solution)/shard_map/jit(_where)/select_n | solution.py:144
  3.3 7.7 %all-to-all-start = ((bf16[8,16,256]{2,1,0:T(8,128)(2,1)}), bf16[8,16,256]{2,1,0:T(8,128)(2,1)S(1)}, u32[]{:S(2)}, u32[]{:S(2)}) async-start(bf16[8,16,256]{2,1,0:T(8,128)(2,1)} %bitcast.10), calls=%async_computation | async-start | bytes 131072 | tf_op jit(solution)/shard_map/all_to_all | solution.py:97
  11.0 0.6 gather_fusion.1
  11.6 7.7 %all-to-all-done = bf16[8,16,256]{2,1,0:T(8,128)(2,1)S(1)} async-done(((bf16[8,16,256]{2,1,0:T(8,128)(2,1)}), bf16[8,16,256]{2,1,0:T(8,128)(2,1)S(1)}, u32[]{:S(2)}, u32[]{:S(2)}) %all-to-all-start) | async-done | bytes 65568 | tf_op jit(solution)/shard_map/all_to_all | solution.py:97
  19.3 0.6 broadcast_in_dim.93
  20.0 12.1 %all-to-all-start.1 = ((bf16[8,16,256]{2,1,0:T(8,128)(2,1)}), bf16[8,16,256]{2,1,0:T(8,128)(2,1)S(1)}, u32[]{:S(2)}, u32[]{:S(2)}) async-start(bf16[8,16,256]{2,1,0:T(8,128)(2,1)} %broadcast_in_dim.93), calls=%async_computation.1 | async-start | bytes 131072 | tf_op jit(solution)/shard_map/all_to_all | solution.py:99
  32.2 6.9 %all-to-all-done.1 = bf16[8,16,256]{2,1,0:T(8,128)(2,1)S(1)} async-done(((bf16[8,16,256]{2,1,0:T(8,128)(2,1)}), bf16[8,16,256]{2,1,0:T(8,128)(2,1)S(1)}, u32[]{:S(2)}, u32[]{:S(2)}) %all-to-all-start.1) | async-done | bytes 65568 | tf_op jit(solution)/shard_map/all_to_all | solution.py:99
  39.1 0.7 broadcast_in_dim.94
  39.8 3.4 %all-to-all-start.2 = ((bf16[8,4,16,256]{3,2,1,0:T(8,128)(2,1)}), bf16[8,4,16,256]{3,2,1,0:T(8,128)(2,1)S(1)}, u32[]{:S(2)}, u32[]{:S(2)}) async-start(bf16[8,4,16,256]{3,2,1,0:T(8,128)(2,1)} %broadcast_in_dim.94), calls=%async_computation.2 | async-start | bytes 524288 | tf_op jit(solution)/shard_map/all_to_all | solution.py:104
  43.5 0.6 copy-done.9
  44.3 9.3 %all-to-all-done.2 = bf16[8,4,16,256]{3,2,1,0:T(8,128)(2,1)S(1)} async-done(((bf16[8,4,16,256]{3,2,1,0:T(8,128)(2,1)}), bf16[8,4,16,256]{3,2,1,0:T(8,128)(2,1)S(1)}, u32[]{:S(2)}, u32[]{:S(2)}) %all-to-all-start.2) | async-done | bytes 262176 | tf_op jit(solution)/shard_map/all_to_all | solution.py:104
  54.4 0.9 copy-done.2
  55.4 1.3 %collective-permute-start = (bf16[128,1024]{1,0:T(8,128)(2,1)S(1)}, bf16[128,1024]{1,0:T(8,128)(2,1)S(1)}, u32[]{:S(2)}, u32[]{:S(2)}) collective-permute-start(bf16[128,1024]{1,0:T(8,128)(2,1)S(1)} %get-tuple-element.59), channel_id=1, source_target_pairs={{512,0},{513,1},{514,2},{515,3},{516,4},{517,5},{518,6},{519,7},{5... | collective-permute-start | bytes 786440 | tf_op jit(solution)/shard_map/ppermute | solution.py:15
  56.7 2.1 %collective-permute-done = bf16[128,1024]{1,0:T(8,128)(2,1)S(1)} collective-permute-done((bf16[128,1024]{1,0:T(8,128)(2,1)S(1)}, bf16[128,1024]{1,0:T(8,128)(2,1)S(1)}, u32[]{:S(2)}, u32[]{:S(2)}) %collective-permute-start) | collective-permute-done | bytes 262176 | tf_op jit(solution)/shard_map/ppermute | solution.py:15
  58.8 8.1 %conditional.3 = (bf16[1,128,1024]{2,1,0:T(8,128)(2,1)S(1)}, f32[128,256]{1,0:T(8,128)S(1)}, f32[2,8,4096]{2,0,1:T(2,128)S(1)}) conditional(s32[]{:T(128)} %convert_element_type.37, (bf16[128,1024]{1,0:T(8,128)(2,1)S(1)}, bf16[384,128]{1,0:T(8,128)(2,1)S(1)}, bf16[384,128]{1,0:T(8,128)(2,1)S(1)}, bf16[128,1024]{1,0:T(8,128)(2,1)S(1)}, ...), branch_computations={%region_5.6_spmd, %region_6.7_spmd} | conditional | flops 229376 | bytes 5636176 | solution.py:168
  58.8 6.0 %branch_0_fun.1 = (f32[128,1024]{1,0:T(8,128)}, f32[384,128]{1,0:T(8,128)}, f32[384,128]{1,0:T(8,128)}) custom-call(bf16[128,1024]{1,0:T(8,128)(2,1)S(1)} %get-tuple-element.40.q_ref, bf16[384,128]{1,0:T(8,128)(2,1)S(1)} %get-tuple-element.41.k_ref, bf16[384,128]{1,0:T(8,128)(2,1)S(1)} %get-tuple-element.42.v_ref, ...), custom_call_target="tpu_custom_call" | custom-call | tf_op jit(solution)/shard_map/cond/branch_0_fun/pallas_call | solution.py:68
  64.9 1.1 %convert_bitcast_fusion = bf16[1,128,1024]{2,1,0:T(8,128)(2,1)S(1)} fusion(f32[128,1024]{1,0:T(8,128)} %get-tuple-element.47), kind=kLoop, calls=%fused_computation.5 | loop fusion | flops 131072 | bytes 786432 | tf_op jit(solution)/shard_map/broadcast_in_dim | solution.py:179
  67.7 13.0 %all_to_all.30 = f32[8,2,4224]{2,1,0:T(2,128)S(1)} all-to-all(f32[8,2,4224]{2,1,0:T(2,128)S(1)} %maximum_bitcast_fusion), channel_id=1, replica_groups=mesh['section'=2,'cx'=8,'cy'=8,'head'=8] {'cy'}, dimensions={0} | all-to-all | bytes 540672 | tf_op jit(solution)/shard_map/all_to_all | solution.py:115
  81.2 11.5 %all_to_all.31 = f32[8,16,256]{2,1,0:T(8,128)S(1)} all-to-all(f32[8,16,256]{2,1,0:T(8,128)S(1)} %bitcast.62), channel_id=1, replica_groups=mesh['section'=2,'cx'=8,'cy'=8,'head'=8] {'cx'}, dimensions={0} | all-to-all | bytes 262144 | tf_op jit(solution)/shard_map/all_to_all | solution.py:123
  92.7 0.7 broadcast_in_dim.104
  93.4 3.4 %all-to-all-start.5 = ((f32[8,16,256]{2,1,0:T(8,128)}), f32[8,16,256]{2,1,0:T(8,128)S(1)}, u32[]{:S(2)}, u32[]{:S(2)}) async-start(f32[8,16,256]{2,1,0:T(8,128)} %broadcast_in_dim.104), calls=%async_computation.5 | async-start | bytes 262144 | tf_op jit(solution)/shard_map/all_to_all | solution.py:125
  98.0 7.7 %all-to-all-done.5 = f32[8,16,256]{2,1,0:T(8,128)S(1)} async-done(((f32[8,16,256]{2,1,0:T(8,128)}), f32[8,16,256]{2,1,0:T(8,128)S(1)}, u32[]{:S(2)}, u32[]{:S(2)}) %all-to-all-start.5) | async-done | bytes 131104 | tf_op jit(solution)/shard_map/all_to_all | solution.py:125
  105.8 0.6 fusion
  (58 shorter events, 4.8 us)
Async XLA Ops:
  0.6 1.3 %copy-start.8 = (bf16[1,128,256]{2,1,0:T(8,128)(2,1)S(1)}, bf16[1,128,256]{2,1,0:T(8,128)(2,1)}, u32[]{:S(2)}) copy-start(bf16[1,128,256]{2,1,0:T(8,128)(2,1)} %param.11) | copy-start | bytes 196612
  0.6 0.7 copy-start
  3.3 7.7 %copy-start.10 = (s32[1,2]{1,0:T(1,128)S(1)}, s32[1,2]{1,0:T(1,128)}, u32[]{:S(2)}) copy-start(s32[1,2]{1,0:T(1,128)} %param.15) | copy-start | bytes 28
  3.3 16.1 %all-to-all-start = ((bf16[8,16,256]{2,1,0:T(8,128)(2,1)}), bf16[8,16,256]{2,1,0:T(8,128)(2,1)S(1)}, u32[]{:S(2)}, u32[]{:S(2)}) async-start(bf16[8,16,256]{2,1,0:T(8,128)(2,1)} %bitcast.10), calls=%async_computation | async-start | bytes 131072 | tf_op jit(solution)/shard_map/all_to_all | solution.py:97
  20.0 19.1 %all-to-all-start.1 = ((bf16[8,16,256]{2,1,0:T(8,128)(2,1)}), bf16[8,16,256]{2,1,0:T(8,128)(2,1)S(1)}, u32[]{:S(2)}, u32[]{:S(2)}) async-start(bf16[8,16,256]{2,1,0:T(8,128)(2,1)} %broadcast_in_dim.93), calls=%async_computation.1 | async-start | bytes 131072 | tf_op jit(solution)/shard_map/all_to_all | solution.py:99
  39.8 13.8 %all-to-all-start.2 = ((bf16[8,4,16,256]{3,2,1,0:T(8,128)(2,1)}), bf16[8,4,16,256]{3,2,1,0:T(8,128)(2,1)S(1)}, u32[]{:S(2)}, u32[]{:S(2)}) async-start(bf16[8,4,16,256]{3,2,1,0:T(8,128)(2,1)} %broadcast_in_dim.94), calls=%async_computation.2 | async-start | bytes 524288 | tf_op jit(solution)/shard_map/all_to_all | solution.py:104
  43.5 0.7 copy-start.9
  54.3 1.0 copy-start.2
  54.4 1.0 copy-start.1
  55.4 3.4 %collective-permute-start = (bf16[128,1024]{1,0:T(8,128)(2,1)S(1)}, bf16[128,1024]{1,0:T(8,128)(2,1)S(1)}, u32[]{:S(2)}, u32[]{:S(2)}) collective-permute-start(bf16[128,1024]{1,0:T(8,128)(2,1)S(1)} %get-tuple-element.59), channel_id=1, source_target_pairs={{512,0},{513,1},{514,2},{515,3},{516,4},{517,5},{518,6},{519,7},{5... | collective-permute-start | bytes 786440 | tf_op jit(solution)/shard_map/ppermute | solution.py:15
  64.9 1.1 %copy-start.3 = (f32[384,128]{1,0:T(8,128)S(1)}, f32[384,128]{1,0:T(8,128)}, u32[]{:S(2)}) copy-start(f32[384,128]{1,0:T(8,128)} %get-tuple-element.45) | copy-start | bytes 589828 | tf_op jit(solution)/shard_map/cond
  64.9 1.2 %copy-start.4 = (f32[384,128]{1,0:T(8,128)S(1)}, f32[384,128]{1,0:T(8,128)}, u32[]{:S(2)}) copy-start(f32[384,128]{1,0:T(8,128)} %get-tuple-element.46) | copy-start | bytes 589828 | tf_op jit(solution)/shard_map/cond
  66.9 0.7 copy-start.7
  93.4 12.4 %all-to-all-start.5 = ((f32[8,16,256]{2,1,0:T(8,128)}), f32[8,16,256]{2,1,0:T(8,128)S(1)}, u32[]{:S(2)}, u32[]{:S(2)}) async-start(f32[8,16,256]{2,1,0:T(8,128)} %broadcast_in_dim.104), calls=%async_computation.5 | async-start | bytes 262144 | tf_op jit(solution)/shard_map/all_to_all | solution.py:125

commit v11 on v6

--- a/solution.py
+++ b/solution.py
@@ -51,29 +51,50 @@
 
 
 def backward(query_rows, kk, vv, probs, cot):
-    rows, width = query_rows.shape
-    kvh = kk.shape[2]
-    feat = 2 * kvh * HEAD_SIZE
+    dscore, pb = scores_grad(kk, vv, probs, cot)
+    dq, band_grad = near_grads(query_rows, kk, cot, dscore, pb)
+    return (dq, band_grad, far_grads(query_rows, cot, dscore, pb))
+
+
+def scores_grad(kk, vv, probs, cot):
+    per_dev, nkeys, kvh, _ = kk.shape
+    width = cot.shape[1]
     group_size = width // (kvh * HEAD_SIZE)
-    per_dev = rows // BLK
-    scale = HEAD_SIZE ** (-0.5)
-    q_blocks = query_rows.reshape(per_dev, BLK, kvh, group_size, HEAD_SIZE)
     pb = probs.astype(jnp.bfloat16)
     outp = jnp.einsum("bkgql,blkd->bqkgd", pb, vv, preferred_element_type=jnp.float32)
     c_blocks = cot.reshape(per_dev, BLK, kvh, group_size, HEAD_SIZE)
     delta = jnp.sum(c_blocks.astype(jnp.float32) * outp, axis=-1).transpose(0, 2, 3, 1)[..., None]
     dprob = jnp.einsum("bqkgd,blkd->bkgql", c_blocks, vv, preferred_element_type=jnp.float32)
     dscore = (probs * (dprob - delta)).astype(jnp.bfloat16)
+    return dscore, pb
+
+
+def key_grads(query_rows, cot, dscore, pb, cols):
+    rows, width = query_rows.shape
+    per_dev, kvh, group_size = dscore.shape[:3]
+    scale = HEAD_SIZE ** (-0.5)
+    q_blocks = query_rows.reshape(per_dev, BLK, kvh, group_size, HEAD_SIZE)
+    c_blocks = cot.reshape(per_dev, BLK, kvh, group_size, HEAD_SIZE)
+    ds = dscore[..., cols]
+    p = pb[..., cols]
+    dk = jnp.einsum("bkgql,bqkgd->blkd", ds, q_blocks, preferred_element_type=jnp.float32) * scale
+    dv = jnp.einsum("bkgql,bqkgd->blkd", p, c_blocks, preferred_element_type=jnp.float32)
+    return jnp.stack([dk, dv], axis=3)
+
+
+def far_grads(query_rows, cot, dscore, pb):
+    feat = 2 * dscore.shape[1] * HEAD_SIZE
+    dkv = key_grads(query_rows, cot, dscore, pb, slice(BLK, None))
+    return dkv.reshape(-1, BLK, feat)
+
+
+def near_grads(query_rows, kk, cot, dscore, pb):
+    rows, width = query_rows.shape
+    feat = 2 * dscore.shape[1] * HEAD_SIZE
+    scale = HEAD_SIZE ** (-0.5)
     dq = jnp.einsum("bkgql,blkd->bqkgd", dscore, kk, preferred_element_type=jnp.float32) * scale
-    dk = (
-        jnp.einsum("bkgql,bqkgd->blkd", dscore, q_blocks, preferred_element_type=jnp.float32)
-        * scale
-    )
-    dv = jnp.einsum("bkgql,bqkgd->blkd", pb, c_blocks, preferred_element_type=jnp.float32)
-    dkv = jnp.stack([dk, dv], axis=3)
-    band_grad = dkv[:, :BLK].reshape(rows, feat)
-    far_grad = dkv[:, BLK:].reshape(-1, BLK, feat)
-    return (dq.reshape(rows, width), band_grad, far_grad)
+    band_grad = key_grads(query_rows, cot, dscore, pb, slice(0, BLK)).reshape(rows, feat)
+    return dq.reshape(rows, width), band_grad
 
 
 def spread_anchors(mine, rows_per_slot):
@@ -157,13 +178,23 @@
         section_one, second_layer, first_layer_probs, out_grad
     )
     arrived = from_behind(sent_back, "section", -1)
-    dq_out, band_grad, far = lax.cond(
+    far, dscore, pb = lax.cond(
         section_one,
-        lambda cot: (sent_back, band_first, far_first),
-        lambda cot: relayed(probs, cot),
+        lambda cot: (far_first, jnp.zeros_like(probs, jnp.bfloat16), jnp.zeros_like(probs, jnp.bfloat16)),
+        lambda cot: (lambda ds, p: (far_grads(query_rows, cot, ds, p), ds, p))(
+            *scores_grad(kk, vv, probs, cot)
+        ),
         arrived,
     )
     total = gather_grads(far, anchor_pick.reshape(-1), nanch, rows_per_slot)
+    dq_out, band_grad = lax.cond(
+        section_one,
+        lambda cot: (sent_back, band_first),
+        lambda cot: (lambda dq, band: (dq.astype(jnp.bfloat16), band))(
+            *near_grads(query_rows, kk, cot, dscore, pb)
+        ),
+        arrived,
+    )
     owner = (anchor_blocks[rank] == blocks).astype(jnp.float32)
     owned = owner[:, None, None] * total[None]
     kv_grad = (band_grad + owned.reshape(band_grad.shape)).astype(jnp.bfloat16)

time: 103 us -> 105 us (1.019)
  the two profiles are of different devices: /device:TPU:2 before, /device:TPU:256 now
where the time goes in v11:
time: 105 us; the launch traced here: 104 us
  blocking collectives  55.2 us (53%)
  waiting for transfers between devices  18.9 us (18%)
  local copies, waits for them, and re-layouts  9.68 us (9%)
  starting transfers between devices  8.22 us (8%)
  matrix products  6.38 us (6%)
  other arithmetic  3.79 us (4%)
  between operations  1.62 us (2%)
    all_to_all x1, blocking collectives, spread_anchors(): got = lax.all_to_all(part, 'cy', 0, 0, tiled=True)  15.7 us
    all_to_all x1, blocking collectives, spread_anchors(): lax.all_to_all(jnp.broadcast_to(row[None], (nx,) + row.shape), 'cx', 0, 0...  14.9 us
    all_to_all x1, blocking collectives, gather_grads(): got = lax.all_to_all(load, 'cy', 0, 0, tiled=True)  13.1 us
    all_to_all x1, blocking collectives, gather_grads(): lax.all_to_all(jnp.repeat(rowsum, rows_per_slot, axis=0), 'cx', 0, 0, til...  11.5 us
    all_to_all x1, waiting for transfers between devices, spread_anchors(): lax.all_to_all(jnp.broadcast_to(slots[None], (ny,) + slots.shape), 'cy',...  9.26 us
    ppermute x1, waiting for transfers between devices, from_behind(): return lax.ppermute(x, axis, pairs)  4.94 us
    all_to_all x1, waiting for transfers between devices, gather_grads(): lax.all_to_all(jnp.broadcast_to(total[None], (ny,) + total.shape), 'cy',...  4.73 us
    all_to_all x1, starting transfers between devices, spread_anchors(): lax.all_to_all(jnp.broadcast_to(slots[None], (ny,) + slots.shape), 'cy',...  3.56 us
  transfers between devices with their start and end apart: 3, of which 3 were waited for; matrix products, arithmetic and copies ran while one was open for 4% of the time, Pallas kernels for 0%

profile of v11, /device:TPU:256, one launch (start us, length us, event | category | flops | bytes accessed | tf_op | source)
XLA Modules:
  0.0 104.1 jit_solution(2638996652011999931)
XLA Ops:
  0.6 1.3 %compare_reduce_fusion = pred[]{:T(512)} fusion(s32[4]{0:T(128)} %param.16, s32[]{:T(128)} %add.22), kind=kLoop, calls=%fused_computation.104 | loop fusion | flops 7 | bytes 21 | tf_op jit(solution)/shard_map/reduce_or | solution.py:151
  1.9 0.7 broadcast_select_fusion
  2.6 15.7 %all_to_all.30 = bf16[8,16,256]{2,1,0:T(8,128)(2,1)S(1)} all-to-all(bf16[8,16,256]{2,1,0:T(8,128)(2,1)S(1)} %bitcast.334), channel_id=1, replica_groups=mesh['section'=2,'cx'=8,'cy'=8,'head'=8] {'cy'}, dimensions={0} | all-to-all | bytes 131072 | tf_op jit(solution)/shard_map/all_to_all | solution.py:105
  18.4 14.9 %all_to_all.31 = bf16[8,16,256]{2,1,0:T(8,128)(2,1)S(1)} all-to-all(bf16[8,16,256]{2,1,0:T(8,128)(2,1)S(1)} %broadcast_in_dim.138), channel_id=1, replica_groups=mesh['section'=2,'cx'=8,'cy'=8,'head'=8] {'cx'}, dimensions={0} | all-to-all | bytes 131072 | tf_op jit(solution)/shard_map/all_to_all | solution.py:107
  33.3 0.7 broadcast_in_dim.139
  34.1 3.6 %all-to-all-start.2 = ((bf16[8,4,16,256]{3,2,1,0:T(8,128)(2,1)}), bf16[8,4,16,256]{3,2,1,0:T(8,128)(2,1)S(1)}, u32[]{:S(2)}, u32[]{:S(2)}) async-start(bf16[8,4,16,256]{3,2,1,0:T(8,128)(2,1)} %broadcast_in_dim.139), calls=%async_computation.2 | async-start | bytes 524288 | tf_op jit(solution)/shard_map/all_to_all | solution.py:112
  37.6 1.0 copy.203
  38.8 9.3 %all-to-all-done.2 = bf16[8,4,16,256]{3,2,1,0:T(8,128)(2,1)S(1)} async-done(((bf16[8,4,16,256]{3,2,1,0:T(8,128)(2,1)}), bf16[8,4,16,256]{3,2,1,0:T(8,128)(2,1)S(1)}, u32[]{:S(2)}, u32[]{:S(2)}) %all-to-all-start.2) | async-done | bytes 262176 | tf_op jit(solution)/shard_map/all_to_all | solution.py:112
  48.8 2.9 %conditional.3 = (f32[1,1,8,128,384]{3,4,2,1,0:T(8,128)S(1)}, bf16[128,1024]{0,1:T(8,128)(2,1)S(1)}, f32[128,256]{0,1:T(8,128)S(1)}, f32[2,128,256]{2,1,0:T(8,128)}) conditional(s32[]{:T(128)} %convert_element_type.101, (s32[128]{0:T(128)S(1)}, s32[1,2]{1,0:T(1,128)S(1)}, s32[4]{0:T(128)S(1)}, s32[]{:T(128)}, bf16[1,384,1,128]{3,1,2,0:T(8,128)(2,1)S(1)}, ...), branch_computations={%region_3.6_spmd, %region_6.0_spmd} | conditional | flops 609204224 | bytes 35293136 | solution.py:177
  51.0 0.7 broadcast.241
  51.8 1.3 %collective-permute-start = (bf16[128,1024]{0,1:T(8,128)(2,1)S(1)}, bf16[128,1024]{0,1:T(8,128)(2,1)}, u32[]{:S(2)}, u32[]{:S(2)}) collective-permute-start(bf16[128,1024]{0,1:T(8,128)(2,1)S(1)} %get-tuple-element.95), channel_id=1, source_target_pairs={{512,0},{513,1},{514,2},{515,3},{516,4},{517,5},{518,6},{519,7},{5... | collective-permute-start | bytes 786440 | tf_op jit(solution)/shard_map/ppermute | solution.py:13
  53.1 4.9 %collective-permute-done = bf16[128,1024]{0,1:T(8,128)(2,1)} collective-permute-done((bf16[128,1024]{0,1:T(8,128)(2,1)S(1)}, bf16[128,1024]{0,1:T(8,128)(2,1)}, u32[]{:S(2)}, u32[]{:S(2)}) %collective-permute-start) | collective-permute-done | bytes 262176 | tf_op jit(solution)/shard_map/ppermute | solution.py:13
  58.0 6.9 %conditional.4 = (bf16[1,1,8,128,384]{3,4,2,1,0:T(8,128)(2,1)S(1)}, bf16[1,1,8,128,384]{3,4,2,1,0:T(8,128)(2,1)S(1)}, f32[2,8,4096]{2,0,1:T(2,128)S(1)}) conditional(s32[]{:T(128)} %convert_element_type.101, (bf16[1,384,1,128]{3,1,2,0:T(8,128)(2,1)S(1)}, bf16[128,1024]{0,1:T(8,128)(2,1)}, f32[1,1,8,128,384]{3,4,2,1,0:T(8,128)S(1)}, ...), branch_computations={%region_10.12_spmd, %region_12.13_spmd} | conditional | flops 337214464 | bytes 13049936 | solution.py:181
  59.5 1.3 %fusion.3 = f32[128,8]{0,1:T(8,128)S(1)} fusion(bf16[1,1,8,128,384]{4,3,2,1,0:T(8,128)(2,1)S(1)} %copy.185, bf16[1,128,1,8,128]{1,4,3,2,0:T(8,128)(2,1)} %bitcast.155, bf16[1,384,1,128]{3,1,2,0:T(8,128)(2,1)S(1)} %copy-done.6), kind=kOutput, calls=%fused_computation.8 | convolution fusion | flops 101055488 | bytes 1150976 | tf_op jit(solution)/shard_map/cond/branch_0_fun/bkgql,blkd->bqkgd/dot_general | solution.py:64
  60.9 1.4 %fusion.1 = bf16[1,1,8,128,384]{3,4,2,1,0:T(8,128)(2,1)S(1)} fusion(f32[1,1,8,128,384]{3,4,2,1,0:T(8,128)S(1)} %get-tuple-element.73, bf16[128,8,128]{0,2,1:T(8,128)(2,1)} %bitcast.65, f32[8,128]{1,0:T(8,128)S(1)} %bitcast.338, bf16[1,384,1,128]{3,1,2,0:T(8,128)(2,1)} %copy-done.5), kind=kOutput, calls=%fused_computation.5 | convolution fusion | flops 101842944 | bytes 2723840 | tf_op jit(solution)/shard_map/cond/branch_0_fun/bqkgd,blkd->bkgql/dot_general | solution.py:67
  62.6 1.3 %convolution_bitcast_fusion.1 = f32[1,256,1,1,128]{4,1,3,2,0:T(8,128)S(1)} fusion(bf16[128,8,128]{0,2,1:T(8,128)(2,1)} %bitcast.65, bf16[1,1,8,128,384]{4,3,2,1,0:T(8,128)(2,1)S(1)} %copy.185), kind=kOutput, calls=%fused_computation.9 | convolution fusion | flops 67108864 | bytes 917504 | tf_op jit(solution)/shard_map/cond/branch_0_fun/bkgql,bqkgd->blkd/dot_general | solution.py:81
  65.2 13.1 %all_to_all.32 = f32[8,2,4224]{2,1,0:T(2,128)S(1)} all-to-all(f32[8,2,4224]{2,1,0:T(2,128)S(1)} %maximum_bitcast_fusion), channel_id=1, replica_groups=mesh['section'=2,'cx'=8,'cy'=8,'head'=8] {'cy'}, dimensions={0} | all-to-all | bytes 540672 | tf_op jit(solution)/shard_map/all_to_all | solution.py:123
  78.9 11.5 %all_to_all.33 = f32[8,16,256]{2,1,0:T(8,128)S(1)} all-to-all(f32[8,16,256]{2,1,0:T(8,128)S(1)} %bitcast.330), channel_id=1, replica_groups=mesh['section'=2,'cx'=8,'cy'=8,'head'=8] {'cx'}, dimensions={0} | all-to-all | bytes 262144 | tf_op jit(solution)/shard_map/all_to_all | solution.py:131
  90.4 0.7 broadcast_in_dim.146
  91.0 3.4 %all-to-all-start.5 = ((f32[8,16,256]{2,1,0:T(8,128)}), f32[8,16,256]{2,1,0:T(8,128)S(1)}, u32[]{:S(2)}, u32[]{:S(2)}) async-start(f32[8,16,256]{2,1,0:T(8,128)} %broadcast_in_dim.146), calls=%async_computation.5 | async-start | bytes 262144 | tf_op jit(solution)/shard_map/all_to_all | solution.py:133
  95.7 3.0 %conditional.5 = (bf16[1,128,1024]{2,1,0:T(8,128)(2,1)S(1)}, f32[128,256]{1,0:T(8,128)S(1)}) conditional(s32[]{:T(128)} %convert_element_type.101, (bf16[1,128,1024]{2,1,0:T(8,128)(2,1)S(1)}, bf16[1,1,8,128,384]{3,4,2,1,0:T(8,128)(2,1)S(1)}, bf16[128,1024]{0,1:T(8,128)(2,1)}, bf16[1,1,8,128,384]{3,4,2,1,0:T(8,128)(2,1)S(1)}, ...), branch_computations={%region_13.14_spmd, %region_14.15_spmd} | conditional | flops 168083456 | bytes 7045136 | solution.py:190
  96.9 1.2 %convolution_bitcast_fusion.3 = f32[1,128,1,1,128]{1,4,3,2,0:T(8,128)S(1)} fusion(bf16[128,8,128]{0,2,1:T(8,128)(2,1)} %bitcast.93, bf16[1,1,8,128,384]{4,3,2,1,0:T(8,128)(2,1)S(1)} %copy.216), kind=kOutput, calls=%fused_computation.22 | convolution fusion | flops 33554432 | bytes 589824 | tf_op jit(solution)/shard_map/cond/branch_0_fun/bkgql,bqkgd->blkd/dot_general | solution.py:81
  98.7 4.7 %all-to-all-done.5 = f32[8,16,256]{2,1,0:T(8,128)S(1)} async-done(((f32[8,16,256]{2,1,0:T(8,128)}), f32[8,16,256]{2,1,0:T(8,128)S(1)}, u32[]{:S(2)}, u32[]{:S(2)}) %all-to-all-start.5) | async-done | bytes 131104 | tf_op jit(solution)/shard_map/all_to_all | solution.py:133
  103.4 0.6 fusion.42
  (79 shorter events, 9.0 us)
Async XLA Ops:
  0.6 38.1 %copy-start.15 = (s32[1,2]{1,0:T(1,128)S(1)}, s32[1,2]{1,0:T(1,128)}, u32[]{:S(2)}) copy-start(s32[1,2]{1,0:T(1,128)} %param.17) | copy-start | bytes 28
  34.1 14.7 %copy-start = (s32[4]{0:T(128)S(1)}, s32[4]{0:T(128)}, u32[]{:S(2)}) copy-start(s32[4]{0:T(128)} %param.16) | copy-start | bytes 52
  34.1 14.7 %copy-start.3 = (bf16[1,128,1024]{2,1,0:T(8,128)(2,1)S(1)}, bf16[1,128,1024]{2,1,0:T(8,128)(2,1)}, u32[]{:S(2)}) copy-start(bf16[1,128,1024]{2,1,0:T(8,128)(2,1)} %param.12) | copy-start | bytes 786436
  34.1 14.7 %copy-start.7 = (bf16[128,1024]{1,0:T(8,128)(2,1)S(1)}, bf16[128,1024]{1,0:T(8,128)(2,1)}, u32[]{:S(2)}) copy-start(bf16[128,1024]{1,0:T(8,128)(2,1)} %param.14) | copy-start | bytes 786436
  34.1 14.8 %copy-start.14 = (s32[128]{0:T(128)S(1)}, s32[128]{0:T(128)}, u32[]{:S(2)}) copy-start(s32[128]{0:T(128)} %param.15) | copy-start | bytes 1540
  34.1 14.0 %all-to-all-start.2 = ((bf16[8,4,16,256]{3,2,1,0:T(8,128)(2,1)}), bf16[8,4,16,256]{3,2,1,0:T(8,128)(2,1)S(1)}, u32[]{:S(2)}, u32[]{:S(2)}) async-start(bf16[8,4,16,256]{3,2,1,0:T(8,128)(2,1)} %broadcast_in_dim.139), calls=%async_computation.2 | async-start | bytes 524288 | tf_op jit(solution)/shard_map/all_to_all | solution.py:112
  51.7 6.3 %copy-start.11 = (f32[128,256]{0,1:T(8,128)}, f32[128,256]{0,1:T(8,128)S(1)}, u32[]{:S(2)}) copy-start(f32[128,256]{0,1:T(8,128)S(1)} %get-tuple-element.100) | copy-start | bytes 393220
  51.8 6.3 %copy-start.9 = (bf16[128,1024]{0,1:T(8,128)(2,1)}, bf16[128,1024]{0,1:T(8,128)(2,1)S(1)}, u32[]{:S(2)}) copy-start(bf16[128,1024]{0,1:T(8,128)(2,1)S(1)} %get-tuple-element.95) | copy-start | bytes 786436
  51.8 6.2 %collective-permute-start = (bf16[128,1024]{0,1:T(8,128)(2,1)S(1)}, bf16[128,1024]{0,1:T(8,128)(2,1)}, u32[]{:S(2)}, u32[]{:S(2)}) collective-permute-start(bf16[128,1024]{0,1:T(8,128)(2,1)S(1)} %get-tuple-element.95), channel_id=1, source_target_pairs={{512,0},{513,1},{514,2},{515,3},{516,4},{517,5},{518,6},{519,7},{5... | collective-permute-start | bytes 786440 | tf_op jit(solution)/shard_map/ppermute | solution.py:13
  58.0 0.6 copy-start.5
  58.6 0.9 copy-start.6
  65.2 30.5 %copy-start.10 = (bf16[128,1024]{0,1:T(8,128)(2,1)S(1)}, bf16[128,1024]{0,1:T(8,128)(2,1)}, u32[]{:S(2)}) copy-start(bf16[128,1024]{0,1:T(8,128)(2,1)} %copy-done.9) | copy-start | bytes 786436
  65.2 30.5 %copy-start.12 = (f32[128,256]{0,1:T(8,128)S(1)}, f32[128,256]{0,1:T(8,128)}, u32[]{:S(2)}) copy-start(f32[128,256]{0,1:T(8,128)} %copy-done.11) | copy-start | bytes 393220
  91.0 12.4 %all-to-all-start.5 = ((f32[8,16,256]{2,1,0:T(8,128)}), f32[8,16,256]{2,1,0:T(8,128)S(1)}, u32[]{:S(2)}, u32[]{:S(2)}) async-start(f32[8,16,256]{2,1,0:T(8,128)} %broadcast_in_dim.146), calls=%async_computation.5 | async-start | bytes 262144 | tf_op jit(solution)/shard_map/all_to_all | solution.py:133
  98.7 5.4 %copy-start.13 = (bf16[1,128,1024]{2,1,0:T(8,128)(2,1)}, bf16[1,128,1024]{2,1,0:T(8,128)(2,1)S(1)}, u32[]{:S(2)}) copy-start(bf16[1,128,1024]{2,1,0:T(8,128)(2,1)S(1)} %get-tuple-element.271) | copy-start | bytes 786436

commit v12 on v6

--- a/solution.py
+++ b/solution.py
@@ -107,10 +107,11 @@
         jnp.where(ids[None, :, :, None] == slot_ids[:, None, None, None], vals[None], 0.0),
         axis=(1, 2),
     ).reshape(nslot, blk // ny, feat)
-    got = lax.all_to_all(jnp.repeat(rowsum, rows_per_slot, axis=0), "cx", 0, 0, tiled=True)
-    total = jnp.sum(got, axis=0)
+    part = jnp.repeat(rowsum.astype(jnp.bfloat16), rows_per_slot, axis=0)
+    got = lax.all_to_all(part, "cx", 0, 0, tiled=True)
+    total = jnp.sum(got.astype(jnp.float32), axis=0).astype(jnp.bfloat16)
     got = lax.all_to_all(jnp.broadcast_to(total[None], (ny,) + total.shape), "cy", 0, 0, tiled=True)
-    return got.reshape(blk, feat)
+    return got.reshape(blk, feat).astype(jnp.float32)
 
 
 def body(layer_in, kv_in, out_grad, sentences, anchor_blocks, anchor_pick):

time: 103 us -> 101 us (0.981)
  no operation moved by 1% of the time
where the time goes in v12:
time: 101 us; the launch traced here: 100 us
  blocking collectives  57 us (56%)
  waiting for transfers between devices  18.3 us (18%)
  local copies, waits for them, and re-layouts  8.34 us (8%)
  starting transfers between devices  8.19 us (8%)
  other arithmetic  3.79 us (4%)
  matrix products  3.06 us (3%)
  between operations  1.6 us (2%)
    all_to_all x1, blocking collectives, spread_anchors(): lax.all_to_all(jnp.broadcast_to(row[None], (nx,) + row.shape), 'cx', 0, 0...  17.5 us
    all_to_all x1, blocking collectives, spread_anchors(): got = lax.all_to_all(part, 'cy', 0, 0, tiled=True)  15.7 us
    all_to_all x1, blocking collectives, gather_grads(): got = lax.all_to_all(load, 'cy', 0, 0, tiled=True)  13.1 us
    all_to_all x1, blocking collectives, gather_grads(): got = lax.all_to_all(part, 'cx', 0, 0, tiled=True)  10.8 us
    all_to_all x1, waiting for transfers between devices, spread_anchors(): lax.all_to_all(jnp.broadcast_to(slots[None], (ny,) + slots.shape), 'cy',...  9.25 us
    all_to_all x1, waiting for transfers between devices, gather_grads(): lax.all_to_all(jnp.broadcast_to(total[None], (ny,) + total.shape), 'cy',...  6.91 us
    all_to_all x1, starting transfers between devices, spread_anchors(): lax.all_to_all(jnp.broadcast_to(slots[None], (ny,) + slots.shape), 'cy',...  3.56 us
    all_to_all x1, starting transfers between devices, gather_grads(): lax.all_to_all(jnp.broadcast_to(total[None], (ny,) + total.shape), 'cy',...  3.35 us
  transfers between devices with their start and end apart: 3, of which 3 were waited for; matrix products, arithmetic and copies ran while one was open for 2% of the time, Pallas kernels for 0%

profile of v12, /device:TPU:2, one launch (start us, length us, event | category | flops | bytes accessed | tf_op | source)
XLA Modules:
  0.0 100.5 jit_solution(3048228095934838123)
XLA Ops:
  0.6 1.3 %compare_reduce_fusion = pred[]{:T(512)} fusion(s32[4]{0:T(128)} %param.14, s32[]{:T(128)} %add.22), kind=kLoop, calls=%fused_computation.90 | loop fusion | flops 7 | bytes 21 | tf_op jit(solution)/shard_map/reduce_or | solution.py:131
  1.9 0.7 broadcast_select_fusion
  2.6 15.7 %all_to_all.30 = bf16[8,16,256]{2,1,0:T(8,128)(2,1)S(1)} all-to-all(bf16[8,16,256]{2,1,0:T(8,128)(2,1)S(1)} %bitcast.267), channel_id=1, replica_groups=mesh['section'=2,'cx'=8,'cy'=8,'head'=8] {'cy'}, dimensions={0} | all-to-all | bytes 131072 | tf_op jit(solution)/shard_map/all_to_all | solution.py:84
  18.4 17.5 %all_to_all.31 = bf16[8,16,256]{2,1,0:T(8,128)(2,1)S(1)} all-to-all(bf16[8,16,256]{2,1,0:T(8,128)(2,1)S(1)} %broadcast_in_dim.139), channel_id=1, replica_groups=mesh['section'=2,'cx'=8,'cy'=8,'head'=8] {'cx'}, dimensions={0} | all-to-all | bytes 131072 | tf_op jit(solution)/shard_map/all_to_all | solution.py:86
  35.9 0.7 broadcast_in_dim.140
  36.6 3.6 %all-to-all-start.2 = ((bf16[8,4,16,256]{3,2,1,0:T(8,128)(2,1)}), bf16[8,4,16,256]{3,2,1,0:T(8,128)(2,1)S(1)}, u32[]{:S(2)}, u32[]{:S(2)}) async-start(bf16[8,4,16,256]{3,2,1,0:T(8,128)(2,1)} %broadcast_in_dim.140), calls=%async_computation.2 | async-start | bytes 524288 | tf_op jit(solution)/shard_map/all_to_all | solution.py:91
  40.2 1.0 copy.180
  41.3 9.3 %all-to-all-done.2 = bf16[8,4,16,256]{3,2,1,0:T(8,128)(2,1)S(1)} async-done(((bf16[8,4,16,256]{3,2,1,0:T(8,128)(2,1)}), bf16[8,4,16,256]{3,2,1,0:T(8,128)(2,1)S(1)}, u32[]{:S(2)}, u32[]{:S(2)}) %all-to-all-start.2) | async-done | bytes 262176 | tf_op jit(solution)/shard_map/all_to_all | solution.py:91
  51.4 3.6 %conditional.2 = (f32[1,1,8,128,384]{3,4,2,1,0:T(8,128)S(1)}, bf16[128,1024]{0,1:T(8,128)(2,1)S(1)}, f32[128,256]{0,1:T(8,128)}, f32[2,128,256]{1,0,2:T(2,128)}) conditional(s32[]{:T(128)} %convert_element_type.117, (s32[128]{0:T(128)S(1)}, s32[1,2]{1,0:T(1,128)S(1)}, s32[4]{0:T(128)S(1)}, s32[]{:T(128)}, bf16[1,384,1,128]{3,1,2,0:T(8,128)(2,1)S(1)}, ...), branch_computations={%region_3.6_spmd, %region_6.0_spmd} | conditional | flops 609597440 | bytes 31229848 | solution.py:157
  51.7 0.6 gather_fusion
  53.5 0.8 broadcast.227
  54.3 0.7 broadcast.226
  55.0 1.3 %collective-permute-start = (bf16[128,1024]{0,1:T(8,128)(2,1)S(1)}, bf16[128,1024]{0,1:T(8,128)(2,1)S(1)}, u32[]{:S(2)}, u32[]{:S(2)}) collective-permute-start(bf16[128,1024]{0,1:T(8,128)(2,1)S(1)} %get-tuple-element.83), channel_id=1, source_target_pairs={{512,0},{513,1},{514,2},{515,3},{516,4},{517,5},{518,6},{519,7},{5... | collective-permute-start | bytes 786440 | tf_op jit(solution)/shard_map/ppermute | solution.py:13
  56.3 2.1 %collective-permute-done = bf16[128,1024]{0,1:T(8,128)(2,1)S(1)} collective-permute-done((bf16[128,1024]{0,1:T(8,128)(2,1)S(1)}, bf16[128,1024]{0,1:T(8,128)(2,1)S(1)}, u32[]{:S(2)}, u32[]{:S(2)}) %collective-permute-start) | collective-permute-done | bytes 262176 | tf_op jit(solution)/shard_map/ppermute | solution.py:13
  58.4 4.5 %conditional.3 = (bf16[1,128,1024]{2,1,0:T(8,128)(2,1)S(1)}, f32[128,256]{1,0:T(8,128)S(1)}, f32[2,8,4096]{2,0,1:T(2,128)S(1)}) conditional(s32[]{:T(128)} %convert_element_type.117, (bf16[1,384,1,128]{3,1,2,0:T(8,128)(2,1)S(1)}, bf16[128,1024]{0,1:T(8,128)(2,1)S(1)}, f32[1,1,8,128,384]{3,4,2,1,0:T(8,128)S(1)}, ...), branch_computations={%region_10.12_spmd, %region_12.13_spmd} | conditional | flops 506084352 | bytes 13148184 | solution.py:161
  59.1 0.8 copy.192
  59.9 1.3 %fusion.7 = f32[1,384,1,1,128]{1,4,3,2,0:T(8,128)S(1)} fusion(bf16[8,128,384]{1,2,0:T(8,128)(2,1)S(1)} %fusion.2, bf16[128,8,128]{0,2,1:T(8,128)(2,1)} %bitcast.260), kind=kOutput, calls=%fused_computation.15 | convolution fusion | flops 100712448 | bytes 1245184 | tf_op jit(solution)/shard_map/cond/branch_0_fun/bkgql,bqkgd->blkd/dot_general | solution.py:69
  63.1 13.1 %all_to_all.32 = f32[8,2,4224]{2,1,0:T(2,128)S(1)} all-to-all(f32[8,2,4224]{2,1,0:T(2,128)S(1)} %maximum_bitcast_fusion), channel_id=1, replica_groups=mesh['section'=2,'cx'=8,'cy'=8,'head'=8] {'cy'}, dimensions={0} | all-to-all | bytes 540672 | tf_op jit(solution)/shard_map/all_to_all | solution.py:102
  76.8 10.8 %all_to_all.33 = bf16[8,16,256]{2,1,0:T(8,128)(2,1)S(1)} all-to-all(bf16[8,16,256]{2,1,0:T(8,128)(2,1)S(1)} %bitcast.268), channel_id=1, replica_groups=mesh['section'=2,'cx'=8,'cy'=8,'head'=8] {'cx'}, dimensions={0} | all-to-all | bytes 131072 | tf_op jit(solution)/shard_map/all_to_all | solution.py:111
  87.5 0.6 broadcast_in_dim.147
  88.2 3.4 %all-to-all-start.5 = ((bf16[8,16,256]{2,1,0:T(8,128)(2,1)}), bf16[8,16,256]{2,1,0:T(8,128)(2,1)S(1)}, u32[]{:S(2)}, u32[]{:S(2)}) async-start(bf16[8,16,256]{2,1,0:T(8,128)(2,1)} %broadcast_in_dim.147), calls=%async_computation.5 | async-start | bytes 131072 | tf_op jit(solution)/shard_map/all_to_all | solution.py:113
  91.5 0.7 dynamic_slice.3
  92.9 6.9 %all-to-all-done.5 = bf16[8,16,256]{2,1,0:T(8,128)(2,1)S(1)} async-done(((bf16[8,16,256]{2,1,0:T(8,128)(2,1)}), bf16[8,16,256]{2,1,0:T(8,128)(2,1)S(1)}, u32[]{:S(2)}, u32[]{:S(2)}) %all-to-all-start.5) | async-done | bytes 65568 | tf_op jit(solution)/shard_map/all_to_all | solution.py:113
  99.8 0.6 fusion.40
  (59 shorter events, 5.4 us)
Async XLA Ops:
  0.6 40.6 %copy-start.7 = (s32[1,2]{1,0:T(1,128)S(1)}, s32[1,2]{1,0:T(1,128)}, u32[]{:S(2)}) copy-start(s32[1,2]{1,0:T(1,128)} %param.15) | copy-start | bytes 28
  36.6 14.7 %copy-start = (s32[4]{0:T(128)S(1)}, s32[4]{0:T(128)}, u32[]{:S(2)}) copy-start(s32[4]{0:T(128)} %param.14) | copy-start | bytes 52
  36.6 14.7 %copy-start.3 = (bf16[1,128,1024]{2,1,0:T(8,128)(2,1)S(1)}, bf16[1,128,1024]{2,1,0:T(8,128)(2,1)}, u32[]{:S(2)}) copy-start(bf16[1,128,1024]{2,1,0:T(8,128)(2,1)} %param.10) | copy-start | bytes 786436
  36.6 14.7 %copy-start.4 = (bf16[128,1024]{1,0:T(8,128)(2,1)S(1)}, bf16[128,1024]{1,0:T(8,128)(2,1)}, u32[]{:S(2)}) copy-start(bf16[128,1024]{1,0:T(8,128)(2,1)} %param.12) | copy-start | bytes 786436
  36.6 14.8 %copy-start.6 = (s32[128]{0:T(128)S(1)}, s32[128]{0:T(128)}, u32[]{:S(2)}) copy-start(s32[128]{0:T(128)} %param.13) | copy-start | bytes 1540
  36.6 14.0 %all-to-all-start.2 = ((bf16[8,4,16,256]{3,2,1,0:T(8,128)(2,1)}), bf16[8,4,16,256]{3,2,1,0:T(8,128)(2,1)S(1)}, u32[]{:S(2)}, u32[]{:S(2)}) async-start(bf16[8,4,16,256]{3,2,1,0:T(8,128)(2,1)} %broadcast_in_dim.140), calls=%async_computation.2 | async-start | bytes 524288 | tf_op jit(solution)/shard_map/all_to_all | solution.py:91
  55.0 3.4 %collective-permute-start = (bf16[128,1024]{0,1:T(8,128)(2,1)S(1)}, bf16[128,1024]{0,1:T(8,128)(2,1)S(1)}, u32[]{:S(2)}, u32[]{:S(2)}) collective-permute-start(bf16[128,1024]{0,1:T(8,128)(2,1)S(1)} %get-tuple-element.83), channel_id=1, source_target_pairs={{512,0},{513,1},{514,2},{515,3},{516,4},{517,5},{518,6},{519,7},{5... | collective-permute-start | bytes 786440 | tf_op jit(solution)/shard_map/ppermute | solution.py:13
  62.9 37.0 %copy-start.5 = (bf16[1,128,1024]{2,1,0:T(8,128)(2,1)}, bf16[1,128,1024]{2,1,0:T(8,128)(2,1)S(1)}, u32[]{:S(2)}) copy-start(bf16[1,128,1024]{2,1,0:T(8,128)(2,1)S(1)} %get-tuple-element.240) | copy-start | bytes 786436
  88.2 11.7 %all-to-all-start.5 = ((bf16[8,16,256]{2,1,0:T(8,128)(2,1)}), bf16[8,16,256]{2,1,0:T(8,128)(2,1)S(1)}, u32[]{:S(2)}, u32[]{:S(2)}) async-start(bf16[8,16,256]{2,1,0:T(8,128)(2,1)} %broadcast_in_dim.147), calls=%async_computation.5 | async-start | bytes 131072 | tf_op jit(solution)/shard_map/all_to_all | solution.py:113

commit v13 on v12

--- a/solution.py
+++ b/solution.py
@@ -95,18 +95,18 @@
 def gather_grads(far, picks, nslot, rows_per_slot):
     ny = lax.axis_size("cy")
     npick, blk, feat = far.shape
-    size = (blk // ny) * feat
-    data = far.reshape(npick, ny, size)
-    tag = jnp.broadcast_to(picks.astype(jnp.float32)[:, None, None], (npick, ny, 128))
-    load = jnp.concatenate([data, tag], axis=2).transpose(1, 0, 2)
+    rows = blk // ny
+    data = far.astype(jnp.bfloat16).reshape(npick, ny, rows, feat)
+    tag = jnp.broadcast_to(picks.astype(jnp.bfloat16)[:, None, None, None], (npick, ny, rows, 128))
+    load = jnp.concatenate([data, tag], axis=3).transpose(1, 0, 2, 3)
     got = lax.all_to_all(load, "cy", 0, 0, tiled=True)
-    vals = got[:, :, :size]
-    ids = got[:, :, size]
+    vals = got[..., :feat].astype(jnp.float32)
+    ids = got[:, :, 0, feat].astype(jnp.float32)
     slot_ids = jnp.arange(nslot, dtype=jnp.float32)
     rowsum = jnp.sum(
-        jnp.where(ids[None, :, :, None] == slot_ids[:, None, None, None], vals[None], 0.0),
+        jnp.where(ids[None, :, :, None, None] == slot_ids[:, None, None, None, None], vals[None], 0.0),
         axis=(1, 2),
-    ).reshape(nslot, blk // ny, feat)
+    )
     part = jnp.repeat(rowsum.astype(jnp.bfloat16), rows_per_slot, axis=0)
     got = lax.all_to_all(part, "cx", 0, 0, tiled=True)
     total = jnp.sum(got.astype(jnp.float32), axis=0).astype(jnp.bfloat16)

time: 101 us -> 99.9 us (0.989)
  no operation moved by 1% of the time
where the time goes in v13:
time: 99.9 us; the launch traced here: 99.7 us
  blocking collectives  56.9 us (57%)
  waiting for transfers between devices  18.3 us (18%)
  starting transfers between devices  8.19 us (8%)
  local copies, waits for them, and re-layouts  7.88 us (8%)
  other arithmetic  3.58 us (4%)
  matrix products  3.06 us (3%)
  between operations  1.59 us (2%)
    all_to_all x1, blocking collectives, spread_anchors(): lax.all_to_all(jnp.broadcast_to(row[None], (nx,) + row.shape), 'cx', 0, 0...  18.3 us
    all_to_all x1, blocking collectives, spread_anchors(): got = lax.all_to_all(part, 'cy', 0, 0, tiled=True)  15.7 us
    all_to_all x1, blocking collectives, gather_grads(): got = lax.all_to_all(load, 'cy', 0, 0, tiled=True)  12.2 us
    all_to_all x1, blocking collectives, gather_grads(): got = lax.all_to_all(part, 'cx', 0, 0, tiled=True)  10.8 us
    all_to_all x1, waiting for transfers between devices, spread_anchors(): lax.all_to_all(jnp.broadcast_to(slots[None], (ny,) + slots.shape), 'cy',...  9.25 us
    all_to_all x1, waiting for transfers between devices, gather_grads(): lax.all_to_all(jnp.broadcast_to(total[None], (ny,) + total.shape), 'cy',...  6.91 us
    all_to_all x1, starting transfers between devices, spread_anchors(): lax.all_to_all(jnp.broadcast_to(slots[None], (ny,) + slots.shape), 'cy',...  3.56 us
    all_to_all x1, starting transfers between devices, gather_grads(): lax.all_to_all(jnp.broadcast_to(total[None], (ny,) + total.shape), 'cy',...  3.35 us
  transfers between devices with their start and end apart: 3, of which 3 were waited for; matrix products, arithmetic and copies ran while one was open for 2% of the time, Pallas kernels for 0%

profile of v13, /device:TPU:2, one launch (start us, length us, event | category | flops | bytes accessed | tf_op | source)
XLA Modules:
  0.0 99.7 jit_solution(4067622406039624330)
XLA Ops:
  0.6 1.3 %compare_reduce_fusion = pred[]{:T(512)} fusion(s32[4]{0:T(128)} %param.14, s32[]{:T(128)} %add.22), kind=kLoop, calls=%fused_computation.93 | loop fusion | flops 7 | bytes 21 | tf_op jit(solution)/shard_map/reduce_or | solution.py:131
  1.9 0.7 broadcast_select_fusion
  2.6 15.7 %all_to_all.30 = bf16[8,16,256]{2,1,0:T(8,128)(2,1)S(1)} all-to-all(bf16[8,16,256]{2,1,0:T(8,128)(2,1)S(1)} %bitcast.267), channel_id=1, replica_groups=mesh['section'=2,'cx'=8,'cy'=8,'head'=8] {'cy'}, dimensions={0} | all-to-all | bytes 131072 | tf_op jit(solution)/shard_map/all_to_all | solution.py:84
  18.4 18.3 %all_to_all.31 = bf16[8,16,256]{2,1,0:T(8,128)(2,1)S(1)} all-to-all(bf16[8,16,256]{2,1,0:T(8,128)(2,1)S(1)} %broadcast_in_dim.140), channel_id=1, replica_groups=mesh['section'=2,'cx'=8,'cy'=8,'head'=8] {'cx'}, dimensions={0} | all-to-all | bytes 131072 | tf_op jit(solution)/shard_map/all_to_all | solution.py:86
  36.7 0.7 broadcast_in_dim.141
  37.4 3.6 %all-to-all-start.2 = ((bf16[8,4,16,256]{3,2,1,0:T(8,128)(2,1)}), bf16[8,4,16,256]{3,2,1,0:T(8,128)(2,1)S(1)}, u32[]{:S(2)}, u32[]{:S(2)}) async-start(bf16[8,4,16,256]{3,2,1,0:T(8,128)(2,1)} %broadcast_in_dim.141), calls=%async_computation.2 | async-start | bytes 524288 | tf_op jit(solution)/shard_map/all_to_all | solution.py:91
  41.0 1.0 copy.215
  42.1 9.3 %all-to-all-done.2 = bf16[8,4,16,256]{3,2,1,0:T(8,128)(2,1)S(1)} async-done(((bf16[8,4,16,256]{3,2,1,0:T(8,128)(2,1)}), bf16[8,4,16,256]{3,2,1,0:T(8,128)(2,1)S(1)}, u32[]{:S(2)}, u32[]{:S(2)}) %all-to-all-start.2) | async-done | bytes 262176 | tf_op jit(solution)/shard_map/all_to_all | solution.py:91
  52.2 3.6 %conditional.2 = (f32[1,1,8,128,384]{3,4,2,1,0:T(8,128)S(1)}, bf16[128,1024]{0,1:T(8,128)(2,1)S(1)}, f32[128,256]{0,1:T(8,128)}, bf16[2,128,256]{1,0,2:T(2,128)(2,1)}) conditional(s32[]{:T(128)} %convert_element_type.136, (s32[128]{0:T(128)S(1)}, s32[1,2]{1,0:T(1,128)S(1)}, s32[4]{0:T(128)S(1)}, s32[]{:T(128)}, ...), branch_computations={%region_3.6_spmd, %region_6.0_spmd} | conditional | flops 609794048 | bytes 30836632 | solution.py:157
  52.5 0.6 gather_fusion
  54.4 0.7 broadcast.226
  55.0 0.7 broadcast.227
  55.7 1.3 %collective-permute-start = (bf16[128,1024]{0,1:T(8,128)(2,1)S(1)}, bf16[128,1024]{0,1:T(8,128)(2,1)S(1)}, u32[]{:S(2)}, u32[]{:S(2)}) collective-permute-start(bf16[128,1024]{0,1:T(8,128)(2,1)S(1)} %get-tuple-element.83), channel_id=1, source_target_pairs={{512,0},{513,1},{514,2},{515,3},{516,4},{517,5},{518,6},{519,7},{5... | collective-permute-start | bytes 786440 | tf_op jit(solution)/shard_map/ppermute | solution.py:13
  57.0 2.1 %collective-permute-done = bf16[128,1024]{0,1:T(8,128)(2,1)S(1)} collective-permute-done((bf16[128,1024]{0,1:T(8,128)(2,1)S(1)}, bf16[128,1024]{0,1:T(8,128)(2,1)S(1)}, u32[]{:S(2)}, u32[]{:S(2)}) %collective-permute-start) | collective-permute-done | bytes 262176 | tf_op jit(solution)/shard_map/ppermute | solution.py:13
  59.2 4.1 %conditional.3 = (bf16[1,128,1024]{2,1,0:T(8,128)(2,1)S(1)}, f32[128,256]{1,0:T(8,128)S(1)}, bf16[2,8,16,256]{3,2,0,1:T(8,128)(2,1)S(1)}) conditional(s32[]{:T(128)} %convert_element_type.136, (bf16[1,384,1,128]{3,1,2,0:T(8,128)(2,1)S(1)}, bf16[128,1024]{0,1:T(8,128)(2,1)S(1)}, f32[1,1,8,128,384]{3,4,2,1,0:T(8,128)S(1)}, ...), branch_computations={%region_10.12_spmd, %region_12.13_spmd} | conditional | flops 506280960 | bytes 12230680 | solution.py:161
  59.9 0.8 copy.227
  60.7 1.3 %fusion.7 = f32[1,384,1,1,128]{1,4,3,2,0:T(8,128)S(1)} fusion(bf16[8,128,384]{1,2,0:T(8,128)(2,1)S(1)} %fusion.2, bf16[128,8,128]{0,2,1:T(8,128)(2,1)} %bitcast.259), kind=kOutput, calls=%fused_computation.15 | convolution fusion | flops 100712448 | bytes 1245184 | tf_op jit(solution)/shard_map/cond/branch_0_fun/bkgql,bqkgd->blkd/dot_general | solution.py:69
  63.4 12.2 %all_to_all.32 = bf16[8,2,16,384]{3,2,1,0:T(8,128)(2,1)S(1)} all-to-all(bf16[8,2,16,384]{3,2,1,0:T(8,128)(2,1)S(1)} %maximum_bitcast_fusion), channel_id=1, replica_groups=mesh['section'=2,'cx'=8,'cy'=8,'head'=8] {'cy'}, dimensions={0} | all-to-all | bytes 393216 | tf_op jit(solution)/shard_map/all_to_all | solution.py:102
  76.0 10.8 %all_to_all.33 = bf16[8,16,256]{2,1,0:T(8,128)(2,1)S(1)} all-to-all(bf16[8,16,256]{2,1,0:T(8,128)(2,1)S(1)} %bitcast.268), channel_id=1, replica_groups=mesh['section'=2,'cx'=8,'cy'=8,'head'=8] {'cx'}, dimensions={0} | all-to-all | bytes 131072 | tf_op jit(solution)/shard_map/all_to_all | solution.py:111
  86.8 0.6 broadcast_in_dim.148
  87.4 3.4 %all-to-all-start.5 = ((bf16[8,16,256]{2,1,0:T(8,128)(2,1)}), bf16[8,16,256]{2,1,0:T(8,128)(2,1)S(1)}, u32[]{:S(2)}, u32[]{:S(2)}) async-start(bf16[8,16,256]{2,1,0:T(8,128)(2,1)} %broadcast_in_dim.148), calls=%async_computation.5 | async-start | bytes 131072 | tf_op jit(solution)/shard_map/all_to_all | solution.py:113
  90.8 0.7 dynamic_slice.3
  92.1 6.9 %all-to-all-done.5 = bf16[8,16,256]{2,1,0:T(8,128)(2,1)S(1)} async-done(((bf16[8,16,256]{2,1,0:T(8,128)(2,1)}), bf16[8,16,256]{2,1,0:T(8,128)(2,1)S(1)}, u32[]{:S(2)}, u32[]{:S(2)}) %all-to-all-start.5) | async-done | bytes 65568 | tf_op jit(solution)/shard_map/all_to_all | solution.py:113
  99.1 0.6 fusion.42
  (59 shorter events, 4.8 us)
Async XLA Ops:
  0.6 41.4 %copy-start.7 = (s32[1,2]{1,0:T(1,128)S(1)}, s32[1,2]{1,0:T(1,128)}, u32[]{:S(2)}) copy-start(s32[1,2]{1,0:T(1,128)} %param.15) | copy-start | bytes 28
  37.4 14.7 %copy-start = (s32[4]{0:T(128)S(1)}, s32[4]{0:T(128)}, u32[]{:S(2)}) copy-start(s32[4]{0:T(128)} %param.14) | copy-start | bytes 52
  37.4 14.7 %copy-start.3 = (bf16[1,128,1024]{2,1,0:T(8,128)(2,1)S(1)}, bf16[1,128,1024]{2,1,0:T(8,128)(2,1)}, u32[]{:S(2)}) copy-start(bf16[1,128,1024]{2,1,0:T(8,128)(2,1)} %param.10) | copy-start | bytes 786436
  37.4 14.7 %copy-start.4 = (bf16[128,1024]{1,0:T(8,128)(2,1)S(1)}, bf16[128,1024]{1,0:T(8,128)(2,1)}, u32[]{:S(2)}) copy-start(bf16[128,1024]{1,0:T(8,128)(2,1)} %param.12) | copy-start | bytes 786436
  37.4 14.8 %copy-start.6 = (s32[128]{0:T(128)S(1)}, s32[128]{0:T(128)}, u32[]{:S(2)}) copy-start(s32[128]{0:T(128)} %param.13) | copy-start | bytes 1540
  37.4 14.0 %all-to-all-start.2 = ((bf16[8,4,16,256]{3,2,1,0:T(8,128)(2,1)}), bf16[8,4,16,256]{3,2,1,0:T(8,128)(2,1)S(1)}, u32[]{:S(2)}, u32[]{:S(2)}) async-start(bf16[8,4,16,256]{3,2,1,0:T(8,128)(2,1)} %broadcast_in_dim.141), calls=%async_computation.2 | async-start | bytes 524288 | tf_op jit(solution)/shard_map/all_to_all | solution.py:91
  55.7 3.4 %collective-permute-start = (bf16[128,1024]{0,1:T(8,128)(2,1)S(1)}, bf16[128,1024]{0,1:T(8,128)(2,1)S(1)}, u32[]{:S(2)}, u32[]{:S(2)}) collective-permute-start(bf16[128,1024]{0,1:T(8,128)(2,1)S(1)} %get-tuple-element.83), channel_id=1, source_target_pairs={{512,0},{513,1},{514,2},{515,3},{516,4},{517,5},{518,6},{519,7},{5... | collective-permute-start | bytes 786440 | tf_op jit(solution)/shard_map/ppermute | solution.py:13
  63.3 36.4 %copy-start.5 = (bf16[1,128,1024]{2,1,0:T(8,128)(2,1)}, bf16[1,128,1024]{2,1,0:T(8,128)(2,1)S(1)}, u32[]{:S(2)}) copy-start(bf16[1,128,1024]{2,1,0:T(8,128)(2,1)S(1)} %get-tuple-element.262) | copy-start | bytes 786436
  87.4 11.7 %all-to-all-start.5 = ((bf16[8,16,256]{2,1,0:T(8,128)(2,1)}), bf16[8,16,256]{2,1,0:T(8,128)(2,1)S(1)}, u32[]{:S(2)}, u32[]{:S(2)}) async-start(bf16[8,16,256]{2,1,0:T(8,128)(2,1)} %broadcast_in_dim.148), calls=%async_computation.5 | async-start | bytes 131072 | tf_op jit(solution)/shard_map/all_to_all | solution.py:113
